TPU v7x, 1024 devices: a whole 4x8x16 slice. The times are simulated.
1024 devices in a mesh: tile: 64 (over z, y_hi, core), thick: 4 (over x), rve: 4 (over y_lo).
Axes of the slice: x: 4, y: 8 (y_hi: 2, y_lo: 4; y = y_hi * 4 + y_lo), z: 16, core: 2. Of those that a mesh axis runs over, the one named last changes fastest.
Arguments:
- gen_strain: float32 [6, 2048], P(None, 'tile'), may hold values from -2.5 to 2.5
- ply_class: int32 [8], replicated, may hold values from 0 to 3
- route: int32 [4, 2048, 2, 1], P('thick', 'tile'), may hold values from 0 to 63; in each aligned block of 64 rows (0 to 63, 64 to 127, ..., all dimensions but the last counted through in order) at most 2 rows name the same one
- phase: int32 [4, 16, 16, 16], P(None, 'rve'), may hold values from 0 to 1
- rve_state: float32 [3, 16, 16, 16, 32768], P(None, 'rve', None, None, ('tile', 'thick')), may hold values from -2.5 to 2.5
- connect: int32 [4, 2048], P(None, 'tile'), may hold values from 0 to 39
- bmat: float32 [4, 6, 6, 2048], P(None, None, None, 'tile'), may hold values from -2.5 to 2.5
- velocity: float32 [6, 2048], P(None, 'tile'), may hold values from -6 to 6
- force_ext: float32 [6, 2048], P(None, 'tile'), may hold values from -6 to 6
- mass: float32 [2048], P('tile'), may hold values from 0.5 to 2
Outputs:
- new_velocity: float32 [6, 2048], P(None, 'tile')
- resultants: float32 [6, 2048], P(None, 'tile')
- new_state: float32 [3, 16, 16, 16, 32768], P(None, 'rve', None, None, ('tile', 'thick'))
Inputs may be any that keep to these rules, and one draw needn't show every extreme that they name: `route`: among the rows of one device (32 elements times 2 points) no tile is named more than 2 times, a bound that some block reaches. `connect`: A value below 32 is a node of the element's own tile; 32 + j is node j of the next tile.
All inputs are finite; a program needn't handle non-finite values.
Results may differ from a plain program's by a relative error of at most 0.000098.
Values sent between devices are 32-bit elements; how exact they have to be, the bound alone decides.
No kernel may reach another device: no remote copies, remote signals or barrier semaphores. Data moves between devices by JAX's collectives and lax.ppermute only.
A program may use at most 32 MiB of HBM per device.

v0:
```python
import math

import jax
import jax.numpy as jnp
from jax import lax
from jax.sharding import PartitionSpec as P

TP = 8
NCLASS = 4
RES = 16
ITERS = 2
GHOST = 8


matrix_lame = 1.2
matrix_shear = 0.8
fiber_lame = 8.0
fiber_shear = 5.0
relax_rate = 1.0 / 288.0
time_step = 0.25


def with_halo(cells, sides, width):
    for axis, dim in sides:
        count = lax.axis_size(axis)
        head = lax.slice_in_dim(cells, 0, width, axis=dim)
        tail = lax.slice_in_dim(cells, cells.shape[dim] - width, cells.shape[dim], axis=dim)
        cells = jnp.concatenate(
            [
                lax.ppermute(tail, axis, [(i, (i + 1) % count) for i in range(count)]),
                cells,
                lax.ppermute(head, axis, [((i + 1) % count, i) for i in range(count)]),
            ],
            axis=dim,
        )
    return cells


def from_behind(value, axis, steps):
    count = lax.axis_size(axis)
    pairs = [(source, (source + steps) % count) for source in range(count)]
    return lax.ppermute(value, axis, pairs)


def material_stress(grads, lame_field, shear_field, macro):
    eps11 = macro[0] + grads[0][0]
    eps22 = macro[1] + grads[1][1]
    eps33 = grads[2][2]
    eps12 = macro[2] + 0.5 * (grads[0][1] + grads[1][0])
    eps13 = 0.5 * (grads[0][2] + grads[2][0])
    eps23 = 0.5 * (grads[1][2] + grads[2][1])
    volume = lame_field * (eps11 + eps22 + eps33)
    twice = 2.0 * shear_field
    return (
        volume + twice * eps11,
        volume + twice * eps22,
        volume + twice * eps33,
        twice * eps12,
        twice * eps13,
        twice * eps23,
    )


def rotate_in(strain, cosine, sine):
    first, second, shear = (strain[0], strain[1], strain[2])
    return jnp.stack(
        [
            cosine * cosine * first + sine * sine * second + 2.0 * cosine * sine * shear,
            sine * sine * first + cosine * cosine * second - 2.0 * cosine * sine * shear,
            -cosine * sine * first
            + cosine * sine * second
            + (cosine * cosine - sine * sine) * shear,
        ]
    )


def rotate_out(stress, cosine, sine):
    first, second, shear = (stress[0], stress[1], stress[2])
    return jnp.stack(
        [
            cosine * cosine * first + sine * sine * second - 2.0 * cosine * sine * shear,
            sine * sine * first + cosine * cosine * second + 2.0 * cosine * sine * shear,
            cosine * sine * first
            - cosine * sine * second
            + (cosine * cosine - sine * sine) * shear,
        ]
    )


def back_diff(field, axis):
    if axis == 0:
        return field[1:] - field[:-1]
    return (field - jnp.roll(field, 1, axis))[1:]


def relax_slab(displace, lame_field, shear_field, macro):
    front = displace[:, :-1]
    grads = [
        [
            displace[i, 1:] - front[i],
            jnp.roll(front[i], -1, 1) - front[i],
            jnp.roll(front[i], -1, 2) - front[i],
        ]
        for i in range(3)
    ]
    s11, s22, s33, s12, s13, s23 = material_stress(grads, lame_field, shear_field, macro)
    first = back_diff(s11, 0) + back_diff(s12, 1) + back_diff(s13, 2)
    second = back_diff(s12, 0) + back_diff(s22, 1) + back_diff(s23, 2)
    third = back_diff(s13, 0) + back_diff(s23, 1) + back_diff(s33, 2)
    shifted = displace[:, 1:-1] + relax_rate * jnp.stack([first, second, third])
    return (shifted, (s11, s22, s12))


def moduli_planes(phase_planes, class_hot):
    fiber_share = phase_planes[0].astype(jnp.float32)[..., None] * class_hot[0]
    for class_number in range(1, NCLASS):
        fiber_share = (
            fiber_share
            + phase_planes[class_number].astype(jnp.float32)[..., None] * class_hot[class_number]
        )
    lame_field = matrix_lame + (fiber_lame - matrix_lame) * fiber_share
    shear_field = matrix_shear + (fiber_shear - matrix_shear) * fiber_share
    return (lame_field, shear_field)


def shards(
    gen_strain, ply_class, route, phase, rve_state, connect, bmat, velocity, force_ext, mass
):
    highest = lax.Precision.HIGHEST
    thick_index = lax.axis_index("thick")
    per_group = route.shape[2]
    elements = gen_strain.shape[1]
    tile_count = lax.axis_size("tile")
    slots = rve_state.shape[4]
    capacity = slots // tile_count
    row_count = elements * per_group
    layer = thick_index * per_group + jnp.arange(per_group, dtype=jnp.int32)
    heights = -1.0 + (2.0 * layer.astype(jnp.float32) + 1.0) / TP
    classes = lax.dynamic_slice_in_dim(ply_class, thick_index * per_group, per_group)
    angle = classes.astype(jnp.float32) * (math.pi / NCLASS)
    cosine = jnp.cos(angle)[None, :]
    sine = jnp.sin(angle)[None, :]
    membrane = gen_strain[:3][:, :, None]
    bending = gen_strain[3:][:, :, None]
    point_strain = membrane + heights[None, None, :] * bending
    rotated = rotate_in(point_strain, cosine, sine)
    strain_rows = rotated.reshape(3, row_count).T
    row_class = jnp.broadcast_to(classes[None, :], (elements, per_group)).reshape(row_count)
    target = route.reshape(row_count)
    tile_hot = (target[:, None] == jnp.arange(tile_count, dtype=jnp.int32)[None, :]).astype(
        jnp.float32
    )
    row_ids = jnp.arange(row_count, dtype=jnp.int32)
    earlier_mask = (row_ids[:, None] > row_ids[None, :]).astype(jnp.float32)
    earlier = jnp.dot(earlier_mask, tile_hot, precision=highest)
    row_rank = jnp.sum(earlier * tile_hot, axis=1).astype(jnp.int32)
    slot_index = target * capacity + row_rank
    choose = (slot_index[:, None] == jnp.arange(slots, dtype=jnp.int32)[None, :]).astype(
        jnp.float32
    )
    send_strain = jnp.dot(choose.T, strain_rows, precision=highest)
    send_class = jnp.sum(choose.astype(jnp.int32) * row_class[:, None], axis=0)
    recv_strain, recv_class = (
        lax.all_to_all(
            send_strain.reshape(tile_count, capacity, 3),
            "tile",
            split_axis=0,
            concat_axis=0,
            tiled=True,
        ),
        lax.all_to_all(
            send_class.reshape(tile_count, capacity),
            "tile",
            split_axis=0,
            concat_axis=0,
            tiled=True,
        ),
    )
    macro = recv_strain.reshape(slots, 3).T
    slot_class = recv_class.reshape(slots)
    class_hot = (slot_class[None, :] == jnp.arange(NCLASS, dtype=jnp.int32)[:, None]).astype(
        jnp.float32
    )
    margin_depth = 1
    round_count = ITERS
    lame_field, shear_field = moduli_planes(phase, class_hot)
    displace = rve_state
    stress = None
    for round_number in range(round_count):
        stacked = with_halo(
            jnp.concatenate([displace, lame_field[None], shear_field[None]], 0),
            (("rve", 1),),
            margin_depth,
        )
        widened = stacked[:3]
        lame_wide, shear_wide = (stacked[3], stacked[4])
        planes = widened.shape[1]
        offset = (lame_wide.shape[0] - planes) // 2
        widened, stress = relax_slab(
            widened,
            lame_wide[offset : offset + planes - 1],
            shear_wide[offset : offset + planes - 1],
            macro,
        )
        displace = widened
    average = jnp.stack([jnp.sum(part[1:], axis=(0, 1, 2)) for part in stress]) / float(RES**3)
    returned = lax.all_to_all(
        average.T.reshape(tile_count, capacity, 3), "tile", split_axis=0, concat_axis=0, tiled=True
    )
    point_stress = jnp.dot(choose, returned.reshape(slots, 3), precision=highest)
    point_stress = point_stress.T.reshape(3, elements, per_group)
    global_stress = rotate_out(point_stress, cosine, sine)
    weight = 1.0 / TP
    forces = jnp.sum(global_stress, axis=2) * weight
    moments = jnp.sum(global_stress * heights[None, None, :], axis=2) * weight
    partial_terms = jnp.concatenate([forces, moments], 0)
    resultants = lax.psum(partial_terms, ("thick", "rve"))
    corner_force = jnp.einsum("akme,me->ake", bmat, resultants, precision=highest)
    node_count = velocity.shape[1]
    node_hot = (
        connect[:, :, None] == jnp.arange(node_count + GHOST, dtype=jnp.int32)[None, None, :]
    ).astype(jnp.float32)
    assembled = jnp.einsum("ake,aen->kn", corner_force, node_hot, precision=highest)
    incoming = from_behind(assembled[:, node_count:], "tile", 1)
    internal = assembled[:, :node_count].at[:, :GHOST].add(incoming)
    new_velocity = velocity + time_step * (force_ext - internal) / mass[None, :]
    return (new_velocity, resultants, displace)


def solution(mesh):
    placed = (
        P(None, "tile"),
        P(),
        P("thick", "tile", None, None),
        P(None, "rve", None, None),
        P(None, "rve", None, None, ("tile", "thick")),
        P(None, "tile"),
        P(None, None, None, "tile"),
        P(None, "tile"),
        P(None, "tile"),
        P("tile"),
    )
    return jax.shard_map(
        shards,
        mesh=mesh,
        in_specs=placed,
        out_specs=(P(None, "tile"), P(None, "tile"), P(None, "rve", None, None, ("tile", "thick"))),
        check_vma=False,
    )
```

profile of v0, /device:TPU:64, one launch (start us, length us, event | category | flops | bytes accessed | tf_op | source)
XLA Modules:
  0.0 213.4 jit_solution(14400004829829861636)
XLA Ops:
  0.6 0.9 fusion.89
  1.5 0.1 mul.511
  1.6 0.8 copy.26
  2.4 0.1 reshape.520
  2.5 0.2 fusion.6
  2.8 0.8 all_to_all.12
  3.6 24.2 %all-to-all-start = ((s32[64,1,2]{2,1,0:T(1,128)}), s32[64,1,2]{2,1,0:T(1,128)S(1)}, u32[]{:S(2)}, u32[]{:S(2)}) async-start(s32[64,1,2]{2,1,0:T(1,128)} %bitcast.3), calls=%async_computation | async-start | bytes 65536 | tf_op jit(solution)/shard_map/all_to_all | solution.py:171
  27.8 0.8 convert_bitcast_fusion.3
  28.7 0.8 fusion.95
  29.6 14.5 %all-to-all-done = s32[64,1,2]{2,1,0:T(1,128)S(1)} async-done(((s32[64,1,2]{2,1,0:T(1,128)}), s32[64,1,2]{2,1,0:T(1,128)S(1)}, u32[]{:S(2)}, u32[]{:S(2)}) %all-to-all-start) | async-done | bytes 544 | tf_op jit(solution)/shard_map/all_to_all | solution.py:171
  44.1 0.5 broadcast.561
  44.6 0.7 reduce.25
  45.3 0.1 eq.75
  45.5 0.6 multiply_add_fusion.7
  46.1 0.3 pad_maximum_fusion.9
  46.4 1.2 fusion.94
  47.6 2.6 %collective-permute-start = (f32[5,1,16,16,128]{4,3,2,1,0:T(8,128)}, f32[5,1,16,16,128]{4,3,2,1,0:T(8,128)S(1)}, u32[]{:S(2)}, u32[]{:S(2)}) collective-permute-start(f32[5,1,16,16,128]{4,3,2,1,0:T(8,128)} %get-tuple-element.48), channel_id=1, source_target_pairs={{0,1},{1,2},{2,3},{3,0},{4,5},{5,6},{6,7},{7,4},{8,9},{9,10},{10,1... | collective-permute-start | bytes 1966088 | tf_op jit(solution)/shard_map/ppermute | solution.py:30
  50.2 5.1 %collective-permute-start.1 = (f32[5,1,16,16,128]{4,3,2,1,0:T(8,128)}, f32[5,1,16,16,128]{4,3,2,1,0:T(8,128)}, u32[]{:S(2)}, u32[]{:S(2)}) collective-permute-start(f32[5,1,16,16,128]{4,3,2,1,0:T(8,128)} %get-tuple-element.47), channel_id=1, source_target_pairs={{1,0},{2,1},{3,2},{0,3},{5,4},{6,5},{7,6},{4,7},{9,8},{10,9},{11,1... | collective-permute-start | bytes 1966088 | tf_op jit(solution)/shard_map/ppermute | solution.py:32
  55.4 0.1 stack.55
  55.5 0.1 stack.56
  55.6 0.2 fusion.68
  55.8 0.2 copy.28
  56.0 24.4 %all_to_all.19 = f32[64,2,3]{2,1,0:T(2,128)S(1)} all-to-all(f32[64,2,3]{2,1,0:T(2,128)S(1)} %copy.28), channel_id=1, replica_groups=mesh['tile'=64,'thick'=4,'rve'=4] {'tile'}, dimensions={0} | all-to-all | bytes 3072 | tf_op jit(solution)/shard_map/all_to_all | solution.py:164
  80.5 3.0 %collective-permute-done.1 = f32[5,1,16,16,128]{4,3,2,1,0:T(8,128)} collective-permute-done((f32[5,1,16,16,128]{4,3,2,1,0:T(8,128)}, f32[5,1,16,16,128]{4,3,2,1,0:T(8,128)}, u32[]{:S(2)}, u32[]{:S(2)}) %collective-permute-start.1) | collective-permute-done | bytes 655392 | tf_op jit(solution)/shard_map/ppermute | solution.py:32
  83.5 1.5 fusion
  85.1 0.2 slice_bitcast_fusion.11
  85.4 0.4 fusion.28
  86.2 0.4 multiply_add_fusion.5
  86.6 0.5 multiply_add_fusion.4
  87.4 0.2 fusion.56
  87.6 0.5 fusion.65
  88.1 0.2 fusion.4
  88.3 0.2 pad_maximum_fusion.8
  88.6 2.5 %collective-permute-start.2 = (f32[5,1,16,16,128]{4,3,2,1,0:T(8,128)S(1)}, f32[5,1,16,16,128]{4,3,2,1,0:T(8,128)S(1)}, u32[]{:S(2)}, u32[]{:S(2)}) collective-permute-start(f32[5,1,16,16,128]{4,3,2,1,0:T(8,128)S(1)} %get-tuple-element.43), channel_id=1, source_target_pairs={{0,1},{1,2},{2,3},{3,0},{4,5},{5,6},{6,7},{7,4},{8,9},{9,10},{10,1... | collective-permute-start | bytes 1966088 | tf_op jit(solution)/shard_map/ppermute | solution.py:30
  91.1 5.1 %collective-permute-start.3 = (f32[5,1,16,16,128]{4,3,2,1,0:T(8,128)S(1)}, f32[5,1,16,16,128]{4,3,2,1,0:T(8,128)S(1)}, u32[]{:S(2)}, u32[]{:S(2)}) collective-permute-start(f32[5,1,16,16,128]{4,3,2,1,0:T(8,128)S(1)} %get-tuple-element.44), channel_id=1, source_target_pairs={{1,0},{2,1},{3,2},{0,3},{5,4},{6,5},{7,6},{4,7},{9,8},{10,9},{11,1... | collective-permute-start | bytes 1966088 | tf_op jit(solution)/shard_map/ppermute | solution.py:32
  96.3 0.7 compare_reduce_fusion
  97.0 13.0 %collective-permute-done.2 = f32[5,1,16,16,128]{4,3,2,1,0:T(8,128)S(1)} collective-permute-done((f32[5,1,16,16,128]{4,3,2,1,0:T(8,128)S(1)}, f32[5,1,16,16,128]{4,3,2,1,0:T(8,128)S(1)}, u32[]{:S(2)}, u32[]{:S(2)}) %collective-permute-start.2) | collective-permute-done | bytes 655392 | tf_op jit(solution)/shard_map/ppermute | solution.py:30
  110.0 13.0 %collective-permute-done.3 = f32[5,1,16,16,128]{4,3,2,1,0:T(8,128)S(1)} collective-permute-done((f32[5,1,16,16,128]{4,3,2,1,0:T(8,128)S(1)}, f32[5,1,16,16,128]{4,3,2,1,0:T(8,128)S(1)}, u32[]{:S(2)}, u32[]{:S(2)}) %collective-permute-start.3) | collective-permute-done | bytes 655392 | tf_op jit(solution)/shard_map/ppermute | solution.py:32
  123.0 0.6 fusion.3
  123.6 0.1 slice_bitcast_fusion.3
  124.2 0.6 multiply_add_fusion
  124.8 0.9 slice.664
  125.7 0.6 slice.663
  126.3 0.2 multiply_add_fusion.1
  126.5 0.5 fusion.10
  127.2 0.6 slice.666
  127.9 1.4 fusion.52
  129.3 0.7 copy.40
  130.1 7.0 %all-to-all-start.2 = ((f32[64,2,3]{2,1,0:T(2,128)}), f32[64,2,3]{2,1,0:T(2,128)}, u32[]{:S(2)}, u32[]{:S(2)}) async-start(f32[64,2,3]{2,1,0:T(2,128)} %bitcast.243), calls=%async_computation.2 | async-start | bytes 131072 | tf_op jit(solution)/shard_map/all_to_all | solution.py:207
  137.1 2.0 fusion.42
  139.1 15.4 %all-to-all-done.2 = f32[64,2,3]{2,1,0:T(2,128)} async-done(((f32[64,2,3]{2,1,0:T(2,128)}), f32[64,2,3]{2,1,0:T(2,128)}, u32[]{:S(2)}, u32[]{:S(2)}) %all-to-all-start.2) | async-done | bytes 1568 | tf_op jit(solution)/shard_map/all_to_all | solution.py:207
  154.5 1.1 fusion.74
  155.6 0.1 squeeze.41
  156.0 0.7 add_subtract_fusion
  156.7 0.8 fusion.70
  157.5 42.8 %psum.7 = f32[6,32]{1,0:T(8,128)S(1)} all-reduce(f32[6,32]{1,0:T(8,128)S(1)} %pad_maximum_fusion.25), channel_id=1, replica_groups=mesh['tile'=64,'thick'=4,'rve'=4] {'thick','rve'}, use_global_device_ids=true, to_apply=%region_7.8 | all-reduce | flops 192 | bytes 1536 | tf_op jit(solution)/shard_map/psum | solution.py:217
  200.2 0.9 multiply_reduce_fusion
  201.2 0.9 convolution_bitcast_fusion
  202.1 1.9 collective-permute-start.4
  204.1 3.3 %fusion.5 = f32[3,4,16,16,128]{4,3,2,1,0:T(8,128)} fusion(f32[1,4,16,16,128]{4,3,2,1,0:T(8,128)} %fusion.42, f32[1,4,16,16,128]{4,3,2,1,0:T(8,128)} %get-tuple-element.50, f32[1,4,16,16,128]{4,3,2,1,0:T(8,128)} %get-tuple-element.49, f32[3,4,16,16,128]{4,3,2,1,0:T(8,128)S(1)} %copy-done, f32[1,4,16,16,128]{4,3,2,1,0:T(8,128)} %copy-done.3, ...), kind=kLoop, calls=%fused_computation.19 | loop fusion | flops 3145728 | bytes 6291456 | tf_op jit(solution)/shard_map/add | solution.py:110
  207.4 4.5 %collective-permute-done.4 = f32[6,8]{1,0:T(8,128)S(1)} collective-permute-done((f32[6,8]{1,0:T(8,128)S(1)}, f32[6,8]{1,0:T(8,128)S(1)}, u32[]{:S(2)}, u32[]{:S(2)}) %collective-permute-start.4) | collective-permute-done | bytes 224 | tf_op jit(solution)/shard_map/ppermute | solution.py:42
  211.9 0.6 add_select_fusion
  212.5 0.2 scatter-add.4
  212.8 0.6 divide_add_fusion
  (85 shorter events, 2.1 us)
Async XLA Ops:
  0.6 45.5 %copy-start = (f32[3,4,16,16,128]{4,3,2,1,0:T(8,128)S(1)}, f32[3,4,16,16,128]{4,3,2,1,0:T(8,128)}, u32[]{:S(2)}) copy-start(f32[3,4,16,16,128]{4,3,2,1,0:T(8,128)} %param.16) | copy-start | bytes 4718596
  2.7 52.9 %copy-start.10 = (s32[64]{0:T(128)}, s32[64]{0:T(128)S(1)}, u32[]{:S(2)}) copy-start(s32[64]{0:T(128)S(1)} %convert_add_fusion) | copy-start | bytes 772
  3.6 40.5 %all-to-all-start = ((s32[64,1,2]{2,1,0:T(1,128)}), s32[64,1,2]{2,1,0:T(1,128)S(1)}, u32[]{:S(2)}, u32[]{:S(2)}) async-start(s32[64,1,2]{2,1,0:T(1,128)} %bitcast.3), calls=%async_computation | async-start | bytes 65536 | tf_op jit(solution)/shard_map/all_to_all | solution.py:171
  27.8 18.6 %copy-start.9 = (f32[2]{0:T(128)}, f32[2]{0:T(128)S(1)}, u32[]{:S(2)}) copy-start(f32[2]{0:T(128)S(1)} %multiply_add_fusion.13) | copy-start | bytes 28
  29.6 25.7 %copy-start.5 = (f32[2]{0:T(128)}, f32[2]{0:T(128)S(1)}, u32[]{:S(2)}) copy-start(f32[2]{0:T(128)S(1)} %get-tuple-element.80) | copy-start | bytes 28
  29.6 25.7 %copy-start.6 = (f32[2]{0:T(128)}, f32[2]{0:T(128)S(1)}, u32[]{:S(2)}) copy-start(f32[2]{0:T(128)S(1)} %get-tuple-element.81) | copy-start | bytes 28
  47.6 32.9 %collective-permute-start = (f32[5,1,16,16,128]{4,3,2,1,0:T(8,128)}, f32[5,1,16,16,128]{4,3,2,1,0:T(8,128)S(1)}, u32[]{:S(2)}, u32[]{:S(2)}) collective-permute-start(f32[5,1,16,16,128]{4,3,2,1,0:T(8,128)} %get-tuple-element.48), channel_id=1, source_target_pairs={{0,1},{1,2},{2,3},{3,0},{4,5},{5,6},{6,7},{7,4},{8,9},{9,10},{10,1... | collective-permute-start | bytes 1966088 | tf_op jit(solution)/shard_map/ppermute | solution.py:30
  50.2 33.3 %collective-permute-start.1 = (f32[5,1,16,16,128]{4,3,2,1,0:T(8,128)}, f32[5,1,16,16,128]{4,3,2,1,0:T(8,128)}, u32[]{:S(2)}, u32[]{:S(2)}) collective-permute-start(f32[5,1,16,16,128]{4,3,2,1,0:T(8,128)} %get-tuple-element.47), channel_id=1, source_target_pairs={{1,0},{2,1},{3,2},{0,3},{5,4},{6,5},{7,6},{4,7},{9,8},{10,9},{11,1... | collective-permute-start | bytes 1966088 | tf_op jit(solution)/shard_map/ppermute | solution.py:32
  87.6 0.9 copy-start.3
  88.1 21.9 %copy-start.1 = (f32[1,4,16,16,128]{4,3,2,1,0:T(8,128)}, f32[1,4,16,16,128]{4,3,2,1,0:T(8,128)S(1)}, u32[]{:S(2)}) copy-start(f32[1,4,16,16,128]{4,3,2,1,0:T(8,128)S(1)} %get-tuple-element.54) | copy-start | bytes 1572868
  88.1 35.5 %copy-start.2 = (f32[1,4,16,16,128]{4,3,2,1,0:T(8,128)}, f32[1,4,16,16,128]{4,3,2,1,0:T(8,128)S(1)}, u32[]{:S(2)}) copy-start(f32[1,4,16,16,128]{4,3,2,1,0:T(8,128)S(1)} %get-tuple-element.55) | copy-start | bytes 1572868
  88.6 21.3 %collective-permute-start.2 = (f32[5,1,16,16,128]{4,3,2,1,0:T(8,128)S(1)}, f32[5,1,16,16,128]{4,3,2,1,0:T(8,128)S(1)}, u32[]{:S(2)}, u32[]{:S(2)}) collective-permute-start(f32[5,1,16,16,128]{4,3,2,1,0:T(8,128)S(1)} %get-tuple-element.43), channel_id=1, source_target_pairs={{0,1},{1,2},{2,3},{3,0},{4,5},{5,6},{6,7},{7,4},{8,9},{9,10},{10,1... | collective-permute-start | bytes 1966088 | tf_op jit(solution)/shard_map/ppermute | solution.py:30
  91.1 31.8 %collective-permute-start.3 = (f32[5,1,16,16,128]{4,3,2,1,0:T(8,128)S(1)}, f32[5,1,16,16,128]{4,3,2,1,0:T(8,128)S(1)}, u32[]{:S(2)}, u32[]{:S(2)}) collective-permute-start(f32[5,1,16,16,128]{4,3,2,1,0:T(8,128)S(1)} %get-tuple-element.44), channel_id=1, source_target_pairs={{1,0},{2,1},{3,2},{0,3},{5,4},{6,5},{7,6},{4,7},{9,8},{10,9},{11,1... | collective-permute-start | bytes 1966088 | tf_op jit(solution)/shard_map/ppermute | solution.py:32
  130.1 24.5 %all-to-all-start.2 = ((f32[64,2,3]{2,1,0:T(2,128)}), f32[64,2,3]{2,1,0:T(2,128)}, u32[]{:S(2)}, u32[]{:S(2)}) async-start(f32[64,2,3]{2,1,0:T(2,128)} %bitcast.243), calls=%async_computation.2 | async-start | bytes 131072 | tf_op jit(solution)/shard_map/all_to_all | solution.py:207
  200.2 7.2 %copy-start.4 = (f32[6,32]{1,0:T(8,128)}, f32[6,32]{1,0:T(8,128)S(1)}, u32[]{:S(2)}) copy-start(f32[6,32]{1,0:T(8,128)S(1)} %psum.7) | copy-start | bytes 2308
  202.1 9.7 %collective-permute-start.4 = (f32[6,8]{1,0:T(8,128)S(1)}, f32[6,8]{1,0:T(8,128)S(1)}, u32[]{:S(2)}, u32[]{:S(2)}) collective-permute-start(f32[6,8]{1,0:T(8,128)S(1)} %slice.543), channel_id=1, source_target_pairs={{0,16},{16,32},{32,48},{48,64},{64,80},{80,96},{96,112},{112,128},... | collective-permute-start | bytes 584 | tf_op jit(solution)/shard_map/ppermute | solution.py:42
  204.1 8.7 %copy-start.7 = (f32[6,32]{1,0:T(8,128)S(1)}, f32[6,32]{1,0:T(8,128)}, u32[]{:S(2)}) copy-start(f32[6,32]{1,0:T(8,128)} %param.19) | copy-start | bytes 2308
  204.1 8.7 %copy-start.8 = (f32[6,32]{1,0:T(8,128)S(1)}, f32[6,32]{1,0:T(8,128)}, u32[]{:S(2)}) copy-start(f32[6,32]{1,0:T(8,128)} %param.20) | copy-start | bytes 2308
  204.1 8.7 %copy-start.11 = (f32[32]{0:T(128)S(1)}, f32[32]{0:T(128)}, u32[]{:S(2)}) copy-start(f32[32]{0:T(128)} %param.21) | copy-start | bytes 388
where the time goes:
time: 214 us; the launch traced here: 213 us
  blocking collectives  67.2 us (31%)
  waiting for transfers between devices  63.4 us (30%)
  starting transfers between devices  48.4 us (23%)
  other arithmetic  20.5 us (10%)
  local copies, waits for them, and re-layouts  10.1 us (5%)
  matrix products  2.31 us (1%)
    psum x1, blocking collectives, shards(): resultants = lax.psum(partial_terms, ('thick', 'rve'))  42.8 us
    all_to_all x1, blocking collectives, shards(): lax.all_to_all(send_strain.reshape(tile_count, capacity, 3), 'tile', spli...  24.4 us
    all_to_all x1, starting transfers between devices, shards(): lax.all_to_all(send_class.reshape(tile_count, capacity), 'tile', split_ax...  24.2 us
    ppermute x2, waiting for transfers between devices, with_halo(): lax.ppermute(head, axis, [((i + 1) % count, i) for i in range(count)])  16 us
    all_to_all x1, waiting for transfers between devices, shards(): lax.all_to_all(average.T.reshape(tile_count, capacity, 3), 'tile', split_...  15.4 us
    all_to_all x1, waiting for transfers between devices, shards(): lax.all_to_all(send_class.reshape(tile_count, capacity), 'tile', split_ax...  14.5 us
    ppermute x2, waiting for transfers between devices, with_halo(): lax.ppermute(tail, axis, [(i, (i + 1) % count) for i in range(count)])  13 us
    ppermute x2, starting transfers between devices, with_halo(): lax.ppermute(head, axis, [((i + 1) % count, i) for i in range(count)])  10.2 us
  transfers between devices with their start and end apart: 7, of which 6 were waited for; matrix products, arithmetic and copies ran while one was open for 4% of the time, Pallas kernels for 0%

commit v1 on v0

--- a/solution.py
+++ b/solution.py
@@ -131,9 +131,18 @@
     per_group = route.shape[2]
     elements = gen_strain.shape[1]
     tile_count = lax.axis_size("tile")
+    slab_count = lax.axis_size("rve")
     slots = rve_state.shape[4]
     capacity = slots // tile_count
     row_count = elements * per_group
+    depth = ITERS
+    up = [(i, (i + 1) % slab_count) for i in range(slab_count)]
+    down = [((i + 1) % slab_count, i) for i in range(slab_count)]
+    planes = rve_state.shape[1]
+    below = lax.ppermute(rve_state[:, planes - depth :], "rve", up)
+    above = lax.ppermute(rve_state[:, :depth], "rve", down)
+    phase_below = lax.ppermute(phase[:, planes - depth :], "rve", up)
+    phase_above = lax.ppermute(phase[:, :depth], "rve", down)
     layer = thick_index * per_group + jnp.arange(per_group, dtype=jnp.int32)
     heights = -1.0 + (2.0 * layer.astype(jnp.float32) + 1.0) / TP
     classes = lax.dynamic_slice_in_dim(ply_class, thick_index * per_group, per_group)
@@ -144,8 +153,10 @@
     bending = gen_strain[3:][:, :, None]
     point_strain = membrane + heights[None, None, :] * bending
     rotated = rotate_in(point_strain, cosine, sine)
-    strain_rows = rotated.reshape(3, row_count).T
     row_class = jnp.broadcast_to(classes[None, :], (elements, per_group)).reshape(row_count)
+    payload = jnp.concatenate(
+        [rotated.reshape(3, row_count), row_class.astype(jnp.float32)[None, :]], 0
+    ).T
     target = route.reshape(row_count)
     tile_hot = (target[:, None] == jnp.arange(tile_count, dtype=jnp.int32)[None, :]).astype(
         jnp.float32
@@ -158,51 +169,27 @@
     choose = (slot_index[:, None] == jnp.arange(slots, dtype=jnp.int32)[None, :]).astype(
         jnp.float32
     )
-    send_strain = jnp.dot(choose.T, strain_rows, precision=highest)
-    send_class = jnp.sum(choose.astype(jnp.int32) * row_class[:, None], axis=0)
-    recv_strain, recv_class = (
-        lax.all_to_all(
-            send_strain.reshape(tile_count, capacity, 3),
-            "tile",
-            split_axis=0,
-            concat_axis=0,
-            tiled=True,
-        ),
-        lax.all_to_all(
-            send_class.reshape(tile_count, capacity),
-            "tile",
-            split_axis=0,
-            concat_axis=0,
-            tiled=True,
-        ),
-    )
-    macro = recv_strain.reshape(slots, 3).T
-    slot_class = recv_class.reshape(slots)
+    send = jnp.dot(choose.T, payload, precision=highest)
+    received = lax.all_to_all(
+        send.reshape(tile_count, capacity, 4), "tile", split_axis=0, concat_axis=0, tiled=True
+    ).reshape(slots, 4)
+    macro = received[:, :3].T
+    slot_class = received[:, 3].astype(jnp.int32)
     class_hot = (slot_class[None, :] == jnp.arange(NCLASS, dtype=jnp.int32)[:, None]).astype(
         jnp.float32
     )
-    margin_depth = 1
-    round_count = ITERS
-    lame_field, shear_field = moduli_planes(phase, class_hot)
-    displace = rve_state
+    wide_phase = jnp.concatenate([phase_below, phase, phase_above], 1)
+    lame_field, shear_field = moduli_planes(wide_phase, class_hot)
+    displace = jnp.concatenate([below, rve_state, above], 1)
     stress = None
-    for round_number in range(round_count):
-        stacked = with_halo(
-            jnp.concatenate([displace, lame_field[None], shear_field[None]], 0),
-            (("rve", 1),),
-            margin_depth,
-        )
-        widened = stacked[:3]
-        lame_wide, shear_wide = (stacked[3], stacked[4])
-        planes = widened.shape[1]
-        offset = (lame_wide.shape[0] - planes) // 2
-        widened, stress = relax_slab(
-            widened,
-            lame_wide[offset : offset + planes - 1],
-            shear_wide[offset : offset + planes - 1],
+    for round_number in range(ITERS):
+        count = displace.shape[1]
+        displace, stress = relax_slab(
+            displace,
+            lame_field[round_number : round_number + count - 1],
+            shear_field[round_number : round_number + count - 1],
             macro,
         )
-        displace = widened
     average = jnp.stack([jnp.sum(part[1:], axis=(0, 1, 2)) for part in stress]) / float(RES**3)
     returned = lax.all_to_all(
         average.T.reshape(tile_count, capacity, 3), "tile", split_axis=0, concat_axis=0, tiled=True
@@ -214,7 +201,7 @@
     forces = jnp.sum(global_stress, axis=2) * weight
     moments = jnp.sum(global_stress * heights[None, None, :], axis=2) * weight
     partial_terms = jnp.concatenate([forces, moments], 0)
-    resultants = lax.psum(partial_terms, ("thick", "rve"))
+    resultants = lax.psum(lax.psum(partial_terms, "rve"), "thick")
     corner_force = jnp.einsum("akme,me->ake", bmat, resultants, precision=highest)
     node_count = velocity.shape[1]
     node_hot = (

time: 214 us -> 140 us (0.65)
  the two profiles are of different devices: /device:TPU:64 before, /device:TPU:8 now
where the time goes in v1:
time: 140 us; the launch traced here: 139 us
  starting transfers between devices  56 us (40%)
  waiting for transfers between devices  30.8 us (22%)
  blocking collectives  20.3 us (14%)
  other arithmetic  18.1 us (13%)
  local copies, waits for them, and re-layouts  9.56 us (7%)
  matrix products  3.04 us (2%)
  between operations  1.5 us (1%)
    psum x2, blocking collectives, shards(): resultants = lax.psum(lax.psum(partial_terms, 'rve'), 'thick')  20.3 us
    all_to_all x1, starting transfers between devices, shards(): lax.all_to_all(average.T.reshape(tile_count, capacity, 3), 'tile', split_...  17.2 us
    all_to_all x1, waiting for transfers between devices, shards(): lax.all_to_all(average.T.reshape(tile_count, capacity, 3), 'tile', split_...  14.4 us
    ppermute x1, starting transfers between devices, shards(): above = lax.ppermute(rve_state[:, :depth], 'rve', down)  13.4 us
    all_to_all x1, starting transfers between devices, shards(): lax.all_to_all(send.reshape(tile_count, capacity, 4), 'tile', split_axis=...  13 us
    all_to_all x1, waiting for transfers between devices, shards(): lax.all_to_all(send.reshape(tile_count, capacity, 4), 'tile', split_axis=...  9.96 us
    ppermute x1, waiting for transfers between devices, from_behind(): return lax.ppermute(value, axis, pairs)  6.4 us
    another operation x4, other arithmetic, relax_slab(): shifted = displace[:, 1:-1] + relax_rate * jnp.stack([first, second, third])  5.18 us
  transfers between devices with their start and end apart: 7, of which 3 were waited for; matrix products, arithmetic and copies ran while one was open for 8% of the time, Pallas kernels for 0%

profile of v1, /device:TPU:8, one launch (start us, length us, event | category | flops | bytes accessed | tf_op | source)
XLA Modules:
  0.0 139.4 jit_solution(13914841761472956109)
XLA Ops:
  0.7 1.6 %fusion.87 = (f32[3,2,16,16,128]{4,3,2,1,0:T(8,128)S(1)}, f32[3,2,16,16,128]{4,3,2,1,0:T(8,128)S(1)}) fusion(f32[3,4,16,16,128]{4,3,2,1,0:T(8,128)} %param.16), kind=kLoop, calls=%fused_computation.206 | loop fusion | bytes 3145728 | tf_op jit(solution)/shard_map/slice | solution.py:143
  2.3 3.5 %collective-permute-start.2 = (f32[3,2,16,16,128]{4,3,2,1,0:T(8,128)S(1)}, f32[3,2,16,16,128]{4,3,2,1,0:T(8,128)S(1)}, u32[]{:S(2)}, u32[]{:S(2)}) collective-permute-start(f32[3,2,16,16,128]{4,3,2,1,0:T(8,128)S(1)} %get-tuple-element.46), channel_id=1, source_target_pairs={{0,1},{1,2},{2,3},{3,0},{4,5},{5,6},{6,7},{7,4},{8,9},{9,10},{10,1... | collective-permute-start | bytes 2359304 | tf_op jit(solution)/shard_map/ppermute | solution.py:142
  5.8 13.4 %collective-permute-start.3 = (f32[3,2,16,16,128]{4,3,2,1,0:T(8,128)S(1)}, f32[3,2,16,16,128]{4,3,2,1,0:T(8,128)S(1)}, u32[]{:S(2)}, u32[]{:S(2)}) collective-permute-start(f32[3,2,16,16,128]{4,3,2,1,0:T(8,128)S(1)} %get-tuple-element.45), channel_id=1, source_target_pairs={{1,0},{2,1},{3,2},{0,3},{5,4},{6,5},{7,6},{4,7},{9,8},{10,9},{11,1... | collective-permute-start | bytes 2359304 | tf_op jit(solution)/shard_map/ppermute | solution.py:143
  19.2 0.1 copy.26
  19.3 0.1 reshape.478
  19.4 0.2 fusion
  19.7 0.1 fusion.85
  19.9 0.1 convert_element_type.91
  20.0 0.1 multiply_add_fusion.9
  20.1 0.1 copy-done.9
  20.2 0.1 stack.54
  20.3 0.1 stack.53
  20.5 0.1 stack.52
  20.6 0.9 fusion.67
  21.5 13.0 %all-to-all-start = ((f32[64,2,4]{2,1,0:T(2,128)}), f32[64,2,4]{2,1,0:T(2,128)S(1)}, u32[]{:S(2)}, u32[]{:S(2)}) async-start(f32[64,2,4]{2,1,0:T(2,128)} %bitcast.3), calls=%async_computation | async-start | bytes 131072 | tf_op jit(solution)/shard_map/all_to_all | solution.py:173
  34.6 0.6 fusion.88
  35.2 2.6 %collective-permute-start = (s32[4,2,16,16]{3,2,1,0:T(8,128)}, s32[4,2,16,16]{3,2,1,0:T(8,128)S(1)}, u32[]{:S(2)}, u32[]{:S(2)}) collective-permute-start(s32[4,2,16,16]{3,2,1,0:T(8,128)} %get-tuple-element.61), channel_id=1, source_target_pairs={{0,1},{1,2},{2,3},{3,0},{4,5},{5,6},{6,7},{7,4},{8,9},{9,10},{10,1... | collective-permute-start | bytes 24584 | tf_op jit(solution)/shard_map/ppermute | solution.py:144
  37.8 4.4 %collective-permute-start.1 = (s32[4,2,16,16]{3,2,1,0:T(8,128)S(1)}, s32[4,2,16,16]{3,2,1,0:T(8,128)S(1)}, u32[]{:S(2)}, u32[]{:S(2)}) collective-permute-start(s32[4,2,16,16]{3,2,1,0:T(8,128)S(1)} %get-tuple-element.60), channel_id=1, source_target_pairs={{1,0},{2,1},{3,2},{0,3},{5,4},{6,5},{7,6},{4,7},{9,8},{10,9},{11,1... | collective-permute-start | bytes 24584 | tf_op jit(solution)/shard_map/ppermute | solution.py:145
  42.2 0.7 compare_reduce_fusion
  42.9 10.0 %all-to-all-done = f32[64,2,4]{2,1,0:T(2,128)S(1)} async-done(((f32[64,2,4]{2,1,0:T(2,128)}), f32[64,2,4]{2,1,0:T(2,128)S(1)}, u32[]{:S(2)}, u32[]{:S(2)}) %all-to-all-start) | async-done | bytes 2080 | tf_op jit(solution)/shard_map/all_to_all | solution.py:173
  52.8 0.2 fusion.61
  53.1 0.2 slice_reduce_fusion.3
  53.4 1.1 multiply_add_fusion.1
  54.5 0.1 constant_dynamic-update-slice_fusion.5
  54.6 0.1 copy-done.1
  54.7 0.2 constant_dynamic-update-slice_fusion.4
  55.0 0.2 slice_bitcast_fusion.4
  55.3 0.1 slice.569
  55.5 0.1 slice.581
  55.8 0.1 slice.592
  55.9 0.7 fusion.9
  56.8 0.5 multiply_add_fusion.5
  57.3 0.8 multiply_add_fusion.4
  58.3 0.4 fusion.17
  58.7 0.8 fusion.26
  59.5 0.4 slice_add_fusion
  59.9 0.1 slice_bitcast_fusion.9
  60.5 1.3 multiply_add_fusion.6
  61.8 0.4 multiply_add_fusion.8
  62.3 0.5 fusion.32
  62.8 1.0 slice.647
  63.8 0.6 slice.646
  64.5 1.3 fusion.55
  65.8 0.7 copy.38
  66.5 17.2 %all-to-all-start.1 = ((f32[64,2,3]{2,1,0:T(2,128)}), f32[64,2,3]{2,1,0:T(2,128)}, u32[]{:S(2)}, u32[]{:S(2)}) async-start(f32[64,2,3]{2,1,0:T(2,128)} %bitcast.199), calls=%async_computation.1 | async-start | bytes 131072 | tf_op jit(solution)/shard_map/all_to_all | solution.py:194
  83.7 1.0 slice.649
  84.7 2.7 %fusion.45 = f32[1,4,16,16,128]{4,3,2,1,0:T(8,128)} fusion(f32[5,16,16,128]{3,2,1,0:T(8,128)} %get-tuple-element.23, f32[5,16,15,128]{3,2,1,0:T(8,128)} %bitcast.196, f32[5,16,1,128]{3,2,1,0:T(1,128)S(1)} %slice.649, f32[5,15,16,128]{3,2,1,0:T(8,128)} %slice.647, f32[5,1,16,128]{3,2,1,0:T(8,128)} %slice.646, f32[5,16,16,128]{3,2,1,0:T(8,128)} %copy-done, ...), kind=kLoop, calls=%fused_computation.100 | loop fusion | flops 917504 | bytes 3932160 | tf_op jit(solution)/shard_map/stack | solution.py:110
  87.4 14.4 %all-to-all-done.1 = f32[64,2,3]{2,1,0:T(2,128)} async-done(((f32[64,2,3]{2,1,0:T(2,128)}), f32[64,2,3]{2,1,0:T(2,128)}, u32[]{:S(2)}, u32[]{:S(2)}) %all-to-all-start.1) | async-done | bytes 1568 | tf_op jit(solution)/shard_map/all_to_all | solution.py:194
  101.8 1.1 fusion.65
  102.9 0.1 squeeze.42
  103.0 0.1 squeeze.41
  103.2 0.1 squeeze.43
  103.3 0.7 add_subtract_fusion
  103.9 0.8 fusion.63
  104.8 9.8 %psum.14 = f32[6,32]{1,0:T(8,128)S(1)} all-reduce(f32[6,32]{1,0:T(8,128)S(1)} %pad_maximum_fusion.13), channel_id=1, replica_groups=mesh['tile'=64,'thick'=4,'rve'=4] {'rve'}, use_global_device_ids=true, to_apply=%region_6.7 | all-reduce | flops 192 | bytes 1536 | tf_op jit(solution)/shard_map/psum | solution.py:204
  114.5 10.5 %psum.15 = f32[6,32]{1,0:T(8,128)S(1)} all-reduce(f32[6,32]{1,0:T(8,128)S(1)} %psum.14), channel_id=1, replica_groups=mesh['tile'=64,'thick'=4,'rve'=4] {'thick'}, use_global_device_ids=true, to_apply=%region_7.8 | all-reduce | flops 192 | bytes 1536 | tf_op jit(solution)/shard_map/psum | solution.py:204
  125.0 0.9 multiply_reduce_fusion
  125.9 0.9 convolution_bitcast_fusion
  126.9 1.9 %collective-permute-start.4 = (f32[6,8]{1,0:T(8,128)S(1)}, f32[6,8]{1,0:T(8,128)S(1)}, u32[]{:S(2)}, u32[]{:S(2)}) collective-permute-start(f32[6,8]{1,0:T(8,128)S(1)} %slice.518), channel_id=1, source_target_pairs={{0,16},{16,32},{32,48},{48,64},{64,80},{80,96},{96,112},{112,128},... | collective-permute-start | bytes 584 | tf_op jit(solution)/shard_map/ppermute | solution.py:42
  128.9 2.6 %slice_add_fusion.1 = f32[3,4,16,16,128]{4,3,2,1,0:T(8,128)} fusion(f32[3,6,16,16,128]{4,3,2,1,0:T(8,128)S(1)} %slice_add_fusion, f32[1,4,16,16,128]{4,3,2,1,0:T(8,128)} %fusion.45, f32[1,4,16,16,128]{4,3,2,1,0:T(8,128)} %get-tuple-element.50, f32[1,4,16,16,128]{4,3,2,1,0:T(8,128)S(1)} %get-tuple-element.49), kind=kLoop, calls=%fused_computation.2 | loop fusion | flops 1572864 | bytes 4718592 | tf_op jit(solution)/shard_map/add | solution.py:110
  131.5 6.4 %collective-permute-done.4 = f32[6,8]{1,0:T(8,128)S(1)} collective-permute-done((f32[6,8]{1,0:T(8,128)S(1)}, f32[6,8]{1,0:T(8,128)S(1)}, u32[]{:S(2)}, u32[]{:S(2)}) %collective-permute-start.4) | collective-permute-done | bytes 224 | tf_op jit(solution)/shard_map/ppermute | solution.py:42
  137.9 0.6 add_select_fusion
  138.5 0.2 scatter-add.4
  138.8 0.6 divide_add_fusion
  (85 shorter events, 1.7 us)
Async XLA Ops:
  0.6 18.6 %copy-start.11 = (s32[1,32,2,1]{1,3,2,0:T(1,128)S(1)}, s32[1,32,2,1]{1,3,2,0:T(1,128)}, u32[]{:S(2)}) copy-start(s32[1,32,2,1]{1,3,2,0:T(1,128)} %param.14) | copy-start | bytes 772
  0.6 19.0 %copy-start.13 = (s32[8]{0:T(128)S(1)}, s32[8]{0:T(128)}, u32[]{:S(2)}) copy-start(s32[8]{0:T(128)} %param.13) | copy-start | bytes 100
  0.7 19.3 %copy-start.6 = (f32[6,32]{1,0:T(8,128)S(1)}, f32[6,32]{1,0:T(8,128)}, u32[]{:S(2)}) copy-start(f32[6,32]{1,0:T(8,128)} %param.12) | copy-start | bytes 2308
  0.7 33.9 %copy-start.2 = (s32[4,4,16,16]{3,2,1,0:T(8,128)S(1)}, s32[4,4,16,16]{3,2,1,0:T(8,128)}, u32[]{:S(2)}) copy-start(s32[4,4,16,16]{3,2,1,0:T(8,128)} %param.15) | copy-start | bytes 49156
  2.3 52.3 %collective-permute-start.2 = (f32[3,2,16,16,128]{4,3,2,1,0:T(8,128)S(1)}, f32[3,2,16,16,128]{4,3,2,1,0:T(8,128)S(1)}, u32[]{:S(2)}, u32[]{:S(2)}) collective-permute-start(f32[3,2,16,16,128]{4,3,2,1,0:T(8,128)S(1)} %get-tuple-element.46), channel_id=1, source_target_pairs={{0,1},{1,2},{2,3},{3,0},{4,5},{5,6},{6,7},{7,4},{8,9},{9,10},{10,1... | collective-permute-start | bytes 2359304 | tf_op jit(solution)/shard_map/ppermute | solution.py:142
  5.8 49.1 %collective-permute-start.3 = (f32[3,2,16,16,128]{4,3,2,1,0:T(8,128)S(1)}, f32[3,2,16,16,128]{4,3,2,1,0:T(8,128)S(1)}, u32[]{:S(2)}, u32[]{:S(2)}) collective-permute-start(f32[3,2,16,16,128]{4,3,2,1,0:T(8,128)S(1)} %get-tuple-element.45), channel_id=1, source_target_pairs={{1,0},{2,1},{3,2},{0,3},{5,4},{6,5},{7,6},{4,7},{9,8},{10,9},{11,1... | collective-permute-start | bytes 2359304 | tf_op jit(solution)/shard_map/ppermute | solution.py:143
  19.6 18.2 %copy-start.10 = (s32[64]{0:T(128)}, s32[64]{0:T(128)S(1)}, u32[]{:S(2)}) copy-start(s32[64]{0:T(128)S(1)} %convert_add_fusion) | copy-start | bytes 772
  19.6 0.6 copy-start.9
  19.8 18.0 %copy-start.4 = (f32[2]{0:T(128)}, f32[2]{0:T(128)S(1)}, u32[]{:S(2)}) copy-start(f32[2]{0:T(128)S(1)} %get-tuple-element.77) | copy-start | bytes 28
  19.8 18.0 %copy-start.5 = (f32[2]{0:T(128)}, f32[2]{0:T(128)S(1)}, u32[]{:S(2)}) copy-start(f32[2]{0:T(128)S(1)} %get-tuple-element.78) | copy-start | bytes 28
  21.5 31.3 %all-to-all-start = ((f32[64,2,4]{2,1,0:T(2,128)}), f32[64,2,4]{2,1,0:T(2,128)S(1)}, u32[]{:S(2)}, u32[]{:S(2)}) async-start(f32[64,2,4]{2,1,0:T(2,128)} %bitcast.3), calls=%async_computation | async-start | bytes 131072 | tf_op jit(solution)/shard_map/all_to_all | solution.py:173
  35.2 18.1 %collective-permute-start = (s32[4,2,16,16]{3,2,1,0:T(8,128)}, s32[4,2,16,16]{3,2,1,0:T(8,128)S(1)}, u32[]{:S(2)}, u32[]{:S(2)}) collective-permute-start(s32[4,2,16,16]{3,2,1,0:T(8,128)} %get-tuple-element.61), channel_id=1, source_target_pairs={{0,1},{1,2},{2,3},{3,0},{4,5},{5,6},{6,7},{7,4},{8,9},{9,10},{10,1... | collective-permute-start | bytes 24584 | tf_op jit(solution)/shard_map/ppermute | solution.py:144
  37.8 15.5 %collective-permute-start.1 = (s32[4,2,16,16]{3,2,1,0:T(8,128)S(1)}, s32[4,2,16,16]{3,2,1,0:T(8,128)S(1)}, u32[]{:S(2)}, u32[]{:S(2)}) collective-permute-start(s32[4,2,16,16]{3,2,1,0:T(8,128)S(1)} %get-tuple-element.60), channel_id=1, source_target_pairs={{1,0},{2,1},{3,2},{0,3},{5,4},{6,5},{7,6},{4,7},{9,8},{10,9},{11,1... | collective-permute-start | bytes 24584 | tf_op jit(solution)/shard_map/ppermute | solution.py:145
  53.3 1.4 %copy-start.1 = (f32[3,4,16,16,128]{4,3,2,1,0:T(8,128)S(1)}, f32[3,4,16,16,128]{4,3,2,1,0:T(8,128)}, u32[]{:S(2)}) copy-start(f32[3,4,16,16,128]{4,3,2,1,0:T(8,128)} %param.16) | copy-start | bytes 4718596
  62.8 3.0 %copy-start = (f32[5,16,16,128]{3,2,1,0:T(8,128)}, f32[5,16,16,128]{3,2,1,0:T(8,128)S(1)}, u32[]{:S(2)}) copy-start(f32[5,16,16,128]{3,2,1,0:T(8,128)S(1)} %get-tuple-element.36) | copy-start | bytes 1966084
  66.5 35.3 %all-to-all-start.1 = ((f32[64,2,3]{2,1,0:T(2,128)}), f32[64,2,3]{2,1,0:T(2,128)}, u32[]{:S(2)}, u32[]{:S(2)}) async-start(f32[64,2,3]{2,1,0:T(2,128)} %bitcast.199), calls=%async_computation.1 | async-start | bytes 131072 | tf_op jit(solution)/shard_map/all_to_all | solution.py:194
  125.0 6.4 %copy-start.3 = (f32[6,32]{1,0:T(8,128)}, f32[6,32]{1,0:T(8,128)S(1)}, u32[]{:S(2)}) copy-start(f32[6,32]{1,0:T(8,128)S(1)} %psum.15) | copy-start | bytes 2308
  126.9 11.0 %collective-permute-start.4 = (f32[6,8]{1,0:T(8,128)S(1)}, f32[6,8]{1,0:T(8,128)S(1)}, u32[]{:S(2)}, u32[]{:S(2)}) collective-permute-start(f32[6,8]{1,0:T(8,128)S(1)} %slice.518), channel_id=1, source_target_pairs={{0,16},{16,32},{32,48},{48,64},{64,80},{80,96},{96,112},{112,128},... | collective-permute-start | bytes 584 | tf_op jit(solution)/shard_map/ppermute | solution.py:42
  128.8 9.9 %copy-start.7 = (f32[6,32]{1,0:T(8,128)S(1)}, f32[6,32]{1,0:T(8,128)}, u32[]{:S(2)}) copy-start(f32[6,32]{1,0:T(8,128)} %param.19) | copy-start | bytes 2308
  128.9 9.9 %copy-start.8 = (f32[6,32]{1,0:T(8,128)S(1)}, f32[6,32]{1,0:T(8,128)}, u32[]{:S(2)}) copy-start(f32[6,32]{1,0:T(8,128)} %param.20) | copy-start | bytes 2308
  128.9 9.9 %copy-start.12 = (f32[32]{0:T(128)S(1)}, f32[32]{0:T(128)}, u32[]{:S(2)}) copy-start(f32[32]{0:T(128)} %param.21) | copy-start | bytes 388

commit v2 on v1

--- a/solution.py
+++ b/solution.py
@@ -123,6 +123,42 @@
     return (lame_field, shear_field)
 
 
+def slot_choice(target, tile_count, capacity, slots):
+    highest = lax.Precision.HIGHEST
+    row_count = target.shape[0]
+    tile_hot = (target[:, None] == jnp.arange(tile_count, dtype=jnp.int32)[None, :]).astype(
+        jnp.float32
+    )
+    row_ids = jnp.arange(row_count, dtype=jnp.int32)
+    earlier_mask = (row_ids[:, None] > row_ids[None, :]).astype(jnp.float32)
+    earlier = jnp.dot(earlier_mask, tile_hot, precision=highest)
+    row_rank = jnp.sum(earlier * tile_hot, axis=1).astype(jnp.int32)
+    slot_index = target * capacity + row_rank
+    return (slot_index[:, None] == jnp.arange(slots, dtype=jnp.int32)[None, :]).astype(
+        jnp.float32
+    )
+
+
+def tile_terms(choose, returned, cosine, sine, heights, elements, per_group):
+    highest = lax.Precision.HIGHEST
+    point_stress = jnp.dot(choose, returned, precision=highest)
+    point_stress = point_stress.T.reshape(3, elements, per_group)
+    global_stress = rotate_out(point_stress, cosine, sine)
+    weight = 1.0 / TP
+    forces = jnp.sum(global_stress, axis=2) * weight
+    moments = jnp.sum(global_stress * heights[None, None, :], axis=2) * weight
+    return jnp.concatenate([forces, moments], 0)
+
+
+def node_forces(bmat, terms, connect, node_count):
+    highest = lax.Precision.HIGHEST
+    corner_force = jnp.einsum("akme,me->ake", bmat, terms, precision=highest)
+    node_hot = (
+        connect[:, :, None] == jnp.arange(node_count + GHOST, dtype=jnp.int32)[None, None, :]
+    ).astype(jnp.float32)
+    return jnp.einsum("ake,aen->kn", corner_force, node_hot, precision=highest)
+
+
 def shards(
     gen_strain, ply_class, route, phase, rve_state, connect, bmat, velocity, force_ext, mass
 ):
@@ -143,6 +179,9 @@
     above = lax.ppermute(rve_state[:, :depth], "rve", down)
     phase_below = lax.ppermute(phase[:, planes - depth :], "rve", up)
     phase_above = lax.ppermute(phase[:, :depth], "rve", down)
+    route_rows = route.reshape(elements, per_group).T
+    prev_ints = from_behind(jnp.concatenate([route_rows, connect], 0), "tile", 1)
+    prev_bmat = from_behind(bmat, "tile", 1)
     layer = thick_index * per_group + jnp.arange(per_group, dtype=jnp.int32)
     heights = -1.0 + (2.0 * layer.astype(jnp.float32) + 1.0) / TP
     classes = lax.dynamic_slice_in_dim(ply_class, thick_index * per_group, per_group)
@@ -157,18 +196,7 @@
     payload = jnp.concatenate(
         [rotated.reshape(3, row_count), row_class.astype(jnp.float32)[None, :]], 0
     ).T
-    target = route.reshape(row_count)
-    tile_hot = (target[:, None] == jnp.arange(tile_count, dtype=jnp.int32)[None, :]).astype(
-        jnp.float32
-    )
-    row_ids = jnp.arange(row_count, dtype=jnp.int32)
-    earlier_mask = (row_ids[:, None] > row_ids[None, :]).astype(jnp.float32)
-    earlier = jnp.dot(earlier_mask, tile_hot, precision=highest)
-    row_rank = jnp.sum(earlier * tile_hot, axis=1).astype(jnp.int32)
-    slot_index = target * capacity + row_rank
-    choose = (slot_index[:, None] == jnp.arange(slots, dtype=jnp.int32)[None, :]).astype(
-        jnp.float32
-    )
+    choose = slot_choice(route.reshape(row_count), tile_count, capacity, slots)
     send = jnp.dot(choose.T, payload, precision=highest)
     received = lax.all_to_all(
         send.reshape(tile_count, capacity, 4), "tile", split_axis=0, concat_axis=0, tiled=True
@@ -191,25 +219,23 @@
             macro,
         )
     average = jnp.stack([jnp.sum(part[1:], axis=(0, 1, 2)) for part in stress]) / float(RES**3)
-    returned = lax.all_to_all(
-        average.T.reshape(tile_count, capacity, 3), "tile", split_axis=0, concat_axis=0, tiled=True
-    )
-    point_stress = jnp.dot(choose, returned.reshape(slots, 3), precision=highest)
-    point_stress = point_stress.T.reshape(3, elements, per_group)
-    global_stress = rotate_out(point_stress, cosine, sine)
-    weight = 1.0 / TP
-    forces = jnp.sum(global_stress, axis=2) * weight
-    moments = jnp.sum(global_stress * heights[None, None, :], axis=2) * weight
-    partial_terms = jnp.concatenate([forces, moments], 0)
-    resultants = lax.psum(lax.psum(partial_terms, "rve"), "thick")
-    corner_force = jnp.einsum("akme,me->ake", bmat, resultants, precision=highest)
+    own_chunks = average.T.reshape(tile_count, capacity, 3)
+    both_chunks = jnp.concatenate([own_chunks, jnp.roll(own_chunks, 1, axis=0)], 1)
+    returned = lax.all_to_all(both_chunks, "tile", split_axis=0, concat_axis=0, tiled=True)
+    own_returned = returned[:, :capacity].reshape(slots, 3)
+    prev_returned = returned[:, capacity:].reshape(slots, 3)
+    own_terms = tile_terms(choose, own_returned, cosine, sine, heights, elements, per_group)
+    prev_route = prev_ints[:per_group].T.reshape(row_count)
+    prev_connect = prev_ints[per_group:]
+    prev_choose = slot_choice(prev_route, tile_count, capacity, slots)
+    prev_terms = tile_terms(prev_choose, prev_returned, cosine, sine, heights, elements, per_group)
     node_count = velocity.shape[1]
-    node_hot = (
-        connect[:, :, None] == jnp.arange(node_count + GHOST, dtype=jnp.int32)[None, None, :]
-    ).astype(jnp.float32)
-    assembled = jnp.einsum("ake,aen->kn", corner_force, node_hot, precision=highest)
-    incoming = from_behind(assembled[:, node_count:], "tile", 1)
-    internal = assembled[:, :node_count].at[:, :GHOST].add(incoming)
+    own_nodes = node_forces(bmat, own_terms, connect, node_count)[:, :node_count]
+    ghost_nodes = node_forces(prev_bmat, prev_terms, prev_connect, node_count)[:, node_count:]
+    partial_internal = own_nodes.at[:, :GHOST].add(ghost_nodes)
+    totals = lax.psum(lax.psum(jnp.concatenate([own_terms, partial_internal], 0), "rve"), "thick")
+    resultants = totals[:6]
+    internal = totals[6:]
     new_velocity = velocity + time_step * (force_ext - internal) / mass[None, :]
     return (new_velocity, resultants, displace)
 

time: 140 us -> 139 us (level)
  the two profiles are of different devices: /device:TPU:8 before, /device:TPU:64 now
where the time goes in v2:
time: 139 us
  starting transfers between devices  61.8 us (44%)
  blocking collectives  22.5 us (16%)
  other arithmetic  18.2 us (13%)
  local copies, waits for them, and re-layouts  15.9 us (11%)
  waiting for transfers between devices  15.5 us (11%)
  matrix products  2.78 us (2%)
  between operations  1.85 us (1%)
    all_to_all x1, starting transfers between devices, shards(): lax.all_to_all(send.reshape(tile_count, capacity, 4), 'tile', split_axis=...  24.2 us
    all_to_all x1, waiting for transfers between devices, shards(): lax.all_to_all(both_chunks, 'tile', split_axis=0, concat_axis=0, tiled=True)  15.5 us
    all_to_all x1, starting transfers between devices, shards(): lax.all_to_all(both_chunks, 'tile', split_axis=0, concat_axis=0, tiled=True)  13.6 us
    psum x1, blocking collectives, shards(): lax.psum(jnp.concatenate([own_terms, partial_internal], 0), 'rve')  11.9 us
    psum x1, blocking collectives, shards(): lax.psum(lax.psum(jnp.concatenate([own_terms, partial_internal], 0), 'rve...  10.6 us
    ppermute x2, starting transfers between devices, from_behind(): return lax.ppermute(value, axis, pairs)  8.74 us
    ppermute x1, starting transfers between devices, shards(): phase_above = lax.ppermute(phase[:, :depth], 'rve', down)  5.72 us
    another operation x4, other arithmetic, relax_slab(): shifted = displace[:, 1:-1] + relax_rate * jnp.stack([first, second, third])  4.38 us
  transfers between devices with their start and end apart: 8, of which 1 were waited for; matrix products, arithmetic and copies ran while one was open for 23% of the time, Pallas kernels for 0%

profile of v2, /device:TPU:64, one launch (start us, length us, event | category | flops | bytes accessed | tf_op | source)
XLA Modules:
  0.0 138.5 jit_solution(17705057834582005989)
XLA Ops:
  0.7 1.6 %fusion.98 = (f32[3,2,16,16,128]{4,3,2,1,0:T(8,128)S(1)}, f32[3,2,16,16,128]{4,3,2,1,0:T(8,128)S(1)}) fusion(f32[3,4,16,16,128]{4,3,2,1,0:T(8,128)} %param.16), kind=kLoop, calls=%fused_computation.240 | loop fusion | bytes 3145728 | tf_op jit(solution)/shard_map/slice | solution.py:179
  2.3 3.5 %collective-permute-start.2 = (f32[3,2,16,16,128]{4,3,2,1,0:T(8,128)S(1)}, f32[3,2,16,16,128]{4,3,2,1,0:T(8,128)S(1)}, u32[]{:S(2)}, u32[]{:S(2)}) collective-permute-start(f32[3,2,16,16,128]{4,3,2,1,0:T(8,128)S(1)} %get-tuple-element.51), channel_id=1, source_target_pairs={{0,1},{1,2},{2,3},{3,0},{4,5},{5,6},{6,7},{7,4},{8,9},{9,10},{10,1... | collective-permute-start | bytes 2359304 | tf_op jit(solution)/shard_map/ppermute | solution.py:178
  5.8 4.2 %collective-permute-start.3 = (f32[3,2,16,16,128]{4,3,2,1,0:T(8,128)S(1)}, f32[3,2,16,16,128]{4,3,2,1,0:T(8,128)S(1)}, u32[]{:S(2)}, u32[]{:S(2)}) collective-permute-start(f32[3,2,16,16,128]{4,3,2,1,0:T(8,128)S(1)} %get-tuple-element.50), channel_id=1, source_target_pairs={{1,0},{2,1},{3,2},{0,3},{5,4},{6,5},{7,6},{4,7},{9,8},{10,9},{11,1... | collective-permute-start | bytes 2359304 | tf_op jit(solution)/shard_map/ppermute | solution.py:179
  10.0 0.1 reshape.789
  10.1 0.2 fusion
  10.4 0.1 fusion.96
  11.0 0.1 stack.59
  11.1 0.1 stack.58
  11.2 0.9 fusion.71
  12.1 24.2 %all-to-all-start = ((f32[64,2,4]{2,1,0:T(2,128)}), f32[64,2,4]{2,1,0:T(2,128)S(1)}, u32[]{:S(2)}, u32[]{:S(2)}) async-start(f32[64,2,4]{2,1,0:T(2,128)} %bitcast.5), calls=%async_computation | async-start | bytes 131072 | tf_op jit(solution)/shard_map/all_to_all | solution.py:201
  36.4 2.1 %collective-permute-start.4 = (s32[6,32]{1,0:T(8,128)S(1)}, s32[6,32]{1,0:T(8,128)S(1)}, u32[]{:S(2)}, u32[]{:S(2)}) collective-permute-start(s32[6,32]{1,0:T(8,128)S(1)} %pad_add_fusion), channel_id=1, source_target_pairs={{0,16},{16,32},{32,48},{48,64},{64,80},{80,96},{96,112},{112,128},... | collective-permute-start | bytes 2312 | tf_op jit(solution)/shard_map/ppermute | solution.py:42
  38.5 0.6 fusion.100
  39.1 1.9 %collective-permute-start = (s32[4,2,16,16]{3,2,1,0:T(8,128)}, s32[4,2,16,16]{3,2,1,0:T(8,128)S(1)}, u32[]{:S(2)}, u32[]{:S(2)}) collective-permute-start(s32[4,2,16,16]{3,2,1,0:T(8,128)} %get-tuple-element.68), channel_id=1, source_target_pairs={{0,1},{1,2},{2,3},{3,0},{4,5},{5,6},{6,7},{7,4},{8,9},{9,10},{10,1... | collective-permute-start | bytes 24584 | tf_op jit(solution)/shard_map/ppermute | solution.py:180
  41.1 5.7 %collective-permute-start.1 = (s32[4,2,16,16]{3,2,1,0:T(8,128)S(1)}, s32[4,2,16,16]{3,2,1,0:T(8,128)S(1)}, u32[]{:S(2)}, u32[]{:S(2)}) collective-permute-start(s32[4,2,16,16]{3,2,1,0:T(8,128)S(1)} %get-tuple-element.67), channel_id=1, source_target_pairs={{1,0},{2,1},{3,2},{0,3},{5,4},{6,5},{7,6},{4,7},{9,8},{10,9},{11,1... | collective-permute-start | bytes 24584 | tf_op jit(solution)/shard_map/ppermute | solution.py:181
  46.8 0.7 compare_reduce_fusion
  47.5 6.7 %collective-permute-start.5 = (f32[4,6,6,32]{3,0,2,1:T(4,128)}, f32[4,6,6,32]{3,0,2,1:T(4,128)}, u32[]{:S(2)}, u32[]{:S(2)}) collective-permute-start(f32[4,6,6,32]{3,0,2,1:T(4,128)} %param.18), channel_id=1, source_target_pairs={{0,16},{16,32},{32,48},{48,64},{64,80},{80,96},{96,112},{112,128},... | collective-permute-start | bytes 55304 | tf_op jit(solution)/shard_map/ppermute | solution.py:42
  54.2 0.6 slice_bitcast_fusion.14
  54.8 0.8 copy.62
  55.5 0.6 reshape.796
  56.1 0.9 fusion.1
  57.0 1.2 convert_add_fusion
  58.2 1.3 slice.572
  59.5 0.2 fusion.62
  59.7 0.2 slice_reduce_fusion.3
  60.0 1.1 multiply_add_fusion.1
  61.4 0.2 constant_dynamic-update-slice_fusion.4
  61.7 0.2 slice_bitcast_fusion.4
  62.6 0.7 fusion.10
  63.5 0.5 multiply_add_fusion.5
  64.0 0.8 multiply_add_fusion.4
  65.0 0.4 fusion.18
  65.4 0.8 fusion.27
  66.2 0.4 slice_add_fusion
  66.5 0.1 slice_bitcast_fusion.9
  67.2 1.3 multiply_add_fusion.6
  68.4 0.4 multiply_add_fusion.8
  69.0 0.5 fusion.33
  69.5 1.3 fusion.56
  70.9 0.8 reshape.792
  71.7 0.9 slice.708
  72.6 0.6 slice.707
  73.2 0.8 slice.560
  74.0 1.0 maximum_maximum_fusion
  75.0 0.7 copy.59
  75.7 13.6 %all-to-all-start.1 = ((f32[64,4,3]{1,2,0:T(4,128)}), f32[64,4,3]{1,2,0:T(4,128)}, u32[]{:S(2)}, u32[]{:S(2)}) async-start(f32[64,4,3]{1,2,0:T(4,128)} %copy.59), calls=%async_computation.1 | async-start | bytes 262144 | tf_op jit(solution)/shard_map/all_to_all | solution.py:224
  89.3 1.1 slice.710
  90.4 1.9 %fusion.46 = f32[1,4,16,16,128]{4,3,2,1,0:T(8,128)S(1)} fusion(f32[5,16,16,128]{3,2,1,0:T(8,128)} %get-tuple-element.28, f32[5,16,15,128]{3,2,1,0:T(8,128)} %bitcast.221, f32[5,16,1,128]{3,2,1,0:T(1,128)S(1)} %slice.710, f32[5,15,16,128]{3,2,1,0:T(8,128)} %slice.708, f32[5,1,16,128]{3,2,1,0:T(8,128)} %slice.707, f32[5,16,16,128]{3,2,1,0:T(8,128)} %copy-done, ...), kind=kLoop, calls=%fused_computation.103 | loop fusion | flops 917504 | bytes 3932160 | tf_op jit(solution)/shard_map/stack | solution.py:110
  92.5 1.4 slice_add_fusion.1
  93.8 15.5 %all-to-all-done.1 = f32[64,4,3]{1,2,0:T(4,128)} async-done(((f32[64,4,3]{1,2,0:T(4,128)}), f32[64,4,3]{1,2,0:T(4,128)}, u32[]{:S(2)}, u32[]{:S(2)}) %all-to-all-start.1) | async-done | bytes 3104 | tf_op jit(solution)/shard_map/all_to_all | solution.py:224
  109.3 1.1 fusion.99
  110.4 0.1 reshape.794
  110.6 0.1 reshape.793
  110.8 0.2 fusion.68
  110.9 0.2 fusion.70
  112.0 0.1 fusion.64
  112.1 0.9 multiply_reduce_fusion.1
  113.1 0.2 convolution_bitcast_fusion.1
  113.3 0.9 multiply_reduce_fusion
  114.2 0.2 convolution_bitcast_fusion
  114.5 0.8 add_select_fusion
  115.2 0.1 scatter-add.4
  115.4 11.9 %psum.14 = f32[12,32]{1,0:T(8,128)S(1)} all-reduce(f32[12,32]{1,0:T(8,128)S(1)} %pad_maximum_fusion.14), channel_id=1, replica_groups=mesh['tile'=64,'thick'=4,'rve'=4] {'rve'}, use_global_device_ids=true, to_apply=%region_10.11 | all-reduce | flops 384 | bytes 3072 | tf_op jit(solution)/shard_map/psum | solution.py:236
  127.3 10.6 %psum.15 = f32[12,32]{1,0:T(8,128)S(1)} all-reduce(f32[12,32]{1,0:T(8,128)S(1)} %psum.14), channel_id=1, replica_groups=mesh['tile'=64,'thick'=4,'rve'=4] {'thick'}, use_global_device_ids=true, to_apply=%region_11.12 | all-reduce | flops 384 | bytes 3072 | tf_op jit(solution)/shard_map/psum | solution.py:236
  137.9 0.6 fusion.101
  (144 shorter events, 3.3 us)
Async XLA Ops:
  0.6 9.3 %copy-start.16 = (s32[1,32,2,1]{1,3,2,0:T(1,128)S(1)}, s32[1,32,2,1]{1,3,2,0:T(1,128)}, u32[]{:S(2)}) copy-start(s32[1,32,2,1]{1,3,2,0:T(1,128)} %param.14) | copy-start | bytes 772
  0.6 9.7 %copy-start.27 = (s32[8]{0:T(128)S(1)}, s32[8]{0:T(128)}, u32[]{:S(2)}) copy-start(s32[8]{0:T(128)} %param.13) | copy-start | bytes 100
  0.7 10.1 %copy-start.17 = (f32[6,32]{1,0:T(8,128)S(1)}, f32[6,32]{1,0:T(8,128)}, u32[]{:S(2)}) copy-start(f32[6,32]{1,0:T(8,128)} %param.12) | copy-start | bytes 2308
  0.7 35.7 %copy-start.21 = (s32[4,32]{1,0:T(4,128)S(1)}, s32[4,32]{1,0:T(4,128)}, u32[]{:S(2)}) copy-start(s32[4,32]{1,0:T(4,128)} %param.17) | copy-start | bytes 1540
  0.7 37.8 %copy-start.3 = (s32[4,4,16,16]{3,2,1,0:T(8,128)S(1)}, s32[4,4,16,16]{3,2,1,0:T(8,128)}, u32[]{:S(2)}) copy-start(s32[4,4,16,16]{3,2,1,0:T(8,128)} %param.15) | copy-start | bytes 49156
  2.3 58.9 %collective-permute-start.2 = (f32[3,2,16,16,128]{4,3,2,1,0:T(8,128)S(1)}, f32[3,2,16,16,128]{4,3,2,1,0:T(8,128)S(1)}, u32[]{:S(2)}, u32[]{:S(2)}) collective-permute-start(f32[3,2,16,16,128]{4,3,2,1,0:T(8,128)S(1)} %get-tuple-element.51), channel_id=1, source_target_pairs={{0,1},{1,2},{2,3},{3,0},{4,5},{5,6},{6,7},{7,4},{8,9},{9,10},{10,1... | collective-permute-start | bytes 2359304 | tf_op jit(solution)/shard_map/ppermute | solution.py:178
  5.8 55.8 %collective-permute-start.3 = (f32[3,2,16,16,128]{4,3,2,1,0:T(8,128)S(1)}, f32[3,2,16,16,128]{4,3,2,1,0:T(8,128)S(1)}, u32[]{:S(2)}, u32[]{:S(2)}) collective-permute-start(f32[3,2,16,16,128]{4,3,2,1,0:T(8,128)S(1)} %get-tuple-element.50), channel_id=1, source_target_pairs={{1,0},{2,1},{3,2},{0,3},{5,4},{6,5},{7,6},{4,7},{9,8},{10,9},{11,1... | collective-permute-start | bytes 2359304 | tf_op jit(solution)/shard_map/ppermute | solution.py:179
  10.3 28.8 %copy-start.24 = (s32[64]{0:T(128)}, s32[64]{0:T(128)S(1)}, u32[]{:S(2)}) copy-start(s32[64]{0:T(128)S(1)} %convert_add_fusion.1) | copy-start | bytes 772
  10.4 0.5 copy-start.19
  10.5 30.5 %copy-start.4 = (f32[2]{0:T(128)}, f32[2]{0:T(128)S(1)}, u32[]{:S(2)}) copy-start(f32[2]{0:T(128)S(1)} %get-tuple-element.32) | copy-start | bytes 28
  10.5 30.5 %copy-start.6 = (f32[2]{0:T(128)}, f32[2]{0:T(128)S(1)}, u32[]{:S(2)}) copy-start(f32[2]{0:T(128)S(1)} %get-tuple-element.91) | copy-start | bytes 28
  10.6 30.5 %copy-start.8 = (f32[2]{0:T(128)}, f32[2]{0:T(128)S(1)}, u32[]{:S(2)}) copy-start(f32[2]{0:T(128)S(1)} %get-tuple-element.93) | copy-start | bytes 28
  10.6 30.5 %copy-start.10 = (f32[2]{0:T(128)}, f32[2]{0:T(128)S(1)}, u32[]{:S(2)}) copy-start(f32[2]{0:T(128)S(1)} %get-tuple-element.94) | copy-start | bytes 28
  10.6 30.5 %copy-start.12 = (f32[2]{0:T(128)}, f32[2]{0:T(128)S(1)}, u32[]{:S(2)}) copy-start(f32[2]{0:T(128)S(1)} %get-tuple-element.95) | copy-start | bytes 28
  12.1 47.4 %all-to-all-start = ((f32[64,2,4]{2,1,0:T(2,128)}), f32[64,2,4]{2,1,0:T(2,128)S(1)}, u32[]{:S(2)}, u32[]{:S(2)}) async-start(f32[64,2,4]{2,1,0:T(2,128)} %bitcast.5), calls=%async_computation | async-start | bytes 131072 | tf_op jit(solution)/shard_map/all_to_all | solution.py:201
  36.4 11.1 %collective-permute-start.4 = (s32[6,32]{1,0:T(8,128)S(1)}, s32[6,32]{1,0:T(8,128)S(1)}, u32[]{:S(2)}, u32[]{:S(2)}) collective-permute-start(s32[6,32]{1,0:T(8,128)S(1)} %pad_add_fusion), channel_id=1, source_target_pairs={{0,16},{16,32},{32,48},{48,64},{64,80},{80,96},{96,112},{112,128},... | collective-permute-start | bytes 2312 | tf_op jit(solution)/shard_map/ppermute | solution.py:42
  39.1 20.8 %collective-permute-start = (s32[4,2,16,16]{3,2,1,0:T(8,128)}, s32[4,2,16,16]{3,2,1,0:T(8,128)S(1)}, u32[]{:S(2)}, u32[]{:S(2)}) collective-permute-start(s32[4,2,16,16]{3,2,1,0:T(8,128)} %get-tuple-element.68), channel_id=1, source_target_pairs={{0,1},{1,2},{2,3},{3,0},{4,5},{5,6},{6,7},{7,4},{8,9},{9,10},{10,1... | collective-permute-start | bytes 24584 | tf_op jit(solution)/shard_map/ppermute | solution.py:180
  41.1 18.9 %collective-permute-start.1 = (s32[4,2,16,16]{3,2,1,0:T(8,128)S(1)}, s32[4,2,16,16]{3,2,1,0:T(8,128)S(1)}, u32[]{:S(2)}, u32[]{:S(2)}) collective-permute-start(s32[4,2,16,16]{3,2,1,0:T(8,128)S(1)} %get-tuple-element.67), channel_id=1, source_target_pairs={{1,0},{2,1},{3,2},{0,3},{5,4},{6,5},{7,6},{4,7},{9,8},{10,9},{11,1... | collective-permute-start | bytes 24584 | tf_op jit(solution)/shard_map/ppermute | solution.py:181
  47.5 6.7 %copy-start.18 = (s32[6,32]{1,0:T(8,128)}, s32[6,32]{1,0:T(8,128)S(1)}, u32[]{:S(2)}) copy-start(s32[6,32]{1,0:T(8,128)S(1)} %collective-permute-done.4) | copy-start | bytes 2308
  47.5 65.8 %collective-permute-start.5 = (f32[4,6,6,32]{3,0,2,1:T(4,128)}, f32[4,6,6,32]{3,0,2,1:T(4,128)}, u32[]{:S(2)}, u32[]{:S(2)}) collective-permute-start(f32[4,6,6,32]{3,0,2,1:T(4,128)} %param.18), channel_id=1, source_target_pairs={{0,16},{16,32},{32,48},{48,64},{64,80},{80,96},{96,112},{112,128},... | collective-permute-start | bytes 55304 | tf_op jit(solution)/shard_map/ppermute | solution.py:42
  60.0 1.4 %copy-start.1 = (f32[3,4,16,16,128]{4,3,2,1,0:T(8,128)S(1)}, f32[3,4,16,16,128]{4,3,2,1,0:T(8,128)}, u32[]{:S(2)}) copy-start(f32[3,4,16,16,128]{4,3,2,1,0:T(8,128)} %param.16) | copy-start | bytes 4718596
  69.4 1.4 %copy-start = (f32[5,16,16,128]{3,2,1,0:T(8,128)}, f32[5,16,16,128]{3,2,1,0:T(8,128)S(1)}, u32[]{:S(2)}) copy-start(f32[5,16,16,128]{3,2,1,0:T(8,128)S(1)} %get-tuple-element.41) | copy-start | bytes 1966084
  75.7 33.6 %all-to-all-start.1 = ((f32[64,4,3]{1,2,0:T(4,128)}), f32[64,4,3]{1,2,0:T(4,128)}, u32[]{:S(2)}, u32[]{:S(2)}) async-start(f32[64,4,3]{1,2,0:T(4,128)} %copy.59), calls=%async_computation.1 | async-start | bytes 262144 | tf_op jit(solution)/shard_map/all_to_all | solution.py:224
  89.3 3.0 %copy-start.2 = (f32[1,4,16,16,128]{4,3,2,1,0:T(8,128)S(1)}, f32[1,4,16,16,128]{4,3,2,1,0:T(8,128)}, u32[]{:S(2)}) copy-start(f32[1,4,16,16,128]{4,3,2,1,0:T(8,128)} %get-tuple-element.55) | copy-start | bytes 1572868
  92.3 18.4 %copy-start.25 = (s32[64]{0:T(128)S(1)}, s32[64]{0:T(128)}, u32[]{:S(2)}) copy-start(s32[64]{0:T(128)} %copy-done.24) | copy-start | bytes 772
  92.3 18.6 %copy-start.28 = (s32[64]{0:T(128)S(1)}, s32[64]{0:T(128)}, u32[]{:S(2)}) copy-start(s32[64]{0:T(128)} %convert_add_fusion) | copy-start | bytes 772
  92.3 19.5 %copy-start.5 = (f32[2]{0:T(128)S(1)}, f32[2]{0:T(128)}, u32[]{:S(2)}) copy-start(f32[2]{0:T(128)} %copy-done.4) | copy-start | bytes 28
  92.3 19.5 %copy-start.7 = (f32[2]{0:T(128)S(1)}, f32[2]{0:T(128)}, u32[]{:S(2)}) copy-start(f32[2]{0:T(128)} %copy-done.6) | copy-start | bytes 28
  92.4 19.5 %copy-start.9 = (f32[2]{0:T(128)S(1)}, f32[2]{0:T(128)}, u32[]{:S(2)}) copy-start(f32[2]{0:T(128)} %copy-done.8) | copy-start | bytes 28
  92.4 19.5 %copy-start.11 = (f32[2]{0:T(128)S(1)}, f32[2]{0:T(128)}, u32[]{:S(2)}) copy-start(f32[2]{0:T(128)} %copy-done.10) | copy-start | bytes 28
  92.4 19.5 %copy-start.13 = (f32[2]{0:T(128)S(1)}, f32[2]{0:T(128)}, u32[]{:S(2)}) copy-start(f32[2]{0:T(128)} %copy-done.12) | copy-start | bytes 28
  92.4 19.6 %copy-start.20 = (f32[2]{0:T(128)S(1)}, f32[2]{0:T(128)}, u32[]{:S(2)}) copy-start(f32[2]{0:T(128)} %copy-done.19) | copy-start | bytes 28
  92.4 20.7 %copy-start.22 = (s32[4,32]{1,0:T(4,128)S(1)}, s32[4,32]{1,0:T(4,128)}, u32[]{:S(2)}) copy-start(s32[4,32]{1,0:T(4,128)} %param.17) | copy-start | bytes 1540
  92.4 21.8 %copy-start.23 = (s32[4,32]{1,0:T(4,128)S(1)}, s32[4,32]{1,0:T(4,128)}, u32[]{:S(2)}) copy-start(s32[4,32]{1,0:T(4,128)} %slice.572) | copy-start | bytes 1540
  92.4 45.5 %copy-start.14 = (f32[6,32]{1,0:T(8,128)S(1)}, f32[6,32]{1,0:T(8,128)}, u32[]{:S(2)}) copy-start(f32[6,32]{1,0:T(8,128)} %param.19) | copy-start | bytes 2308
  92.4 45.5 %copy-start.15 = (f32[6,32]{1,0:T(8,128)S(1)}, f32[6,32]{1,0:T(8,128)}, u32[]{:S(2)}) copy-start(f32[6,32]{1,0:T(8,128)} %param.20) | copy-start | bytes 2308
  92.4 45.5 %copy-start.26 = (f32[32]{0:T(128)S(1)}, f32[32]{0:T(128)}, u32[]{:S(2)}) copy-start(f32[32]{0:T(128)} %param.21) | copy-start | bytes 388

commit v3 on v2

--- a/solution.py
+++ b/solution.py
@@ -159,6 +159,18 @@
     return jnp.einsum("ake,aen->kn", corner_force, node_hot, precision=highest)
 
 
+def halo_pack(cells, phase_planes, pairs):
+    lanes = cells.shape[-1]
+    rows = cells.shape[-2]
+    flat_cells = cells.reshape(-1, rows, lanes)
+    flat_phase = phase_planes.astype(jnp.float32).reshape(-1, rows, lanes)
+    moved = lax.ppermute(jnp.concatenate([flat_cells, flat_phase], 0), "rve", pairs)
+    count = flat_cells.shape[0]
+    cells_in = moved[:count].reshape(cells.shape)
+    phase_in = moved[count:].reshape(phase_planes.shape).astype(jnp.int32)
+    return (cells_in, phase_in)
+
+
 def shards(
     gen_strain, ply_class, route, phase, rve_state, connect, bmat, velocity, force_ext, mass
 ):
@@ -175,13 +187,14 @@
     up = [(i, (i + 1) % slab_count) for i in range(slab_count)]
     down = [((i + 1) % slab_count, i) for i in range(slab_count)]
     planes = rve_state.shape[1]
-    below = lax.ppermute(rve_state[:, planes - depth :], "rve", up)
-    above = lax.ppermute(rve_state[:, :depth], "rve", down)
-    phase_below = lax.ppermute(phase[:, planes - depth :], "rve", up)
-    phase_above = lax.ppermute(phase[:, :depth], "rve", down)
+    below, phase_below = halo_pack(rve_state[:, planes - depth :], phase[:, planes - depth :], up)
+    above, phase_above = halo_pack(rve_state[:, :depth], phase[:, :depth], down)
     route_rows = route.reshape(elements, per_group).T
-    prev_ints = from_behind(jnp.concatenate([route_rows, connect], 0), "tile", 1)
-    prev_bmat = from_behind(bmat, "tile", 1)
+    int_rows = jnp.concatenate([route_rows, connect], 0)
+    flat_bmat = bmat.reshape(-1, elements)
+    prev_pack = from_behind(jnp.concatenate([flat_bmat, int_rows.astype(jnp.float32)], 0), "tile", 1)
+    prev_bmat = prev_pack[: flat_bmat.shape[0]].reshape(bmat.shape)
+    prev_ints = prev_pack[flat_bmat.shape[0] :].astype(jnp.int32)
     layer = thick_index * per_group + jnp.arange(per_group, dtype=jnp.int32)
     heights = -1.0 + (2.0 * layer.astype(jnp.float32) + 1.0) / TP
     classes = lax.dynamic_slice_in_dim(ply_class, thick_index * per_group, per_group)

time: 139 us -> 152 us (1.094)
  the two profiles are of different devices: /device:TPU:64 before, /device:TPU:8 now
where the time goes in v3:
time: 152 us; the launch traced here: 151 us
  starting transfers between devices  42.4 us (28%)
  waiting for transfers between devices  31.7 us (21%)
  local copies, waits for them, and re-layouts  25.8 us (17%)
  blocking collectives  25 us (16%)
  other arithmetic  22.5 us (15%)
  matrix products  2.05 us (1%)
  between operations  1.82 us (1%)
    ppermute x2, starting transfers between devices, halo_pack(): lax.ppermute(jnp.concatenate([flat_cells, flat_phase], 0), 'rve', pairs)  16.9 us
    all_to_all x1, waiting for transfers between devices, shards(): lax.all_to_all(both_chunks, 'tile', split_axis=0, concat_axis=0, tiled=True)  16.3 us
    all_to_all x1, waiting for transfers between devices, shards(): lax.all_to_all(send.reshape(tile_count, capacity, 4), 'tile', split_axis=...  15.4 us
    psum x1, blocking collectives, shards(): lax.psum(jnp.concatenate([own_terms, partial_internal], 0), 'rve')  14.4 us
    all_to_all x1, starting transfers between devices, shards(): lax.all_to_all(send.reshape(tile_count, capacity, 4), 'tile', split_axis=...  13 us
    psum x1, blocking collectives, shards(): lax.psum(lax.psum(jnp.concatenate([own_terms, partial_internal], 0), 'rve...  10.6 us
    all_to_all x1, starting transfers between devices, shards(): lax.all_to_all(both_chunks, 'tile', split_axis=0, concat_axis=0, tiled=True)  10.5 us
    slice x12, local copies, waits for them, and re-layouts, relax_slab(): jnp.roll(front[i], -1, 1) - front[i]  4.37 us
  transfers between devices with their start and end apart: 5, of which 2 were waited for; matrix products, arithmetic and copies ran while one was open for 8% of the time, Pallas kernels for 0%

profile of v3, /device:TPU:8, one launch (start us, length us, event | category | flops | bytes accessed | tf_op | source)
XLA Modules:
  0.0 151.3 jit_solution(14675174519936483766)
XLA Ops:
  0.6 0.9 slice_convert_fusion.6
  1.6 1.5 %fusion.97 = (f32[3,2,16,16,128]{4,3,2,1,0:T(8,128)S(1)}, f32[3,2,16,16,128]{4,3,2,1,0:T(8,128)S(1)}) fusion(f32[3,4,16,16,128]{4,3,2,1,0:T(8,128)} %param.16), kind=kLoop, calls=%fused_computation.245 | loop fusion | bytes 3145728 | tf_op jit(solution)/shard_map/slice | solution.py:190
  3.3 15.0 %collective-permute-start.1 = (f32[97,16,128]{2,1,0:T(8,128)S(1)}, f32[97,16,128]{2,1,0:T(8,128)S(1)}, u32[]{:S(2)}, u32[]{:S(2)}) collective-permute-start(f32[97,16,128]{2,1,0:T(8,128)S(1)} %pad_maximum_fusion.2), channel_id=1, source_target_pairs={{1,0},{2,1},{3,2},{0,3},{5,4},{6,5},{7,6},{4,7},{9,8},{10,9},{11,1... | collective-permute-start | bytes 2383880 | tf_op jit(solution)/shard_map/ppermute | solution.py:167
  18.4 0.9 pad_maximum_fusion.1
  19.3 1.9 %collective-permute-start = (f32[97,16,128]{2,1,0:T(8,128)}, f32[97,16,128]{2,1,0:T(8,128)S(1)}, u32[]{:S(2)}, u32[]{:S(2)}) collective-permute-start(f32[97,16,128]{2,1,0:T(8,128)} %pad_maximum_fusion.1), channel_id=1, source_target_pairs={{0,1},{1,2},{2,3},{3,0},{4,5},{5,6},{6,7},{7,4},{8,9},{9,10},{10,1... | collective-permute-start | bytes 2383880 | tf_op jit(solution)/shard_map/ppermute | solution.py:167
  22.4 0.9 fusion.71
  23.4 13.0 %all-to-all-start = ((f32[64,2,4]{2,1,0:T(2,128)}), f32[64,2,4]{2,1,0:T(2,128)S(1)}, u32[]{:S(2)}, u32[]{:S(2)}) async-start(f32[64,2,4]{2,1,0:T(2,128)} %bitcast.7), calls=%async_computation | async-start | bytes 131072 | tf_op jit(solution)/shard_map/all_to_all | solution.py:214
  36.7 2.0 %collective-permute-start.2 = (f32[150,32]{0,1:T(8,128)S(1)}, f32[150,32]{0,1:T(8,128)S(1)}, u32[]{:S(2)}, u32[]{:S(2)}) collective-permute-start(f32[150,32]{0,1:T(8,128)S(1)} %pad_maximum_fusion.17), channel_id=1, source_target_pairs={{0,16},{16,32},{32,48},{48,64},{64,80},{80,96},{96,112},{112,128},... | collective-permute-start | bytes 57608 | tf_op jit(solution)/shard_map/ppermute | solution.py:42
  38.7 0.6 compare_reduce_fusion
  39.3 15.4 %all-to-all-done = f32[64,2,4]{2,1,0:T(2,128)S(1)} async-done(((f32[64,2,4]{2,1,0:T(2,128)}), f32[64,2,4]{2,1,0:T(2,128)S(1)}, u32[]{:S(2)}, u32[]{:S(2)}) %all-to-all-start) | async-done | bytes 2080 | tf_op jit(solution)/shard_map/all_to_all | solution.py:214
  54.9 0.5 slice_bitcast_fusion.18
  55.4 0.2 slice_reduce_fusion.3
  55.9 0.7 copy.100
  56.7 0.7 reshape.832
  57.5 0.5 convert_add_fusion
  58.2 0.7 copy-done.10
  58.9 0.3 copy-done.11
  59.2 1.7 %pad_maximum_fusion = f32[3,8,16,16,128]{4,3,2,1,0:T(8,128)S(1)} fusion(f32[3,2,16,16,128]{4,3,2,1,0:T(8,128)S(1)} %bitcast.231, f32[3,4,16,16,128]{4,3,2,1,0:T(8,128)} %param.16, f32[3,2,16,16,128]{4,3,2,1,0:T(8,128)S(1)} %bitcast.232), kind=kLoop, calls=%fused_computation | loop fusion | flops 1572864 | bytes 6291456 | tf_op jit(solution)/shard_map/concatenate | solution.py:224
  60.9 0.3 slice_bitcast_fusion.4
  61.2 1.0 slice.654
  62.2 1.0 slice.651
  63.2 1.0 slice.666
  64.3 0.6 slice.661
  64.9 1.0 slice.660
  65.9 0.6 slice.680
  66.5 1.0 slice.679
  67.5 0.7 slice.678
  68.2 1.0 slice.677
  69.2 0.7 slice_convert_fusion.9
  70.1 0.7 copy-done.13
  70.8 0.7 slice_convert_fusion.8
  71.6 0.6 constant_dynamic-update-slice_fusion
  72.2 1.1 fusion.63
  73.3 1.8 %multiply_add_fusion.1 = (f32[8,16,16,128]{3,2,1,0:T(8,128)S(1)}, f32[8,16,16,128]{3,2,1,0:T(8,128)S(1)}) fusion(f32[128]{0:T(128)} %get-tuple-element.86, f32[8,16,16]{2,1,0:T(8,128)S(1)} %get-tuple-element.62, f32[128]{0:T(128)} %get-tuple-element.87, f32[8,16,16]{2,1,0:T(8,128)S(1)} %get-tuple-element.63, f32[128]{0:T(128)} %get-tuple-element.88, ...), kind=kLoop, calls=%fused_computation.12 | loop fusion | flops 2883584 | bytes 2131968 | tf_op jit(solution)/shard_map/add | solution.py:121
  75.2 0.6 fusion.10
  76.1 0.9 copy-done.3
  77.1 0.3 copy-done.4
  77.3 0.7 multiply_add_fusion.5
  78.0 0.5 copy-done.5
  78.5 0.8 multiply_add_fusion.4
  79.5 0.4 fusion.18
  79.9 0.6 fusion.27
  80.5 0.3 slice_add_fusion
  81.5 1.2 multiply_add_fusion.6
  82.8 0.4 multiply_add_fusion.8
  83.3 0.5 fusion.33
  83.9 1.3 fusion.56
  85.2 0.8 reshape.826
  86.0 0.9 slice.740
  86.9 0.6 slice.739
  87.5 0.8 slice.582
  88.3 1.2 maximum_maximum_fusion
  89.5 0.7 copy.93
  90.2 10.5 %all-to-all-start.1 = ((f32[64,4,3]{1,2,0:T(4,128)}), f32[64,4,3]{1,2,0:T(4,128)}, u32[]{:S(2)}, u32[]{:S(2)}) async-start(f32[64,4,3]{1,2,0:T(4,128)} %copy.93), calls=%async_computation.1 | async-start | bytes 262144 | tf_op jit(solution)/shard_map/all_to_all | solution.py:237
  100.7 1.1 slice.742
  101.7 1.9 %fusion.46 = f32[1,4,16,16,128]{4,3,2,1,0:T(8,128)S(1)} fusion(f32[5,16,16,128]{3,2,1,0:T(8,128)} %get-tuple-element.28, f32[5,16,15,128]{3,2,1,0:T(8,128)} %bitcast.230, f32[5,16,1,128]{3,2,1,0:T(1,128)S(1)} %slice.742, f32[5,15,16,128]{3,2,1,0:T(8,128)} %slice.740, f32[5,1,16,128]{3,2,1,0:T(8,128)} %slice.739, f32[5,16,16,128]{3,2,1,0:T(8,128)} %copy-done.2, ...), kind=kLoop, calls=%fused_computation.106 | loop fusion | flops 917504 | bytes 3932160 | tf_op jit(solution)/shard_map/stack | solution.py:110
  103.8 1.4 slice_add_fusion.1
  105.2 16.3 %all-to-all-done.1 = f32[64,4,3]{1,2,0:T(4,128)} async-done(((f32[64,4,3]{1,2,0:T(4,128)}), f32[64,4,3]{1,2,0:T(4,128)}, u32[]{:S(2)}, u32[]{:S(2)}) %all-to-all-start.1) | async-done | bytes 3104 | tf_op jit(solution)/shard_map/all_to_all | solution.py:237
  121.4 1.1 fusion.98
  123.1 0.2 fusion.70
  124.8 0.7 add_select_fusion
  125.6 14.4 %psum.14 = f32[12,32]{1,0:T(8,128)S(1)} all-reduce(f32[12,32]{1,0:T(8,128)S(1)} %pad_maximum_fusion.18), channel_id=1, replica_groups=mesh['tile'=64,'thick'=4,'rve'=4] {'rve'}, use_global_device_ids=true, to_apply=%region_10.11 | all-reduce | flops 384 | bytes 3072 | tf_op jit(solution)/shard_map/psum | solution.py:249
  140.1 10.6 %psum.15 = f32[12,32]{1,0:T(8,128)S(1)} all-reduce(f32[12,32]{1,0:T(8,128)S(1)} %psum.14), channel_id=1, replica_groups=mesh['tile'=64,'thick'=4,'rve'=4] {'thick'}, use_global_device_ids=true, to_apply=%region_11.12 | all-reduce | flops 384 | bytes 3072 | tf_op jit(solution)/shard_map/psum | solution.py:249
  150.7 0.6 fusion.99
  (168 shorter events, 5.9 us)
Async XLA Ops:
  3.2 18.1 %copy-start.24 = (s32[1,32,2,1]{1,3,2,0:T(1,128)S(1)}, s32[1,32,2,1]{1,3,2,0:T(1,128)}, u32[]{:S(2)}) copy-start(s32[1,32,2,1]{1,3,2,0:T(1,128)} %param.14) | copy-start | bytes 772
  3.2 18.5 %copy-start.34 = (s32[8]{0:T(128)S(1)}, s32[8]{0:T(128)}, u32[]{:S(2)}) copy-start(s32[8]{0:T(128)} %param.13) | copy-start | bytes 100
  3.2 18.8 %copy-start.25 = (f32[6,32]{1,0:T(8,128)S(1)}, f32[6,32]{1,0:T(8,128)}, u32[]{:S(2)}) copy-start(f32[6,32]{1,0:T(8,128)} %param.12) | copy-start | bytes 2308
  3.2 33.2 %copy-start.28 = (s32[4,32]{1,0:T(4,128)S(1)}, s32[4,32]{1,0:T(4,128)}, u32[]{:S(2)}) copy-start(s32[4,32]{1,0:T(4,128)} %param.17) | copy-start | bytes 1540
  3.2 33.3 %copy-start.15 = (f32[4,6,6,32]{3,0,2,1:T(4,128)S(1)}, f32[4,6,6,32]{3,0,2,1:T(4,128)}, u32[]{:S(2)}) copy-start(f32[4,6,6,32]{3,0,2,1:T(4,128)} %param.18) | copy-start | bytes 55300
  3.3 54.7 %collective-permute-start.1 = (f32[97,16,128]{2,1,0:T(8,128)S(1)}, f32[97,16,128]{2,1,0:T(8,128)S(1)}, u32[]{:S(2)}, u32[]{:S(2)}) collective-permute-start(f32[97,16,128]{2,1,0:T(8,128)S(1)} %pad_maximum_fusion.2), channel_id=1, source_target_pairs={{1,0},{2,1},{3,2},{0,3},{5,4},{6,5},{7,6},{4,7},{9,8},{10,9},{11,1... | collective-permute-start | bytes 2383880 | tf_op jit(solution)/shard_map/ppermute | solution.py:167
  19.3 38.8 %collective-permute-start = (f32[97,16,128]{2,1,0:T(8,128)}, f32[97,16,128]{2,1,0:T(8,128)S(1)}, u32[]{:S(2)}, u32[]{:S(2)}) collective-permute-start(f32[97,16,128]{2,1,0:T(8,128)} %pad_maximum_fusion.1), channel_id=1, source_target_pairs={{0,1},{1,2},{2,3},{3,0},{4,5},{5,6},{6,7},{7,4},{8,9},{9,10},{10,1... | collective-permute-start | bytes 2383880 | tf_op jit(solution)/shard_map/ppermute | solution.py:167
  21.6 36.6 %copy-start.31 = (s32[64]{0:T(128)}, s32[64]{0:T(128)S(1)}, u32[]{:S(2)}) copy-start(s32[64]{0:T(128)S(1)} %convert_add_fusion.1) | copy-start | bytes 772
  21.6 36.5 %copy-start.26 = (f32[2]{0:T(128)}, f32[2]{0:T(128)S(1)}, u32[]{:S(2)}) copy-start(f32[2]{0:T(128)S(1)} %multiply_add_fusion.13) | copy-start | bytes 28
  21.8 36.4 %copy-start.20 = (f32[2]{0:T(128)}, f32[2]{0:T(128)S(1)}, u32[]{:S(2)}) copy-start(f32[2]{0:T(128)S(1)} %get-tuple-element.95) | copy-start | bytes 28
  23.4 31.3 %all-to-all-start = ((f32[64,2,4]{2,1,0:T(2,128)}), f32[64,2,4]{2,1,0:T(2,128)S(1)}, u32[]{:S(2)}, u32[]{:S(2)}) async-start(f32[64,2,4]{2,1,0:T(2,128)} %bitcast.7), calls=%async_computation | async-start | bytes 131072 | tf_op jit(solution)/shard_map/all_to_all | solution.py:214
  36.7 18.9 %collective-permute-start.2 = (f32[150,32]{0,1:T(8,128)S(1)}, f32[150,32]{0,1:T(8,128)S(1)}, u32[]{:S(2)}, u32[]{:S(2)}) collective-permute-start(f32[150,32]{0,1:T(8,128)S(1)} %pad_maximum_fusion.17), channel_id=1, source_target_pairs={{0,16},{16,32},{32,48},{48,64},{64,80},{80,96},{96,112},{112,128},... | collective-permute-start | bytes 57608 | tf_op jit(solution)/shard_map/ppermute | solution.py:42
  58.0 0.9 copy-start.10
  58.1 1.1 copy-start.11
  65.9 4.1 %copy-start.12 = (s32[4,4,16,16]{3,2,1,0:T(8,128)S(1)}, s32[4,4,16,16]{3,2,1,0:T(8,128)}, u32[]{:S(2)}) copy-start(s32[4,4,16,16]{3,2,1,0:T(8,128)} %param.15) | copy-start | bytes 49156
  70.0 5.1 %copy-start.17 = (f32[7,1,16,128]{3,2,1,0:T(8,128)S(1)}, f32[7,1,16,128]{3,2,1,0:T(8,128)}, u32[]{:S(2)}) copy-start(f32[7,1,16,128]{3,2,1,0:T(8,128)} %slice.661) | copy-start | bytes 172036
  70.0 0.7 copy-start.13
  71.5 3.6 %copy-start.6 = (f32[7,16,15,128]{3,2,1,0:T(8,128)S(1)}, f32[7,16,15,128]{3,2,1,0:T(8,128)}, u32[]{:S(2)}) copy-start(f32[7,16,15,128]{3,2,1,0:T(8,128)} %slice.677) | copy-start | bytes 2580484
  71.6 3.6 %copy-start.7 = (f32[7,15,16,128]{3,2,1,0:T(8,128)S(1)}, f32[7,15,16,128]{3,2,1,0:T(8,128)}, u32[]{:S(2)}) copy-start(f32[7,15,16,128]{3,2,1,0:T(8,128)} %slice.660) | copy-start | bytes 2580484
  71.6 3.6 %copy-start.8 = (f32[7,15,16,128]{3,2,1,0:T(8,128)S(1)}, f32[7,15,16,128]{3,2,1,0:T(8,128)}, u32[]{:S(2)}) copy-start(f32[7,15,16,128]{3,2,1,0:T(8,128)} %slice.679) | copy-start | bytes 2580484
  71.6 3.6 %copy-start.18 = (f32[7,1,16,128]{3,2,1,0:T(8,128)S(1)}, f32[7,1,16,128]{3,2,1,0:T(8,128)}, u32[]{:S(2)}) copy-start(f32[7,1,16,128]{3,2,1,0:T(8,128)} %slice.680) | copy-start | bytes 172036
  71.6 3.6 %copy-start.19 = (f32[7,16,1,128]{3,2,1,0:T(1,128)S(1)}, f32[7,16,1,128]{3,2,1,0:T(1,128)}, u32[]{:S(2)}) copy-start(f32[7,16,1,128]{3,2,1,0:T(1,128)} %slice.678) | copy-start | bytes 172036
  75.9 1.2 copy-start.3
  75.9 1.4 copy-start.4
  77.3 1.2 copy-start.5
  80.8 2.4 %copy-start = (f32[3,6,16,16,128]{4,3,2,1,0:T(8,128)}, f32[3,6,16,16,128]{4,3,2,1,0:T(8,128)S(1)}, u32[]{:S(2)}) copy-start(f32[3,6,16,16,128]{4,3,2,1,0:T(8,128)S(1)} %slice_add_fusion) | copy-start | bytes 7077892
  83.7 1.4 copy-start.2
  88.3 15.4 %copy-start.1 = (f32[3,6,16,16,128]{4,3,2,1,0:T(8,128)S(1)}, f32[3,6,16,16,128]{4,3,2,1,0:T(8,128)}, u32[]{:S(2)}) copy-start(f32[3,6,16,16,128]{4,3,2,1,0:T(8,128)} %copy-done) | copy-start | bytes 7077892
  90.2 31.3 %all-to-all-start.1 = ((f32[64,4,3]{1,2,0:T(4,128)}), f32[64,4,3]{1,2,0:T(4,128)}, u32[]{:S(2)}, u32[]{:S(2)}) async-start(f32[64,4,3]{1,2,0:T(4,128)} %copy.93), calls=%async_computation.1 | async-start | bytes 262144 | tf_op jit(solution)/shard_map/all_to_all | solution.py:237
  100.6 3.0 %copy-start.9 = (f32[1,4,16,16,128]{4,3,2,1,0:T(8,128)S(1)}, f32[1,4,16,16,128]{4,3,2,1,0:T(8,128)}, u32[]{:S(2)}) copy-start(f32[1,4,16,16,128]{4,3,2,1,0:T(8,128)} %get-tuple-element.55) | copy-start | bytes 1572868
  103.7 19.2 %copy-start.32 = (s32[64]{0:T(128)S(1)}, s32[64]{0:T(128)}, u32[]{:S(2)}) copy-start(s32[64]{0:T(128)} %copy-done.31) | copy-start | bytes 772
  103.7 19.4 %copy-start.35 = (s32[64]{0:T(128)S(1)}, s32[64]{0:T(128)}, u32[]{:S(2)}) copy-start(s32[64]{0:T(128)} %convert_add_fusion) | copy-start | bytes 772
  103.7 20.3 %copy-start.21 = (f32[2]{0:T(128)S(1)}, f32[2]{0:T(128)}, u32[]{:S(2)}) copy-start(f32[2]{0:T(128)} %copy-done.20) | copy-start | bytes 28
  103.7 20.3 %copy-start.27 = (f32[2]{0:T(128)S(1)}, f32[2]{0:T(128)}, u32[]{:S(2)}) copy-start(f32[2]{0:T(128)} %copy-done.26) | copy-start | bytes 28
  103.7 20.5 %copy-start.16 = (f32[4,6,6,32]{3,0,2,1:T(4,128)S(1)}, f32[4,6,6,32]{3,0,2,1:T(4,128)}, u32[]{:S(2)}) copy-start(f32[4,6,6,32]{3,0,2,1:T(4,128)} %param.18) | copy-start | bytes 55300
  103.7 20.5 %copy-start.29 = (s32[4,32]{1,0:T(4,128)S(1)}, s32[4,32]{1,0:T(4,128)}, u32[]{:S(2)}) copy-start(s32[4,32]{1,0:T(4,128)} %param.17) | copy-start | bytes 1540
  103.7 20.8 %copy-start.14 = (f32[4,6,6,32]{3,2,1,0:T(8,128)S(1)}, f32[4,6,6,32]{3,2,1,0:T(8,128)}, u32[]{:S(2)}) copy-start(f32[4,6,6,32]{3,2,1,0:T(8,128)} %reshape.832) | copy-start | bytes 55300
  103.7 20.8 %copy-start.30 = (s32[4,32]{1,0:T(4,128)S(1)}, s32[4,32]{1,0:T(4,128)}, u32[]{:S(2)}) copy-start(s32[4,32]{1,0:T(4,128)} %copy.100) | copy-start | bytes 1540
  103.8 46.9 %copy-start.22 = (f32[6,32]{1,0:T(8,128)S(1)}, f32[6,32]{1,0:T(8,128)}, u32[]{:S(2)}) copy-start(f32[6,32]{1,0:T(8,128)} %param.19) | copy-start | bytes 2308
  103.8 46.9 %copy-start.23 = (f32[6,32]{1,0:T(8,128)S(1)}, f32[6,32]{1,0:T(8,128)}, u32[]{:S(2)}) copy-start(f32[6,32]{1,0:T(8,128)} %param.20) | copy-start | bytes 2308
  103.8 46.9 %copy-start.33 = (f32[32]{0:T(128)S(1)}, f32[32]{0:T(128)}, u32[]{:S(2)}) copy-start(f32[32]{0:T(128)} %param.21) | copy-start | bytes 388

commit v4 on v2

--- a/solution.py
+++ b/solution.py
@@ -3,6 +3,8 @@
 import jax
 import jax.numpy as jnp
 from jax import lax
+from jax.experimental import pallas as pl
+from jax.experimental.pallas import tpu as pltpu
 from jax.sharding import PartitionSpec as P
 
 TP = 8
@@ -157,6 +159,77 @@
         connect[:, :, None] == jnp.arange(node_count + GHOST, dtype=jnp.int32)[None, None, :]
     ).astype(jnp.float32)
     return jnp.einsum("ake,aen->kn", corner_force, node_hot, precision=highest)
+
+
+def shift_rows(field, shift, axis):
+    if axis == 1:
+        size = field.shape[1]
+        cut = (size - shift) % size
+        return jnp.concatenate([field[:, cut:], field[:, :cut]], 1)
+    return pltpu.roll(field, shift % field.shape[axis], axis)
+
+
+def kernel_sweep(cells, lame_field, shear_field, macro):
+    front = [part[:-1] for part in cells]
+    grads = [
+        [
+            cells[i][1:] - front[i],
+            shift_rows(front[i], -1, 1) - front[i],
+            shift_rows(front[i], -1, 2) - front[i],
+        ]
+        for i in range(3)
+    ]
+    s11, s22, s33, s12, s13, s23 = material_stress(grads, lame_field, shear_field, macro)
+
+    def diff(field, axis):
+        if axis == 0:
+            return field[1:] - field[:-1]
+        return (field - shift_rows(field, 1, axis))[1:]
+
+    first = diff(s11, 0) + diff(s12, 1) + diff(s13, 2)
+    second = diff(s12, 0) + diff(s22, 1) + diff(s23, 2)
+    third = diff(s13, 0) + diff(s23, 1) + diff(s33, 2)
+    moved = [
+        cells[i][1:-1] + relax_rate * rate_term
+        for i, rate_term in enumerate((first, second, third))
+    ]
+    return (moved, (s11, s22, s12))
+
+
+def relax_kernel(cells_ref, lame_ref, shear_ref, macro_ref, out_ref, mean_ref):
+    cells = [cells_ref[i] for i in range(3)]
+    lame_all = lame_ref[...]
+    shear_all = shear_ref[...]
+    macro = [macro_ref[k : k + 1, :].reshape(1, 1, 1, -1) for k in range(3)]
+    stress = None
+    for round_number in range(ITERS):
+        count = cells[0].shape[0]
+        cells, stress = kernel_sweep(
+            cells,
+            lame_all[round_number : round_number + count - 1],
+            shear_all[round_number : round_number + count - 1],
+            macro,
+        )
+    for i in range(3):
+        out_ref[i] = cells[i]
+    for k in range(3):
+        total = jnp.sum(stress[k][1:], axis=(0, 1))
+        mean_ref[k : k + 1, :] = jnp.sum(total, axis=0, keepdims=True) / float(RES**3)
+
+
+def relax_slab_kernel(displace, lame_field, shear_field, macro):
+    planes = displace.shape[1] - 2 * ITERS
+    out_shape = (
+        jax.ShapeDtypeStruct((3, planes) + displace.shape[2:], jnp.float32),
+        jax.ShapeDtypeStruct((3, displace.shape[-1]), jnp.float32),
+    )
+    return pl.pallas_call(
+        relax_kernel,
+        out_shape=out_shape,
+        in_specs=[pl.BlockSpec(memory_space=pltpu.VMEM)] * 4,
+        out_specs=(pl.BlockSpec(memory_space=pltpu.VMEM), pl.BlockSpec(memory_space=pltpu.VMEM)),
+        compiler_params=pltpu.CompilerParams(vmem_limit_bytes=60 * 1024 * 1024),
+    )(displace, lame_field, shear_field, macro)
 
 
 def shards(
@@ -209,16 +282,7 @@
     wide_phase = jnp.concatenate([phase_below, phase, phase_above], 1)
     lame_field, shear_field = moduli_planes(wide_phase, class_hot)
     displace = jnp.concatenate([below, rve_state, above], 1)
-    stress = None
-    for round_number in range(ITERS):
-        count = displace.shape[1]
-        displace, stress = relax_slab(
-            displace,
-            lame_field[round_number : round_number + count - 1],
-            shear_field[round_number : round_number + count - 1],
-            macro,
-        )
-    average = jnp.stack([jnp.sum(part[1:], axis=(0, 1, 2)) for part in stress]) / float(RES**3)
+    displace, average = relax_slab_kernel(displace, lame_field, shear_field, macro)
     own_chunks = average.T.reshape(tile_count, capacity, 3)
     both_chunks = jnp.concatenate([own_chunks, jnp.roll(own_chunks, 1, axis=0)], 1)
     returned = lax.all_to_all(both_chunks, "tile", split_axis=0, concat_axis=0, tiled=True)

time: 139 us -> 162 us (1.17)
  the two profiles are of different devices: /device:TPU:64 before, /device:TPU:8 now
where the time goes in v4:
time: 162 us; the launch traced here: 161 us
  starting transfers between devices  65.1 us (40%)
  waiting for transfers between devices  37.8 us (23%)
  blocking collectives  21.4 us (13%)
  local copies, waits for them, and re-layouts  16 us (10%)
  other arithmetic  9.27 us (6%)
  Pallas kernels  7.19 us (4%)
  matrix products  3.34 us (2%)
    all_to_all x1, starting transfers between devices, shards(): lax.all_to_all(send.reshape(tile_count, capacity, 4), 'tile', split_axis=...  24.1 us
    all_to_all x1, waiting for transfers between devices, shards(): lax.all_to_all(both_chunks, 'tile', split_axis=0, concat_axis=0, tiled=True)  20.9 us
    all_to_all x1, starting transfers between devices, shards(): lax.all_to_all(both_chunks, 'tile', split_axis=0, concat_axis=0, tiled=True)  18.9 us
    ppermute x1, waiting for transfers between devices, shards(): above = lax.ppermute(rve_state[:, :depth], 'rve', down)  16.9 us
    psum x1, blocking collectives, shards(): lax.psum(jnp.concatenate([own_terms, partial_internal], 0), 'rve')  10.8 us
    psum x1, blocking collectives, shards(): lax.psum(lax.psum(jnp.concatenate([own_terms, partial_internal], 0), 'rve...  10.6 us
    ppermute x2, starting transfers between devices, from_behind(): return lax.ppermute(value, axis, pairs)  9.26 us
    pallas_call x1, Pallas kernels, relax_slab_kernel(): pl.pallas_call(relax_kernel, out_shape=out_shape, in_specs=[pl.BlockSpec(...  7.19 us
  transfers between devices with their start and end apart: 8, of which 2 were waited for; matrix products, arithmetic and copies ran while one was open for 14% of the time, Pallas kernels for 4%

profile of v4, /device:TPU:8, one launch (start us, length us, event | category | flops | bytes accessed | tf_op | source)
XLA Modules:
  0.0 161.4 jit_solution(3364175738040765865)
XLA Ops:
  0.6 0.0 copy-start.1
  0.7 0.8 fusion.38
  1.6 0.8 fusion.44
  2.4 0.1 multiply_add_fusion.3
  2.5 0.1 stack.10
  2.6 0.1 stack.11
  2.7 0.1 stack.24
  2.8 0.1 convert_element_type.102
  2.9 0.8 copy.59
  3.7 0.1 reshape.786
  3.8 0.2 fusion
  4.0 0.9 fusion.14
  4.9 24.1 %all-to-all-start = ((f32[64,2,4]{2,1,0:T(2,128)}), f32[64,2,4]{2,1,0:T(2,128)S(1)}, u32[]{:S(2)}, u32[]{:S(2)}) async-start(f32[64,2,4]{2,1,0:T(2,128)} %bitcast.5), calls=%async_computation | async-start | bytes 131072 | tf_op jit(solution)/shard_map/all_to_all | solution.py:274
  29.1 1.5 fusion.42
  30.6 2.6 %collective-permute-start.2 = (s32[4,2,16,16]{3,2,1,0:T(8,128)}, s32[4,2,16,16]{3,2,1,0:T(8,128)}, u32[]{:S(2)}, u32[]{:S(2)}) collective-permute-start(s32[4,2,16,16]{3,2,1,0:T(8,128)} %get-tuple-element.42), channel_id=1, source_target_pairs={{0,1},{1,2},{2,3},{3,0},{4,5},{5,6},{6,7},{7,4},{8,9},{9,10},{10,1... | collective-permute-start | bytes 24584 | tf_op jit(solution)/shard_map/ppermute | solution.py:253
  33.2 3.3 %collective-permute-start.3 = (s32[4,2,16,16]{3,2,1,0:T(8,128)}, s32[4,2,16,16]{3,2,1,0:T(8,128)S(1)}, u32[]{:S(2)}, u32[]{:S(2)}) collective-permute-start(s32[4,2,16,16]{3,2,1,0:T(8,128)} %get-tuple-element.41), channel_id=1, source_target_pairs={{1,0},{2,1},{3,2},{0,3},{5,4},{6,5},{7,6},{4,7},{9,8},{10,9},{11,1... | collective-permute-start | bytes 24584 | tf_op jit(solution)/shard_map/ppermute | solution.py:254
  36.5 0.7 pad_add_fusion
  37.2 2.1 %collective-permute-start.4 = (s32[6,32]{1,0:T(8,128)S(1)}, s32[6,32]{1,0:T(8,128)S(1)}, u32[]{:S(2)}, u32[]{:S(2)}) collective-permute-start(s32[6,32]{1,0:T(8,128)S(1)} %pad_add_fusion), channel_id=1, source_target_pairs={{0,16},{16,32},{32,48},{48,64},{64,80},{80,96},{96,112},{112,128},... | collective-permute-start | bytes 2312 | tf_op jit(solution)/shard_map/ppermute | solution.py:44
  39.2 2.6 %fusion.40 = (f32[3,2,16,16,128]{4,3,2,1,0:T(8,128)}, f32[3,2,16,16,128]{4,3,2,1,0:T(8,128)}) fusion(f32[3,4,16,16,128]{4,3,2,1,0:T(8,128)} %param.16), kind=kLoop, calls=%fused_computation.113 | loop fusion | bytes 3145728 | tf_op jit(solution)/shard_map/slice | solution.py:251
  41.8 2.6 %collective-permute-start = (f32[3,2,16,16,128]{4,3,2,1,0:T(8,128)}, f32[3,2,16,16,128]{4,3,2,1,0:T(8,128)S(1)}, u32[]{:S(2)}, u32[]{:S(2)}) collective-permute-start(f32[3,2,16,16,128]{4,3,2,1,0:T(8,128)} %get-tuple-element.31), channel_id=1, source_target_pairs={{0,1},{1,2},{2,3},{3,0},{4,5},{5,6},{6,7},{7,4},{8,9},{9,10},{10,1... | collective-permute-start | bytes 2359304 | tf_op jit(solution)/shard_map/ppermute | solution.py:251
  44.4 4.4 %collective-permute-start.1 = (f32[3,2,16,16,128]{4,3,2,1,0:T(8,128)}, f32[3,2,16,16,128]{4,3,2,1,0:T(8,128)S(1)}, u32[]{:S(2)}, u32[]{:S(2)}) collective-permute-start(f32[3,2,16,16,128]{4,3,2,1,0:T(8,128)} %get-tuple-element.32), channel_id=1, source_target_pairs={{1,0},{2,1},{3,2},{0,3},{5,4},{6,5},{7,6},{4,7},{9,8},{10,9},{11,1... | collective-permute-start | bytes 2359304 | tf_op jit(solution)/shard_map/ppermute | solution.py:252
  48.8 0.7 compare_reduce_fusion
  49.6 7.2 %collective-permute-start.5 = (f32[4,6,6,32]{3,0,2,1:T(4,128)S(1)}, f32[4,6,6,32]{3,0,2,1:T(4,128)S(1)}, u32[]{:S(2)}, u32[]{:S(2)}) collective-permute-start(f32[4,6,6,32]{3,0,2,1:T(4,128)S(1)} %copy-done.2), channel_id=1, source_target_pairs={{0,16},{16,32},{32,48},{48,64},{64,80},{80,96},{96,112},{112,128},... | collective-permute-start | bytes 55304 | tf_op jit(solution)/shard_map/ppermute | solution.py:44
  56.8 0.6 slice_bitcast_fusion.1
  57.4 1.4 copy.67
  58.7 1.4 reshape.793
  60.1 1.4 fusion.1
  61.6 0.2 fusion.5
  61.8 0.6 slice_bitcast_fusion.5
  62.4 0.7 copy.85
  63.0 0.8 constant_dynamic-update-slice_fusion.2
  63.9 3.0 %multiply_add_fusion = (f32[8,16,16,128]{3,2,1,0:T(8,128)}, f32[8,16,16,128]{3,2,1,0:T(8,128)}) fusion(f32[128]{0:T(128)} %get-tuple-element.60, f32[8,16,16]{2,1,0:T(8,128)S(1)} %get-tuple-element.36, f32[128]{0:T(128)} %get-tuple-element.61, f32[8,16,16]{2,1,0:T(8,128)S(1)} %get-tuple-element.37, f32[128]{0:T(128)} %get-tuple-element.62, ...), kind=kLoop, calls=%fused_computation.7 | loop fusion | flops 2883584 | bytes 2131968 | tf_op jit(solution)/shard_map/add | solution.py:124
  66.9 16.9 %collective-permute-done.1 = f32[3,2,16,16,128]{4,3,2,1,0:T(8,128)S(1)} collective-permute-done((f32[3,2,16,16,128]{4,3,2,1,0:T(8,128)}, f32[3,2,16,16,128]{4,3,2,1,0:T(8,128)S(1)}, u32[]{:S(2)}, u32[]{:S(2)}) %collective-permute-start.1) | collective-permute-done | bytes 786464 | tf_op jit(solution)/shard_map/ppermute | solution.py:252
  83.8 1.9 %pad_maximum_fusion.cells_ref = f32[3,8,16,16,128]{4,3,2,1,0:T(8,128)} fusion(f32[3,2,16,16,128]{4,3,2,1,0:T(8,128)S(1)} %collective-permute-done.1, f32[3,4,16,16,128]{4,3,2,1,0:T(8,128)S(1)} %copy-done, f32[3,2,16,16,128]{4,3,2,1,0:T(8,128)S(1)} %collective-permute-done), kind=kLoop, calls=%fused_computation | loop fusion | flops 1572864 | bytes 6291456 | tf_op jit(solution)/shard_map/concatenate | solution.py:284
  85.8 0.0 copy-start.14
  85.8 0.0 copy-start.22
  85.8 7.2 %shard_map.121 = (f32[3,4,16,16,128]{4,3,2,1,0:T(8,128)}, f32[3,128]{1,0:T(4,128)}) custom-call(f32[3,8,16,16,128]{4,3,2,1,0:T(8,128)} %pad_maximum_fusion.cells_ref, f32[8,16,16,128]{3,2,1,0:T(8,128)} %get-tuple-element.34.lame_ref, f32[8,16,16,128]{3,2,1,0:T(8,128)} %get-tuple-element.33.shear_ref, f32[3,128]{1,0:T(4,128)} %bitcast.68), custom_call_target="tpu_custom_call" | custom-call | tf_op jit(solution)/shard_map/pallas_call | solution.py:226
  93.0 0.8 reshape.789
  93.8 0.7 slice_bitcast_fusion
  94.6 0.8 slice.161
  95.4 0.1 maximum_maximum_fusion
  95.5 0.7 copy.64
  96.2 18.9 %all-to-all-start.1 = ((f32[64,4,3]{1,2,0:T(4,128)}), f32[64,4,3]{1,2,0:T(4,128)S(1)}, u32[]{:S(2)}, u32[]{:S(2)}) async-start(f32[64,4,3]{1,2,0:T(4,128)} %copy.64), calls=%async_computation.1 | async-start | bytes 262144 | tf_op jit(solution)/shard_map/all_to_all | solution.py:288
  115.1 20.9 %all-to-all-done.1 = f32[64,4,3]{1,2,0:T(4,128)S(1)} async-done(((f32[64,4,3]{1,2,0:T(4,128)}), f32[64,4,3]{1,2,0:T(4,128)S(1)}, u32[]{:S(2)}, u32[]{:S(2)}) %all-to-all-start.1) | async-done | bytes 3104 | tf_op jit(solution)/shard_map/all_to_all | solution.py:288
  136.0 0.1 fusion.41
  136.2 0.1 reshape.791
  136.3 0.1 reshape.790
  136.5 0.2 fusion.11
  136.7 0.2 fusion.13
  136.9 0.1 slice_reduce_fusion.2
  137.0 0.1 squeeze.12
  137.1 0.1 squeeze.13
  137.2 0.1 squeeze.28
  137.3 0.1 squeeze.29
  137.4 0.1 squeeze.30
  137.5 0.1 squeeze.31
  137.7 0.1 fusion.7
  137.9 0.2 convolution_bitcast_fusion.1
  138.2 0.2 convolution_bitcast_fusion
  138.4 0.8 add_select_fusion
  139.2 0.1 scatter-add.4
  139.4 10.8 %psum.14 = f32[12,32]{1,0:T(8,128)S(1)} all-reduce(f32[12,32]{1,0:T(8,128)S(1)} %pad_maximum_fusion.3), channel_id=1, replica_groups=mesh['tile'=64,'thick'=4,'rve'=4] {'rve'}, use_global_device_ids=true, to_apply=%region_7.8 | all-reduce | flops 384 | bytes 3072 | tf_op jit(solution)/shard_map/psum | solution.py:300
  150.2 10.6 %psum.15 = f32[12,32]{1,0:T(8,128)S(1)} all-reduce(f32[12,32]{1,0:T(8,128)S(1)} %psum.14), channel_id=1, replica_groups=mesh['tile'=64,'thick'=4,'rve'=4] {'thick'}, use_global_device_ids=true, to_apply=%region_8.9 | all-reduce | flops 384 | bytes 3072 | tf_op jit(solution)/shard_map/psum | solution.py:300
  160.8 0.6 fusion.43
  (77 shorter events, 0.4 us)
Async XLA Ops:
  0.6 63.2 %copy-start.1 = (s32[4,4,16,16]{3,2,1,0:T(8,128)S(1)}, s32[4,4,16,16]{3,2,1,0:T(8,128)}, u32[]{:S(2)}) copy-start(s32[4,4,16,16]{3,2,1,0:T(8,128)} %param.15) | copy-start | bytes 49156
  0.6 48.9 %copy-start.2 = (f32[4,6,6,32]{3,0,2,1:T(4,128)S(1)}, f32[4,6,6,32]{3,0,2,1:T(4,128)}, u32[]{:S(2)}) copy-start(f32[4,6,6,32]{3,0,2,1:T(4,128)} %param.18) | copy-start | bytes 55300
  0.7 1.8 %copy-start.17 = (f32[2]{0:T(128)}, f32[2]{0:T(128)S(1)}, u32[]{:S(2)}) copy-start(f32[2]{0:T(128)S(1)} %multiply_add_fusion.7) | copy-start | bytes 28
  1.5 48.1 %copy-start.3 = (f32[2]{0:T(128)}, f32[2]{0:T(128)S(1)}, u32[]{:S(2)}) copy-start(f32[2]{0:T(128)S(1)} %get-tuple-element.29) | copy-start | bytes 28
  1.5 0.9 copy-start.7
  1.6 0.9 copy-start.9
  1.6 0.9 copy-start.11
  1.6 48.0 %copy-start.5 = (f32[2]{0:T(128)}, f32[2]{0:T(128)S(1)}, u32[]{:S(2)}) copy-start(f32[2]{0:T(128)S(1)} %get-tuple-element.65) | copy-start | bytes 28
  4.0 45.6 %copy-start.20 = (s32[64]{0:T(128)}, s32[64]{0:T(128)S(1)}, u32[]{:S(2)}) copy-start(s32[64]{0:T(128)S(1)} %convert_add_fusion.1) | copy-start | bytes 772
  4.9 56.6 %all-to-all-start = ((f32[64,2,4]{2,1,0:T(2,128)}), f32[64,2,4]{2,1,0:T(2,128)S(1)}, u32[]{:S(2)}, u32[]{:S(2)}) async-start(f32[64,2,4]{2,1,0:T(2,128)} %bitcast.5), calls=%async_computation | async-start | bytes 131072 | tf_op jit(solution)/shard_map/all_to_all | solution.py:274
  30.6 32.4 %collective-permute-start.2 = (s32[4,2,16,16]{3,2,1,0:T(8,128)}, s32[4,2,16,16]{3,2,1,0:T(8,128)}, u32[]{:S(2)}, u32[]{:S(2)}) collective-permute-start(s32[4,2,16,16]{3,2,1,0:T(8,128)} %get-tuple-element.42), channel_id=1, source_target_pairs={{0,1},{1,2},{2,3},{3,0},{4,5},{5,6},{6,7},{7,4},{8,9},{9,10},{10,1... | collective-permute-start | bytes 24584 | tf_op jit(solution)/shard_map/ppermute | solution.py:253
  33.2 30.7 %collective-permute-start.3 = (s32[4,2,16,16]{3,2,1,0:T(8,128)}, s32[4,2,16,16]{3,2,1,0:T(8,128)S(1)}, u32[]{:S(2)}, u32[]{:S(2)}) collective-permute-start(s32[4,2,16,16]{3,2,1,0:T(8,128)} %get-tuple-element.41), channel_id=1, source_target_pairs={{1,0},{2,1},{3,2},{0,3},{5,4},{6,5},{7,6},{4,7},{9,8},{10,9},{11,1... | collective-permute-start | bytes 24584 | tf_op jit(solution)/shard_map/ppermute | solution.py:254
  37.2 46.6 %copy-start = (f32[3,4,16,16,128]{4,3,2,1,0:T(8,128)S(1)}, f32[3,4,16,16,128]{4,3,2,1,0:T(8,128)}, u32[]{:S(2)}) copy-start(f32[3,4,16,16,128]{4,3,2,1,0:T(8,128)} %param.16) | copy-start | bytes 4718596
  37.2 12.4 %collective-permute-start.4 = (s32[6,32]{1,0:T(8,128)S(1)}, s32[6,32]{1,0:T(8,128)S(1)}, u32[]{:S(2)}, u32[]{:S(2)}) collective-permute-start(s32[6,32]{1,0:T(8,128)S(1)} %pad_add_fusion), channel_id=1, source_target_pairs={{0,16},{16,32},{32,48},{48,64},{64,80},{80,96},{96,112},{112,128},... | collective-permute-start | bytes 2312 | tf_op jit(solution)/shard_map/ppermute | solution.py:44
  41.8 25.0 %collective-permute-start = (f32[3,2,16,16,128]{4,3,2,1,0:T(8,128)}, f32[3,2,16,16,128]{4,3,2,1,0:T(8,128)S(1)}, u32[]{:S(2)}, u32[]{:S(2)}) collective-permute-start(f32[3,2,16,16,128]{4,3,2,1,0:T(8,128)} %get-tuple-element.31), channel_id=1, source_target_pairs={{0,1},{1,2},{2,3},{3,0},{4,5},{5,6},{6,7},{7,4},{8,9},{9,10},{10,1... | collective-permute-start | bytes 2359304 | tf_op jit(solution)/shard_map/ppermute | solution.py:251
  44.4 39.4 %collective-permute-start.1 = (f32[3,2,16,16,128]{4,3,2,1,0:T(8,128)}, f32[3,2,16,16,128]{4,3,2,1,0:T(8,128)S(1)}, u32[]{:S(2)}, u32[]{:S(2)}) collective-permute-start(f32[3,2,16,16,128]{4,3,2,1,0:T(8,128)} %get-tuple-element.32), channel_id=1, source_target_pairs={{1,0},{2,1},{3,2},{0,3},{5,4},{6,5},{7,6},{4,7},{9,8},{10,9},{11,1... | collective-permute-start | bytes 2359304 | tf_op jit(solution)/shard_map/ppermute | solution.py:252
  49.6 7.2 %copy-start.15 = (s32[6,32]{1,0:T(8,128)}, s32[6,32]{1,0:T(8,128)S(1)}, u32[]{:S(2)}) copy-start(s32[6,32]{1,0:T(8,128)S(1)} %collective-permute-done.4) | copy-start | bytes 2308
  49.6 88.6 %collective-permute-start.5 = (f32[4,6,6,32]{3,0,2,1:T(4,128)S(1)}, f32[4,6,6,32]{3,0,2,1:T(4,128)S(1)}, u32[]{:S(2)}, u32[]{:S(2)}) collective-permute-start(f32[4,6,6,32]{3,0,2,1:T(4,128)S(1)} %copy-done.2), channel_id=1, source_target_pairs={{0,16},{16,32},{32,48},{48,64},{64,80},{80,96},{96,112},{112,128},... | collective-permute-start | bytes 55304 | tf_op jit(solution)/shard_map/ppermute | solution.py:44
  85.7 29.4 %copy-start.23 = (s32[64]{0:T(128)S(1)}, s32[64]{0:T(128)}, u32[]{:S(2)}) copy-start(s32[64]{0:T(128)} %reshape.793) | copy-start | bytes 772
  85.7 29.4 %copy-start.24 = (f32[64]{0:T(128)S(1)}, f32[64]{0:T(128)}, u32[]{:S(2)}) copy-start(f32[64]{0:T(128)} %fusion.1) | copy-start | bytes 772
  85.7 29.4 %copy-start.16 = (s32[6,32]{1,0:T(8,128)S(1)}, s32[6,32]{1,0:T(8,128)}, u32[]{:S(2)}) copy-start(s32[6,32]{1,0:T(8,128)} %copy-done.15) | copy-start | bytes 2308
  85.7 50.8 %copy-start.21 = (s32[64]{0:T(128)S(1)}, s32[64]{0:T(128)}, u32[]{:S(2)}) copy-start(s32[64]{0:T(128)} %copy-done.20) | copy-start | bytes 772
  85.7 51.9 %copy-start.4 = (f32[2]{0:T(128)S(1)}, f32[2]{0:T(128)}, u32[]{:S(2)}) copy-start(f32[2]{0:T(128)} %copy-done.3) | copy-start | bytes 28
  85.7 51.9 %copy-start.6 = (f32[2]{0:T(128)S(1)}, f32[2]{0:T(128)}, u32[]{:S(2)}) copy-start(f32[2]{0:T(128)} %copy-done.5) | copy-start | bytes 28
  85.8 51.9 %copy-start.8 = (f32[2]{0:T(128)S(1)}, f32[2]{0:T(128)}, u32[]{:S(2)}) copy-start(f32[2]{0:T(128)} %copy-done.7) | copy-start | bytes 28
  85.8 51.9 %copy-start.10 = (f32[2]{0:T(128)S(1)}, f32[2]{0:T(128)}, u32[]{:S(2)}) copy-start(f32[2]{0:T(128)} %copy-done.9) | copy-start | bytes 28
  85.8 51.9 %copy-start.12 = (f32[2]{0:T(128)S(1)}, f32[2]{0:T(128)}, u32[]{:S(2)}) copy-start(f32[2]{0:T(128)} %copy-done.11) | copy-start | bytes 28
  85.8 51.9 %copy-start.18 = (f32[2]{0:T(128)S(1)}, f32[2]{0:T(128)}, u32[]{:S(2)}) copy-start(f32[2]{0:T(128)} %copy-done.17) | copy-start | bytes 28
  85.8 52.1 %copy-start.19 = (s32[4,32]{1,0:T(4,128)S(1)}, s32[4,32]{1,0:T(4,128)}, u32[]{:S(2)}) copy-start(s32[4,32]{1,0:T(4,128)} %param.17) | copy-start | bytes 1540
  85.8 75.0 %copy-start.13 = (f32[6,32]{1,0:T(8,128)S(1)}, f32[6,32]{1,0:T(8,128)}, u32[]{:S(2)}) copy-start(f32[6,32]{1,0:T(8,128)} %param.19) | copy-start | bytes 2308
  85.8 75.0 %copy-start.14 = (f32[6,32]{1,0:T(8,128)S(1)}, f32[6,32]{1,0:T(8,128)}, u32[]{:S(2)}) copy-start(f32[6,32]{1,0:T(8,128)} %param.20) | copy-start | bytes 2308
  85.8 75.0 %copy-start.22 = (f32[32]{0:T(128)S(1)}, f32[32]{0:T(128)}, u32[]{:S(2)}) copy-start(f32[32]{0:T(128)} %param.21) | copy-start | bytes 388
  96.2 39.8 %all-to-all-start.1 = ((f32[64,4,3]{1,2,0:T(4,128)}), f32[64,4,3]{1,2,0:T(4,128)S(1)}, u32[]{:S(2)}, u32[]{:S(2)}) async-start(f32[64,4,3]{1,2,0:T(4,128)} %copy.64), calls=%async_computation.1 | async-start | bytes 262144 | tf_op jit(solution)/shard_map/all_to_all | solution.py:288

commit v5 on v4

--- a/solution.py
+++ b/solution.py
@@ -196,8 +196,21 @@
     return (moved, (s11, s22, s12))
 
 
-def relax_kernel(cells_ref, lame_ref, shear_ref, macro_ref, out_ref, mean_ref):
-    cells = [cells_ref[i] for i in range(3)]
+def relax_kernel(low_ref, state_ref, high_ref, lame_ref, shear_ref, macro_ref, out_ref, mean_ref):
+    rows = state_ref.shape[2]
+    depth = ITERS
+
+    def halo_planes(ref, component):
+        return [
+            ref[pl.ds((component * depth + p) * rows, rows)][None] for p in range(depth)
+        ]
+
+    cells = [
+        jnp.concatenate(
+            halo_planes(low_ref, i) + [state_ref[i]] + halo_planes(high_ref, i), 0
+        )
+        for i in range(3)
+    ]
     lame_all = lame_ref[...]
     shear_all = shear_ref[...]
     macro = [macro_ref[k : k + 1, :].reshape(1, 1, 1, -1) for k in range(3)]
@@ -217,19 +230,28 @@
         mean_ref[k : k + 1, :] = jnp.sum(total, axis=0, keepdims=True) / float(RES**3)
 
 
-def relax_slab_kernel(displace, lame_field, shear_field, macro):
-    planes = displace.shape[1] - 2 * ITERS
+def relax_slab_kernel(low, state, high, lame_field, shear_field, macro):
     out_shape = (
-        jax.ShapeDtypeStruct((3, planes) + displace.shape[2:], jnp.float32),
-        jax.ShapeDtypeStruct((3, displace.shape[-1]), jnp.float32),
+        jax.ShapeDtypeStruct(state.shape, jnp.float32),
+        jax.ShapeDtypeStruct((3, state.shape[-1]), jnp.float32),
     )
     return pl.pallas_call(
         relax_kernel,
         out_shape=out_shape,
-        in_specs=[pl.BlockSpec(memory_space=pltpu.VMEM)] * 4,
+        in_specs=[pl.BlockSpec(memory_space=pltpu.VMEM)] * 6,
         out_specs=(pl.BlockSpec(memory_space=pltpu.VMEM), pl.BlockSpec(memory_space=pltpu.VMEM)),
         compiler_params=pltpu.CompilerParams(vmem_limit_bytes=60 * 1024 * 1024),
-    )(displace, lame_field, shear_field, macro)
+    )(low, state, high, lame_field, shear_field, macro)
+
+
+def halo_pack(cells, phase_planes, pairs):
+    lanes = cells.shape[-1]
+    rows = cells.shape[-2]
+    flat_cells = cells.reshape(-1, rows, lanes)
+    flat_phase = phase_planes.astype(jnp.float32).reshape(-1, rows, lanes)
+    moved = lax.ppermute(jnp.concatenate([flat_cells, flat_phase], 0), "rve", pairs)
+    phase_in = moved[flat_cells.shape[0] :].reshape(phase_planes.shape).astype(jnp.int32)
+    return (moved, phase_in)
 
 
 def shards(
@@ -248,13 +270,8 @@
     up = [(i, (i + 1) % slab_count) for i in range(slab_count)]
     down = [((i + 1) % slab_count, i) for i in range(slab_count)]
     planes = rve_state.shape[1]
-    below = lax.ppermute(rve_state[:, planes - depth :], "rve", up)
-    above = lax.ppermute(rve_state[:, :depth], "rve", down)
-    phase_below = lax.ppermute(phase[:, planes - depth :], "rve", up)
-    phase_above = lax.ppermute(phase[:, :depth], "rve", down)
-    route_rows = route.reshape(elements, per_group).T
-    prev_ints = from_behind(jnp.concatenate([route_rows, connect], 0), "tile", 1)
-    prev_bmat = from_behind(bmat, "tile", 1)
+    below, phase_below = halo_pack(rve_state[:, planes - depth :], phase[:, planes - depth :], up)
+    above, phase_above = halo_pack(rve_state[:, :depth], phase[:, :depth], down)
     layer = thick_index * per_group + jnp.arange(per_group, dtype=jnp.int32)
     heights = -1.0 + (2.0 * layer.astype(jnp.float32) + 1.0) / TP
     classes = lax.dynamic_slice_in_dim(ply_class, thick_index * per_group, per_group)
@@ -281,25 +298,16 @@
     )
     wide_phase = jnp.concatenate([phase_below, phase, phase_above], 1)
     lame_field, shear_field = moduli_planes(wide_phase, class_hot)
-    displace = jnp.concatenate([below, rve_state, above], 1)
-    displace, average = relax_slab_kernel(displace, lame_field, shear_field, macro)
-    own_chunks = average.T.reshape(tile_count, capacity, 3)
-    both_chunks = jnp.concatenate([own_chunks, jnp.roll(own_chunks, 1, axis=0)], 1)
-    returned = lax.all_to_all(both_chunks, "tile", split_axis=0, concat_axis=0, tiled=True)
-    own_returned = returned[:, :capacity].reshape(slots, 3)
-    prev_returned = returned[:, capacity:].reshape(slots, 3)
-    own_terms = tile_terms(choose, own_returned, cosine, sine, heights, elements, per_group)
-    prev_route = prev_ints[:per_group].T.reshape(row_count)
-    prev_connect = prev_ints[per_group:]
-    prev_choose = slot_choice(prev_route, tile_count, capacity, slots)
-    prev_terms = tile_terms(prev_choose, prev_returned, cosine, sine, heights, elements, per_group)
+    displace, average = relax_slab_kernel(below, rve_state, above, lame_field, shear_field, macro)
+    returned = lax.all_to_all(
+        average.T.reshape(tile_count, capacity, 3), "tile", split_axis=0, concat_axis=0, tiled=True
+    )
+    own_terms = tile_terms(choose, returned.reshape(slots, 3), cosine, sine, heights, elements, per_group)
+    resultants = lax.psum(lax.psum(own_terms, "rve"), "thick")
     node_count = velocity.shape[1]
-    own_nodes = node_forces(bmat, own_terms, connect, node_count)[:, :node_count]
-    ghost_nodes = node_forces(prev_bmat, prev_terms, prev_connect, node_count)[:, node_count:]
-    partial_internal = own_nodes.at[:, :GHOST].add(ghost_nodes)
-    totals = lax.psum(lax.psum(jnp.concatenate([own_terms, partial_internal], 0), "rve"), "thick")
-    resultants = totals[:6]
-    internal = totals[6:]
+    assembled = node_forces(bmat, resultants, connect, node_count)
+    incoming = from_behind(assembled[:, node_count:], "tile", 1)
+    internal = assembled[:, :node_count].at[:, :GHOST].add(incoming)
     new_velocity = velocity + time_step * (force_ext - internal) / mass[None, :]
     return (new_velocity, resultants, displace)
 

time: 162 us -> 137 us (0.85)
  the two profiles are of different devices: /device:TPU:8 before, /device:TPU:2 now
where the time goes in v5:
time: 137 us
  blocking collectives  56 us (41%)
  starting transfers between devices  34.6 us (25%)
  waiting for transfers between devices  25.7 us (19%)
  Pallas kernels  7.22 us (5%)
  other arithmetic  5.8 us (4%)
  local copies, waits for them, and re-layouts  4.65 us (3%)
  matrix products  1.51 us (1%)
    all_to_all x1, blocking collectives, shards(): lax.all_to_all(average.T.reshape(tile_count, capacity, 3), 'tile', split_...  34.8 us
    all_to_all x1, starting transfers between devices, shards(): lax.all_to_all(send.reshape(tile_count, capacity, 4), 'tile', split_axis=...  24.1 us
    psum x2, blocking collectives, shards(): resultants = lax.psum(lax.psum(own_terms, 'rve'), 'thick')  21.2 us
    all_to_all x1, waiting for transfers between devices, shards(): lax.all_to_all(send.reshape(tile_count, capacity, 4), 'tile', split_axis=...  12.2 us
    ppermute x2, starting transfers between devices, halo_pack(): lax.ppermute(jnp.concatenate([flat_cells, flat_phase], 0), 'rve', pairs)  8.53 us
    ppermute x1, waiting for transfers between devices, from_behind(): return lax.ppermute(value, axis, pairs)  8.37 us
    pallas_call x1, Pallas kernels, relax_slab_kernel(): pl.pallas_call(relax_kernel, out_shape=out_shape, in_specs=[pl.BlockSpec(...  7.22 us
    ppermute x2, waiting for transfers between devices, halo_pack(): lax.ppermute(jnp.concatenate([flat_cells, flat_phase], 0), 'rve', pairs)  5.09 us
  transfers between devices with their start and end apart: 4, of which 3 were waited for; matrix products, arithmetic and copies ran while one was open for 3% of the time, Pallas kernels for 0%

profile of v5, /device:TPU:2, one launch (start us, length us, event | category | flops | bytes accessed | tf_op | source)
XLA Modules:
  0.0 136.5 jit_solution(278237441964392882)
XLA Ops:
  0.6 0.0 copy-start.2
  0.6 1.6 %fusion.29 = (f32[3,2,16,16,128]{4,3,2,1,0:T(8,128)S(1)}, f32[3,2,16,16,128]{4,3,2,1,0:T(8,128)S(1)}) fusion(f32[3,4,16,16,128]{4,3,2,1,0:T(8,128)} %state_ref.1), kind=kLoop, calls=%fused_computation.84 | loop fusion | bytes 3145728 | tf_op jit(solution)/shard_map/slice | solution.py:274
  2.2 0.0 copy-done.2
  2.2 0.0 copy-start.10
  2.3 0.0 copy-start.5
  2.3 0.0 copy-start.8
  2.3 0.1 reshape.492
  2.4 0.1 pad_maximum_fusion
  2.4 3.5 %collective-permute-start = (f32[97,16,128]{2,1,0:T(8,128)S(1)}, f32[97,16,128]{2,1,0:T(8,128)S(1)}, u32[]{:S(2)}, u32[]{:S(2)}) collective-permute-start(f32[97,16,128]{2,1,0:T(8,128)S(1)} %pad_maximum_fusion), channel_id=1, source_target_pairs={{0,1},{1,2},{2,3},{3,0},{4,5},{5,6},{6,7},{7,4},{8,9},{9,10},{10,1... | collective-permute-start | bytes 2383880 | tf_op jit(solution)/shard_map/ppermute | solution.py:252
  6.0 0.0 copy-done.10
  6.0 0.1 fusion.27
  6.1 0.0 copy-done.5
  6.2 0.1 multiply_add_fusion.3
  6.3 0.1 stack.16
  6.4 0.1 stack.17
  6.5 0.1 stack.18
  6.6 0.1 convert_element_type.115
  6.7 0.0 copy-done.8
  6.7 0.1 copy.29
  6.8 0.1 reshape.495
  6.9 0.2 fusion
  7.1 0.9 fusion.10
  8.0 24.1 %all-to-all-start = ((f32[64,2,4]{2,1,0:T(2,128)}), f32[64,2,4]{2,1,0:T(2,128)S(1)}, u32[]{:S(2)}, u32[]{:S(2)}) async-start(f32[64,2,4]{2,1,0:T(2,128)} %bitcast.5), calls=%async_computation | async-start | bytes 131072 | tf_op jit(solution)/shard_map/all_to_all | solution.py:291
  32.2 0.1 reshape.494
  32.2 0.9 pad_maximum_fusion.1
  33.2 5.0 %collective-permute-start.1 = (f32[97,16,128]{2,1,0:T(8,128)}, f32[97,16,128]{2,1,0:T(8,128)S(1)}, u32[]{:S(2)}, u32[]{:S(2)}) collective-permute-start(f32[97,16,128]{2,1,0:T(8,128)} %pad_maximum_fusion.1), channel_id=1, source_target_pairs={{1,0},{2,1},{3,2},{0,3},{5,4},{6,5},{7,6},{4,7},{9,8},{10,9},{11,1... | collective-permute-start | bytes 2383880 | tf_op jit(solution)/shard_map/ppermute | solution.py:252
  38.2 12.2 %all-to-all-done = f32[64,2,4]{2,1,0:T(2,128)S(1)} async-done(((f32[64,2,4]{2,1,0:T(2,128)}), f32[64,2,4]{2,1,0:T(2,128)S(1)}, u32[]{:S(2)}, u32[]{:S(2)}) %all-to-all-start) | async-done | bytes 2080 | tf_op jit(solution)/shard_map/all_to_all | solution.py:291
  50.5 0.7 copy.44
  51.1 0.2 fusion.4
  51.3 0.0 collective-permute-done.low_ref
  51.3 0.0 copy-start
  51.3 0.1 convert_element_type.108
  51.5 5.1 %collective-permute-done.1.high_ref = f32[97,16,128]{2,1,0:T(8,128)S(1)} collective-permute-done((f32[97,16,128]{2,1,0:T(8,128)}, f32[97,16,128]{2,1,0:T(8,128)S(1)}, u32[]{:S(2)}, u32[]{:S(2)}) %collective-permute-start.1) | collective-permute-done | bytes 794656 | tf_op jit(solution)/shard_map/ppermute | solution.py:252
  56.6 0.1 convert_element_type.110
  56.7 2.2 %multiply_add_fusion = (f32[8,16,16,128]{3,2,1,0:T(8,128)}, f32[8,16,16,128]{3,2,1,0:T(8,128)}) fusion(f32[128]{0:T(128)S(1)} %get-tuple-element.45, f32[8,16,16]{2,1,0:T(8,128)S(1)} %get-tuple-element.31, f32[128]{0:T(128)S(1)} %get-tuple-element.46, f32[8,16,16]{2,1,0:T(8,128)S(1)} %get-tuple-element.32, f32[128]{0:T(128)S(1)} %get-tuple-element.47, ...), kind=kLoop, calls=%fused_computation.3 | loop fusion | flops 2883584 | bytes 2131968 | tf_op jit(solution)/shard_map/add | solution.py:124
  58.9 0.0 copy-done
  58.9 0.0 copy-done.1
  58.9 0.0 copy-start.11
  59.0 0.0 copy-start.6
  59.0 0.0 copy-start.7
  59.0 0.0 copy-start.9
  59.0 7.2 %shard_map.121 = (f32[3,4,16,16,128]{4,3,2,1,0:T(8,128)}, f32[3,128]{1,0:T(4,128)}) custom-call(f32[97,16,128]{2,1,0:T(8,128)} %copy-done, f32[3,4,16,16,128]{4,3,2,1,0:T(8,128)} %state_ref.1, f32[97,16,128]{2,1,0:T(8,128)} %copy-done.1, f32[8,16,16,128]{3,2,1,0:T(8,128)} %get-tuple-element.29.lame_ref, f32[8,16,16,128]{3,2,1,0:T(8,128)} %get-tuple-element.28.shear_ref, ...), custom_call_target="tpu_custom_call" | custom-call | tf_op jit(solution)/shard_map/pallas_call | solution.py:238
  66.2 0.8 copy.42
  67.0 34.8 %all_to_all.10 = f32[64,2,3]{2,1,0:T(2,128)S(1)} all-to-all(f32[64,2,3]{2,1,0:T(2,128)S(1)} %bitcast.48), channel_id=1, replica_groups=mesh['tile'=64,'thick'=4,'rve'=4] {'tile'}, dimensions={0} | all-to-all | bytes 3072 | tf_op jit(solution)/shard_map/all_to_all | solution.py:302
  101.8 0.2 fusion.8
  102.1 0.1 squeeze.6
  102.2 0.1 squeeze.7
  102.3 0.1 squeeze.8
  102.4 0.1 fusion.6
  102.6 12.5 %psum.14 = f32[6,32]{1,0:T(8,128)S(1)} all-reduce(f32[6,32]{1,0:T(8,128)S(1)} %pad_maximum_fusion.3), channel_id=1, replica_groups=mesh['tile'=64,'thick'=4,'rve'=4] {'rve'}, use_global_device_ids=true, to_apply=%region_3.0 | all-reduce | flops 192 | bytes 1536 | tf_op jit(solution)/shard_map/psum | solution.py:306
  115.1 8.6 %psum.15 = f32[6,32]{1,0:T(8,128)S(1)} all-reduce(f32[6,32]{1,0:T(8,128)S(1)} %psum.14), channel_id=1, replica_groups=mesh['tile'=64,'thick'=4,'rve'=4] {'thick'}, use_global_device_ids=true, to_apply=%region_4.0 | all-reduce | flops 192 | bytes 1536 | tf_op jit(solution)/shard_map/psum | solution.py:306
  123.7 0.0 copy-done.3
  123.8 0.0 copy-done.11
  123.8 0.2 convolution_bitcast_fusion
  124.0 0.1 slice.127
  124.1 1.9 %collective-permute-start.2 = (f32[6,8]{1,0:T(8,128)S(1)}, f32[6,8]{1,0:T(8,128)S(1)}, u32[]{:S(2)}, u32[]{:S(2)}) collective-permute-start(f32[6,8]{1,0:T(8,128)S(1)} %slice.127), channel_id=1, source_target_pairs={{0,16},{16,32},{32,48},{48,64},{64,80},{80,96},{96,112},{112,128},... | collective-permute-start | bytes 584 | tf_op jit(solution)/shard_map/ppermute | solution.py:44
  126.0 0.6 compare_reduce_fusion
  126.6 8.4 %collective-permute-done.2 = f32[6,8]{1,0:T(8,128)S(1)} collective-permute-done((f32[6,8]{1,0:T(8,128)S(1)}, f32[6,8]{1,0:T(8,128)S(1)}, u32[]{:S(2)}, u32[]{:S(2)}) %collective-permute-start.2) | collective-permute-done | bytes 224 | tf_op jit(solution)/shard_map/ppermute | solution.py:44
  135.0 0.6 add_select_fusion
  135.7 0.2 scatter-add.4
  135.9 0.0 copy-done.6
  135.9 0.0 copy-done.7
  135.9 0.0 copy-done.9
  135.9 0.6 divide_add_fusion
  (24 shorter events, 0.3 us)
Async XLA Ops:
  0.6 1.6 %copy-start.2 = (s32[4,4,16,16]{3,2,1,0:T(8,128)S(1)}, s32[4,4,16,16]{3,2,1,0:T(8,128)}, u32[]{:S(2)}) copy-start(s32[4,4,16,16]{3,2,1,0:T(8,128)} %param.15) | copy-start | bytes 49156
  2.2 3.7 %copy-start.10 = (s32[8]{0:T(128)S(1)}, s32[8]{0:T(128)}, u32[]{:S(2)}) copy-start(s32[8]{0:T(128)} %param.13) | copy-start | bytes 100
  2.3 3.9 %copy-start.5 = (f32[6,32]{1,0:T(8,128)S(1)}, f32[6,32]{1,0:T(8,128)}, u32[]{:S(2)}) copy-start(f32[6,32]{1,0:T(8,128)} %param.12) | copy-start | bytes 2308
  2.3 4.4 %copy-start.8 = (s32[1,32,2,1]{1,3,2,0:T(1,128)S(1)}, s32[1,32,2,1]{1,3,2,0:T(1,128)}, u32[]{:S(2)}) copy-start(s32[1,32,2,1]{1,3,2,0:T(1,128)} %param.14) | copy-start | bytes 772
  2.4 48.9 %collective-permute-start = (f32[97,16,128]{2,1,0:T(8,128)S(1)}, f32[97,16,128]{2,1,0:T(8,128)S(1)}, u32[]{:S(2)}, u32[]{:S(2)}) collective-permute-start(f32[97,16,128]{2,1,0:T(8,128)S(1)} %pad_maximum_fusion), channel_id=1, source_target_pairs={{0,1},{1,2},{2,3},{3,0},{4,5},{5,6},{6,7},{7,4},{8,9},{9,10},{10,1... | collective-permute-start | bytes 2383880 | tf_op jit(solution)/shard_map/ppermute | solution.py:252
  8.0 42.4 %all-to-all-start = ((f32[64,2,4]{2,1,0:T(2,128)}), f32[64,2,4]{2,1,0:T(2,128)S(1)}, u32[]{:S(2)}, u32[]{:S(2)}) async-start(f32[64,2,4]{2,1,0:T(2,128)} %bitcast.5), calls=%async_computation | async-start | bytes 131072 | tf_op jit(solution)/shard_map/all_to_all | solution.py:291
  33.2 23.4 %collective-permute-start.1 = (f32[97,16,128]{2,1,0:T(8,128)}, f32[97,16,128]{2,1,0:T(8,128)S(1)}, u32[]{:S(2)}, u32[]{:S(2)}) collective-permute-start(f32[97,16,128]{2,1,0:T(8,128)} %pad_maximum_fusion.1), channel_id=1, source_target_pairs={{1,0},{2,1},{3,2},{0,3},{5,4},{6,5},{7,6},{4,7},{9,8},{10,9},{11,1... | collective-permute-start | bytes 2383880 | tf_op jit(solution)/shard_map/ppermute | solution.py:252
  51.3 7.6 %copy-start = (f32[97,16,128]{2,1,0:T(8,128)}, f32[97,16,128]{2,1,0:T(8,128)S(1)}, u32[]{:S(2)}) copy-start(f32[97,16,128]{2,1,0:T(8,128)S(1)} %collective-permute-done.low_ref) | copy-start | bytes 2383876
  56.6 2.4 %copy-start.1 = (f32[97,16,128]{2,1,0:T(8,128)}, f32[97,16,128]{2,1,0:T(8,128)S(1)}, u32[]{:S(2)}) copy-start(f32[97,16,128]{2,1,0:T(8,128)S(1)} %collective-permute-done.1.high_ref) | copy-start | bytes 2383876
  58.9 64.8 %copy-start.3 = (f32[4,6,6,32]{3,0,2,1:T(4,128)S(1)}, f32[4,6,6,32]{3,0,2,1:T(4,128)}, u32[]{:S(2)}) copy-start(f32[4,6,6,32]{3,0,2,1:T(4,128)} %param.18) | copy-start | bytes 55300
  58.9 64.8 %copy-start.11 = (s32[4,32]{1,0:T(4,128)S(1)}, s32[4,32]{1,0:T(4,128)}, u32[]{:S(2)}) copy-start(s32[4,32]{1,0:T(4,128)} %param.17) | copy-start | bytes 1540
  59.0 76.9 %copy-start.6 = (f32[6,32]{1,0:T(8,128)S(1)}, f32[6,32]{1,0:T(8,128)}, u32[]{:S(2)}) copy-start(f32[6,32]{1,0:T(8,128)} %param.19) | copy-start | bytes 2308
  59.0 76.9 %copy-start.7 = (f32[6,32]{1,0:T(8,128)S(1)}, f32[6,32]{1,0:T(8,128)}, u32[]{:S(2)}) copy-start(f32[6,32]{1,0:T(8,128)} %param.20) | copy-start | bytes 2308
  59.0 76.9 %copy-start.9 = (f32[32]{0:T(128)S(1)}, f32[32]{0:T(128)}, u32[]{:S(2)}) copy-start(f32[32]{0:T(128)} %param.21) | copy-start | bytes 388
  123.7 12.8 %copy-start.4 = (f32[6,32]{1,0:T(8,128)}, f32[6,32]{1,0:T(8,128)S(1)}, u32[]{:S(2)}) copy-start(f32[6,32]{1,0:T(8,128)S(1)} %psum.15) | copy-start | bytes 2308
  124.1 11.0 %collective-permute-start.2 = (f32[6,8]{1,0:T(8,128)S(1)}, f32[6,8]{1,0:T(8,128)S(1)}, u32[]{:S(2)}, u32[]{:S(2)}) collective-permute-start(f32[6,8]{1,0:T(8,128)S(1)} %slice.127), channel_id=1, source_target_pairs={{0,16},{16,32},{32,48},{48,64},{64,80},{80,96},{96,112},{112,128},... | collective-permute-start | bytes 584 | tf_op jit(solution)/shard_map/ppermute | solution.py:44

commit v6 on v5

--- a/solution.py
+++ b/solution.py
@@ -244,14 +244,17 @@
     )(low, state, high, lame_field, shear_field, macro)
 
 
-def halo_pack(cells, phase_planes, pairs):
+def halo_pack(cells, phase_planes):
     lanes = cells.shape[-1]
     rows = cells.shape[-2]
     flat_cells = cells.reshape(-1, rows, lanes)
     flat_phase = phase_planes.astype(jnp.float32).reshape(-1, rows, lanes)
-    moved = lax.ppermute(jnp.concatenate([flat_cells, flat_phase], 0), "rve", pairs)
-    phase_in = moved[flat_cells.shape[0] :].reshape(phase_planes.shape).astype(jnp.int32)
-    return (moved, phase_in)
+    return jnp.concatenate([flat_cells, flat_phase], 0)
+
+
+def halo_unpack(moved, phase_planes):
+    count = moved.shape[0] - phase_planes.size // (moved.shape[1] * moved.shape[2])
+    return moved[count:].reshape(phase_planes.shape).astype(jnp.int32)
 
 
 def shards(
@@ -270,8 +273,13 @@
     up = [(i, (i + 1) % slab_count) for i in range(slab_count)]
     down = [((i + 1) % slab_count, i) for i in range(slab_count)]
     planes = rve_state.shape[1]
-    below, phase_below = halo_pack(rve_state[:, planes - depth :], phase[:, planes - depth :], up)
-    above, phase_above = halo_pack(rve_state[:, :depth], phase[:, :depth], down)
+    low_side = phase[:, planes - depth :]
+    high_side = phase[:, :depth]
+    pack_up = halo_pack(rve_state[:, planes - depth :], low_side)
+    pack_down = halo_pack(rve_state[:, :depth], high_side)
+    route_rows = route.reshape(elements, per_group).T
+    int_rows = jnp.concatenate([route_rows, connect], 0)
+    flat_bmat = bmat.reshape(-1, elements)
     layer = thick_index * per_group + jnp.arange(per_group, dtype=jnp.int32)
     heights = -1.0 + (2.0 * layer.astype(jnp.float32) + 1.0) / TP
     classes = lax.dynamic_slice_in_dim(ply_class, thick_index * per_group, per_group)
@@ -288,6 +296,11 @@
     ).T
     choose = slot_choice(route.reshape(row_count), tile_count, capacity, slots)
     send = jnp.dot(choose.T, payload, precision=highest)
+    send, pack_up, pack_down = lax.optimization_barrier((send, pack_up, pack_down))
+    below = lax.ppermute(pack_up, "rve", up)
+    above = lax.ppermute(pack_down, "rve", down)
+    phase_below = halo_unpack(below, low_side)
+    phase_above = halo_unpack(above, high_side)
     received = lax.all_to_all(
         send.reshape(tile_count, capacity, 4), "tile", split_axis=0, concat_axis=0, tiled=True
     ).reshape(slots, 4)
@@ -299,15 +312,27 @@
     wide_phase = jnp.concatenate([phase_below, phase, phase_above], 1)
     lame_field, shear_field = moduli_planes(wide_phase, class_hot)
     displace, average = relax_slab_kernel(below, rve_state, above, lame_field, shear_field, macro)
-    returned = lax.all_to_all(
-        average.T.reshape(tile_count, capacity, 3), "tile", split_axis=0, concat_axis=0, tiled=True
-    )
-    own_terms = tile_terms(choose, returned.reshape(slots, 3), cosine, sine, heights, elements, per_group)
-    resultants = lax.psum(lax.psum(own_terms, "rve"), "thick")
+    ghost_rows = jnp.concatenate([flat_bmat, int_rows.astype(jnp.float32)], 0)
+    prev_pack = from_behind(ghost_rows + 0.0 * average[0, 0], "tile", 1)
+    own_chunks = average.T.reshape(tile_count, capacity, 3)
+    both_chunks = jnp.concatenate([own_chunks, jnp.roll(own_chunks, 1, axis=0)], 1)
+    returned = lax.all_to_all(both_chunks, "tile", split_axis=0, concat_axis=0, tiled=True)
+    own_returned = returned[:, :capacity].reshape(slots, 3)
+    prev_returned = returned[:, capacity:].reshape(slots, 3)
+    own_terms = tile_terms(choose, own_returned, cosine, sine, heights, elements, per_group)
+    prev_bmat = prev_pack[: flat_bmat.shape[0]].reshape(bmat.shape)
+    prev_ints = prev_pack[flat_bmat.shape[0] :].astype(jnp.int32)
+    prev_route = prev_ints[:per_group].T.reshape(row_count)
+    prev_connect = prev_ints[per_group:]
+    prev_choose = slot_choice(prev_route, tile_count, capacity, slots)
+    prev_terms = tile_terms(prev_choose, prev_returned, cosine, sine, heights, elements, per_group)
     node_count = velocity.shape[1]
-    assembled = node_forces(bmat, resultants, connect, node_count)
-    incoming = from_behind(assembled[:, node_count:], "tile", 1)
-    internal = assembled[:, :node_count].at[:, :GHOST].add(incoming)
+    own_nodes = node_forces(bmat, own_terms, connect, node_count)[:, :node_count]
+    ghost_nodes = node_forces(prev_bmat, prev_terms, prev_connect, node_count)[:, node_count:]
+    partial_internal = own_nodes.at[:, :GHOST].add(ghost_nodes)
+    totals = lax.psum(lax.psum(jnp.concatenate([own_terms, partial_internal], 0), "rve"), "thick")
+    resultants = totals[:6]
+    internal = totals[6:]
     new_velocity = velocity + time_step * (force_ext - internal) / mass[None, :]
     return (new_velocity, resultants, displace)
 

time: 137 us -> 132 us (0.964)
  the two profiles are of different devices: /device:TPU:2 before, /device:TPU:8 now
where the time goes in v6:
time: 132 us
  starting transfers between devices  48.5 us (37%)
  waiting for transfers between devices  34.2 us (26%)
  blocking collectives  19.4 us (15%)
  local copies, waits for them, and re-layouts  13 us (10%)
  Pallas kernels  7.18 us (5%)
  other arithmetic  6 us (5%)
  between operations  2.06 us (2%)
    all_to_all x1, waiting for transfers between devices, shards(): lax.all_to_all(both_chunks, 'tile', split_axis=0, concat_axis=0, tiled=True)  18.3 us
    all_to_all x1, starting transfers between devices, shards(): lax.all_to_all(both_chunks, 'tile', split_axis=0, concat_axis=0, tiled=True)  16.6 us
    all_to_all x1, waiting for transfers between devices, shards(): lax.all_to_all(send.reshape(tile_count, capacity, 4), 'tile', split_axis=...  15.9 us
    ppermute x1, starting transfers between devices, shards(): above = lax.ppermute(pack_down, 'rve', down)  13.4 us
    all_to_all x1, starting transfers between devices, shards(): lax.all_to_all(send.reshape(tile_count, capacity, 4), 'tile', split_axis=...  13 us
    psum x1, blocking collectives, shards(): lax.psum(lax.psum(jnp.concatenate([own_terms, partial_internal], 0), 'rve...  10.6 us
    psum x1, blocking collectives, shards(): lax.psum(jnp.concatenate([own_terms, partial_internal], 0), 'rve')  8.85 us
    pallas_call x1, Pallas kernels, relax_slab_kernel(): pl.pallas_call(relax_kernel, out_shape=out_shape, in_specs=[pl.BlockSpec(...  7.18 us
  transfers between devices with their start and end apart: 5, of which 2 were waited for; matrix products, arithmetic and copies ran while one was open for 4% of the time, Pallas kernels for 0%

profile of v6, /device:TPU:8, one launch (start us, length us, event | category | flops | bytes accessed | tf_op | source)
XLA Modules:
  0.0 131.6 jit_solution(17107621129815990261)
XLA Ops:
  0.7 0.8 fusion.35
  1.5 0.8 fusion.40
  2.3 0.1 multiply_add_fusion.3
  2.4 0.1 stack.10
  2.5 0.1 stack.11
  2.6 0.1 stack.24
  2.7 0.1 convert_element_type.124
  2.9 0.8 copy.94
  3.6 0.1 reshape.810
  3.7 0.2 fusion
  4.0 1.5 %fusion.37 = (f32[3,2,16,16,128]{4,3,2,1,0:T(8,128)S(1)}, f32[3,2,16,16,128]{4,3,2,1,0:T(8,128)S(1)}) fusion(f32[3,4,16,16,128]{4,3,2,1,0:T(8,128)} %state_ref.1), kind=kLoop, calls=%fused_computation.118 | loop fusion | bytes 3145728 | tf_op jit(solution)/shard_map/slice | solution.py:279
  5.5 0.1 reshape.812
  5.6 0.1 reshape.814
  5.9 0.2 fusion.12
  6.1 3.5 %collective-permute-start = (f32[97,16,128]{2,1,0:T(8,128)S(1)}, f32[97,16,128]{2,1,0:T(8,128)S(1)}, u32[]{:S(2)}, u32[]{:S(2)}) collective-permute-start(f32[97,16,128]{2,1,0:T(8,128)S(1)} %pad_maximum_fusion), channel_id=1, source_target_pairs={{0,1},{1,2},{2,3},{3,0},{4,5},{5,6},{6,7},{7,4},{8,9},{9,10},{10,1... | collective-permute-start | bytes 2383880 | tf_op jit(solution)/shard_map/ppermute | solution.py:300
  9.6 13.4 %collective-permute-start.1 = (f32[97,16,128]{2,1,0:T(8,128)S(1)}, f32[97,16,128]{2,1,0:T(8,128)S(1)}, u32[]{:S(2)}, u32[]{:S(2)}) collective-permute-start(f32[97,16,128]{2,1,0:T(8,128)S(1)} %pad_maximum_fusion.1), channel_id=1, source_target_pairs={{1,0},{2,1},{3,2},{0,3},{5,4},{6,5},{7,6},{4,7},{9,8},{10,9},{11,1... | collective-permute-start | bytes 2383880 | tf_op jit(solution)/shard_map/ppermute | solution.py:301
  23.0 0.7 copy.95
  23.7 13.0 %all-to-all-start = ((f32[64,2,4]{2,1,0:T(2,128)}), f32[64,2,4]{2,1,0:T(2,128)S(1)}, u32[]{:S(2)}, u32[]{:S(2)}) async-start(f32[64,2,4]{2,1,0:T(2,128)} %bitcast.7), calls=%async_computation | async-start | bytes 131072 | tf_op jit(solution)/shard_map/all_to_all | solution.py:304
  36.9 0.6 reshape.820
  37.5 0.9 copy.103
  38.5 0.1 copy.104
  38.5 0.7 compare_reduce_fusion
  39.2 15.9 %all-to-all-done = f32[64,2,4]{2,1,0:T(2,128)S(1)} async-done(((f32[64,2,4]{2,1,0:T(2,128)}), f32[64,2,4]{2,1,0:T(2,128)S(1)}, u32[]{:S(2)}, u32[]{:S(2)}) %all-to-all-start) | async-done | bytes 2080 | tf_op jit(solution)/shard_map/all_to_all | solution.py:304
  55.1 0.7 copy.122
  55.7 0.2 fusion.5
  56.0 0.1 convert_element_type.128
  56.1 0.1 convert_element_type.130
  56.2 2.2 %multiply_add_fusion = (f32[8,16,16,128]{3,2,1,0:T(8,128)}, f32[8,16,16,128]{3,2,1,0:T(8,128)}) fusion(f32[128]{0:T(128)S(1)} %get-tuple-element.66, f32[8,16,16]{2,1,0:T(8,128)S(1)} %get-tuple-element.42, f32[128]{0:T(128)S(1)} %get-tuple-element.67, f32[8,16,16]{2,1,0:T(8,128)S(1)} %get-tuple-element.43, f32[128]{0:T(128)S(1)} %get-tuple-element.68, ...), kind=kLoop, calls=%fused_computation.6 | loop fusion | flops 2883584 | bytes 2131968 | tf_op jit(solution)/shard_map/add | solution.py:124
  58.5 7.2 %shard_map.121 = (f32[3,4,16,16,128]{4,3,2,1,0:T(8,128)}, f32[3,128]{1,0:T(4,128)}) custom-call(f32[97,16,128]{2,1,0:T(8,128)} %copy-done, f32[3,4,16,16,128]{4,3,2,1,0:T(8,128)} %state_ref.1, f32[97,16,128]{2,1,0:T(8,128)} %copy-done.1, f32[8,16,16,128]{3,2,1,0:T(8,128)} %get-tuple-element.40.lame_ref, f32[8,16,16,128]{3,2,1,0:T(8,128)} %get-tuple-element.39.shear_ref, ...), custom_call_target="tpu_custom_call" | custom-call | tf_op jit(solution)/shard_map/pallas_call | solution.py:238
  65.7 1.2 slice.186
  66.9 0.8 reshape.817
  67.7 0.8 slice_bitcast_fusion.1
  68.5 0.8 slice.178
  69.3 0.1 maximum_maximum_fusion
  69.5 0.7 copy.99
  70.2 16.6 %all-to-all-start.1 = ((f32[64,4,3]{1,2,0:T(4,128)}), f32[64,4,3]{1,2,0:T(4,128)S(1)}, u32[]{:S(2)}, u32[]{:S(2)}) async-start(f32[64,4,3]{1,2,0:T(4,128)} %copy.99), calls=%async_computation.1 | async-start | bytes 262144 | tf_op jit(solution)/shard_map/all_to_all | solution.py:319
  87.4 0.1 maximum_add_fusion
  87.5 2.0 %collective-permute-start.2 = (f32[150,32]{0,1:T(8,128)S(1)}, f32[150,32]{0,1:T(8,128)S(1)}, u32[]{:S(2)}, u32[]{:S(2)}) collective-permute-start(f32[150,32]{0,1:T(8,128)S(1)} %maximum_add_fusion), channel_id=1, source_target_pairs={{0,16},{16,32},{32,48},{48,64},{64,80},{80,96},{96,112},{112,128},... | collective-permute-start | bytes 57608 | tf_op jit(solution)/shard_map/ppermute | solution.py:44
  89.4 18.3 %all-to-all-done.1 = f32[64,4,3]{1,2,0:T(4,128)S(1)} async-done(((f32[64,4,3]{1,2,0:T(4,128)}), f32[64,4,3]{1,2,0:T(4,128)S(1)}, u32[]{:S(2)}, u32[]{:S(2)}) %all-to-all-start.1) | async-done | bytes 3104 | tf_op jit(solution)/shard_map/all_to_all | solution.py:319
  107.7 0.1 fusion.38
  107.8 0.1 reshape.818
  108.0 0.2 fusion.11
  108.2 0.1 reshape.819
  108.4 0.1 slice_convert_fusion.7
  108.5 0.1 slice.213
  108.5 0.1 reshape.822
  108.6 0.2 fusion.1
  108.8 0.2 fusion.13
  109.1 0.1 squeeze.12
  109.2 0.1 squeeze.13
  109.3 0.1 squeeze.14
  109.4 0.1 squeeze.30
  109.5 0.1 squeeze.31
  109.6 0.1 squeeze.32
  109.8 0.1 fusion.7
  110.0 0.1 copy.105
  110.1 0.1 copy.106
  110.2 0.2 convolution_bitcast_fusion.1
  110.5 0.2 convolution_bitcast_fusion
  110.7 0.7 add_select_fusion
  111.4 0.1 scatter-add.4
  111.5 8.8 %psum.14 = f32[12,32]{1,0:T(8,128)S(1)} all-reduce(f32[12,32]{1,0:T(8,128)S(1)} %pad_maximum_fusion.4), channel_id=1, replica_groups=mesh['tile'=64,'thick'=4,'rve'=4] {'rve'}, use_global_device_ids=true, to_apply=%region_7.8 | all-reduce | flops 384 | bytes 3072 | tf_op jit(solution)/shard_map/psum | solution.py:333
  120.4 10.6 %psum.15 = f32[12,32]{1,0:T(8,128)S(1)} all-reduce(f32[12,32]{1,0:T(8,128)S(1)} %psum.14), channel_id=1, replica_groups=mesh['tile'=64,'thick'=4,'rve'=4] {'thick'}, use_global_device_ids=true, to_apply=%region_8.9 | all-reduce | flops 384 | bytes 3072 | tf_op jit(solution)/shard_map/psum | solution.py:333
  131.0 0.6 fusion.39
  (82 shorter events, 0.7 us)
Async XLA Ops:
  0.6 1.7 %copy-start.15 = (f32[2]{0:T(128)}, f32[2]{0:T(128)S(1)}, u32[]{:S(2)}) copy-start(f32[2]{0:T(128)S(1)} %multiply_add_fusion.7) | copy-start | bytes 28
  1.5 2.4 %copy-start.4 = (f32[2]{0:T(128)}, f32[2]{0:T(128)S(1)}, u32[]{:S(2)}) copy-start(f32[2]{0:T(128)S(1)} %get-tuple-element.71) | copy-start | bytes 28
  1.5 2.4 %copy-start.6 = (f32[2]{0:T(128)}, f32[2]{0:T(128)S(1)}, u32[]{:S(2)}) copy-start(f32[2]{0:T(128)S(1)} %get-tuple-element.73) | copy-start | bytes 28
  1.5 2.4 %copy-start.8 = (f32[2]{0:T(128)}, f32[2]{0:T(128)S(1)}, u32[]{:S(2)}) copy-start(f32[2]{0:T(128)S(1)} %get-tuple-element.74) | copy-start | bytes 28
  1.5 2.4 %copy-start.10 = (f32[2]{0:T(128)}, f32[2]{0:T(128)S(1)}, u32[]{:S(2)}) copy-start(f32[2]{0:T(128)S(1)} %get-tuple-element.75) | copy-start | bytes 28
  3.9 1.9 %copy-start.20 = (s32[64]{0:T(128)}, s32[64]{0:T(128)S(1)}, u32[]{:S(2)}) copy-start(s32[64]{0:T(128)S(1)} %convert_add_fusion.1) | copy-start | bytes 772
  3.9 1.6 %copy-start.2 = (s32[4,4,16,16]{3,2,1,0:T(8,128)S(1)}, s32[4,4,16,16]{3,2,1,0:T(8,128)}, u32[]{:S(2)}) copy-start(s32[4,4,16,16]{3,2,1,0:T(8,128)} %param.15) | copy-start | bytes 49156
  5.7 31.1 %copy-start.14 = (s32[1,32,2,1]{1,3,2,0:T(1,128)S(1)}, s32[1,32,2,1]{1,3,2,0:T(1,128)}, u32[]{:S(2)}) copy-start(s32[1,32,2,1]{1,3,2,0:T(1,128)} %param.14) | copy-start | bytes 772
  5.7 31.1 %copy-start.17 = (s32[4,32]{1,0:T(4,128)S(1)}, s32[4,32]{1,0:T(4,128)}, u32[]{:S(2)}) copy-start(s32[4,32]{1,0:T(4,128)} %param.17) | copy-start | bytes 1540
  5.7 31.1 %copy-start.3 = (f32[4,6,6,32]{3,0,2,1:T(4,128)S(1)}, f32[4,6,6,32]{3,0,2,1:T(4,128)}, u32[]{:S(2)}) copy-start(f32[4,6,6,32]{3,0,2,1:T(4,128)} %param.18) | copy-start | bytes 55300
  6.1 49.9 %collective-permute-start = (f32[97,16,128]{2,1,0:T(8,128)S(1)}, f32[97,16,128]{2,1,0:T(8,128)S(1)}, u32[]{:S(2)}, u32[]{:S(2)}) collective-permute-start(f32[97,16,128]{2,1,0:T(8,128)S(1)} %pad_maximum_fusion), channel_id=1, source_target_pairs={{0,1},{1,2},{2,3},{3,0},{4,5},{5,6},{6,7},{7,4},{8,9},{9,10},{10,1... | collective-permute-start | bytes 2383880 | tf_op jit(solution)/shard_map/ppermute | solution.py:300
  9.6 46.5 %collective-permute-start.1 = (f32[97,16,128]{2,1,0:T(8,128)S(1)}, f32[97,16,128]{2,1,0:T(8,128)S(1)}, u32[]{:S(2)}, u32[]{:S(2)}) collective-permute-start(f32[97,16,128]{2,1,0:T(8,128)S(1)} %pad_maximum_fusion.1), channel_id=1, source_target_pairs={{1,0},{2,1},{3,2},{0,3},{5,4},{6,5},{7,6},{4,7},{9,8},{10,9},{11,1... | collective-permute-start | bytes 2383880 | tf_op jit(solution)/shard_map/ppermute | solution.py:301
  23.7 31.3 %all-to-all-start = ((f32[64,2,4]{2,1,0:T(2,128)}), f32[64,2,4]{2,1,0:T(2,128)S(1)}, u32[]{:S(2)}, u32[]{:S(2)}) async-start(f32[64,2,4]{2,1,0:T(2,128)} %bitcast.7), calls=%async_computation | async-start | bytes 131072 | tf_op jit(solution)/shard_map/all_to_all | solution.py:304
  55.9 2.5 %copy-start = (f32[97,16,128]{2,1,0:T(8,128)}, f32[97,16,128]{2,1,0:T(8,128)S(1)}, u32[]{:S(2)}) copy-start(f32[97,16,128]{2,1,0:T(8,128)S(1)} %collective-permute-done.low_ref) | copy-start | bytes 2383876
  56.1 2.4 %copy-start.1 = (f32[97,16,128]{2,1,0:T(8,128)}, f32[97,16,128]{2,1,0:T(8,128)S(1)}, u32[]{:S(2)}) copy-start(f32[97,16,128]{2,1,0:T(8,128)S(1)} %collective-permute-done.1.high_ref) | copy-start | bytes 2383876
  65.7 42.3 %copy-start.21 = (s32[64]{0:T(128)S(1)}, s32[64]{0:T(128)}, u32[]{:S(2)}) copy-start(s32[64]{0:T(128)} %copy-done.20) | copy-start | bytes 772
  65.7 44.0 %copy-start.5 = (f32[2]{0:T(128)S(1)}, f32[2]{0:T(128)}, u32[]{:S(2)}) copy-start(f32[2]{0:T(128)} %copy-done.4) | copy-start | bytes 28
  65.7 44.0 %copy-start.7 = (f32[2]{0:T(128)S(1)}, f32[2]{0:T(128)}, u32[]{:S(2)}) copy-start(f32[2]{0:T(128)} %copy-done.6) | copy-start | bytes 28
  65.7 44.1 %copy-start.9 = (f32[2]{0:T(128)S(1)}, f32[2]{0:T(128)}, u32[]{:S(2)}) copy-start(f32[2]{0:T(128)} %copy-done.8) | copy-start | bytes 28
  65.7 44.1 %copy-start.11 = (f32[2]{0:T(128)S(1)}, f32[2]{0:T(128)}, u32[]{:S(2)}) copy-start(f32[2]{0:T(128)} %copy-done.10) | copy-start | bytes 28
  65.7 44.1 %copy-start.16 = (f32[2]{0:T(128)S(1)}, f32[2]{0:T(128)}, u32[]{:S(2)}) copy-start(f32[2]{0:T(128)} %copy-done.15) | copy-start | bytes 28
  69.3 40.9 %copy-start.18 = (s32[4,32]{1,0:T(4,128)S(1)}, s32[4,32]{1,0:T(4,128)}, u32[]{:S(2)}) copy-start(s32[4,32]{1,0:T(4,128)} %param.17) | copy-start | bytes 1540
  69.4 61.6 %copy-start.12 = (f32[6,32]{1,0:T(8,128)S(1)}, f32[6,32]{1,0:T(8,128)}, u32[]{:S(2)}) copy-start(f32[6,32]{1,0:T(8,128)} %param.19) | copy-start | bytes 2308
  69.4 61.6 %copy-start.13 = (f32[6,32]{1,0:T(8,128)S(1)}, f32[6,32]{1,0:T(8,128)}, u32[]{:S(2)}) copy-start(f32[6,32]{1,0:T(8,128)} %param.20) | copy-start | bytes 2308
  69.5 61.6 %copy-start.19 = (f32[32]{0:T(128)S(1)}, f32[32]{0:T(128)}, u32[]{:S(2)}) copy-start(f32[32]{0:T(128)} %param.21) | copy-start | bytes 388
  70.2 37.5 %all-to-all-start.1 = ((f32[64,4,3]{1,2,0:T(4,128)}), f32[64,4,3]{1,2,0:T(4,128)S(1)}, u32[]{:S(2)}, u32[]{:S(2)}) async-start(f32[64,4,3]{1,2,0:T(4,128)} %copy.99), calls=%async_computation.1 | async-start | bytes 262144 | tf_op jit(solution)/shard_map/all_to_all | solution.py:319
  87.5 20.9 %collective-permute-start.2 = (f32[150,32]{0,1:T(8,128)S(1)}, f32[150,32]{0,1:T(8,128)S(1)}, u32[]{:S(2)}, u32[]{:S(2)}) collective-permute-start(f32[150,32]{0,1:T(8,128)S(1)} %maximum_add_fusion), channel_id=1, source_target_pairs={{0,16},{16,32},{32,48},{48,64},{64,80},{80,96},{96,112},{112,128},... | collective-permute-start | bytes 57608 | tf_op jit(solution)/shard_map/ppermute | solution.py:44

commit v7 on v6

--- a/solution.py
+++ b/solution.py
@@ -227,13 +227,15 @@
         out_ref[i] = cells[i]
     for k in range(3):
         total = jnp.sum(stress[k][1:], axis=(0, 1))
-        mean_ref[k : k + 1, :] = jnp.sum(total, axis=0, keepdims=True) / float(RES**3)
+        mean_row = jnp.sum(total, axis=0, keepdims=True) / float(RES**3)
+        mean_ref[k : k + 1, :] = mean_row
+        mean_ref[3 + k : 4 + k, :] = pltpu.roll(mean_row, 2, 1)
 
 
 def relax_slab_kernel(low, state, high, lame_field, shear_field, macro):
     out_shape = (
         jax.ShapeDtypeStruct(state.shape, jnp.float32),
-        jax.ShapeDtypeStruct((3, state.shape[-1]), jnp.float32),
+        jax.ShapeDtypeStruct((6, state.shape[-1]), jnp.float32),
     )
     return pl.pallas_call(
         relax_kernel,
@@ -313,9 +315,13 @@
     lame_field, shear_field = moduli_planes(wide_phase, class_hot)
     displace, average = relax_slab_kernel(below, rve_state, above, lame_field, shear_field, macro)
     ghost_rows = jnp.concatenate([flat_bmat, int_rows.astype(jnp.float32)], 0)
-    prev_pack = from_behind(ghost_rows + 0.0 * average[0, 0], "tile", 1)
-    own_chunks = average.T.reshape(tile_count, capacity, 3)
-    both_chunks = jnp.concatenate([own_chunks, jnp.roll(own_chunks, 1, axis=0)], 1)
+    ghost_rows, average = lax.optimization_barrier((ghost_rows, average))
+    prev_pack = from_behind(ghost_rows, "tile", 1)
+    both_chunks = (
+        average.reshape(2, 3, tile_count, capacity)
+        .transpose(2, 0, 3, 1)
+        .reshape(tile_count, 2 * capacity, 3)
+    )
     returned = lax.all_to_all(both_chunks, "tile", split_axis=0, concat_axis=0, tiled=True)
     own_returned = returned[:, :capacity].reshape(slots, 3)
     prev_returned = returned[:, capacity:].reshape(slots, 3)

time: 132 us -> 132 us (level)
  local copies, waits for them, and re-layouts: 13 us -> 10.4 us
  Pallas kernels: 7.18 us -> 9.5 us
    slice x4 -> x0, local copies, waits for them, and re-layouts: 2.77 us -> none  [the longest x3 1.57 us: shards(): jnp.roll(own_chunks, 1, axis=0)]
    pallas_call x1, Pallas kernels: 7.18 us -> 9.5 us  [relax_slab_kernel(): pl.pallas_call(relax_kernel, out_shape=out_shape, in_specs=[pl.BlockSpec(...]
where the time goes in v7:
time: 132 us; the launch traced here: 131 us
  starting transfers between devices  48.5 us (37%)
  waiting for transfers between devices  34.1 us (26%)
  blocking collectives  19.5 us (15%)
  local copies, waits for them, and re-layouts  10.4 us (8%)
  Pallas kernels  9.5 us (7%)
  other arithmetic  6.67 us (5%)
    all_to_all x1, waiting for transfers between devices, shards(): lax.all_to_all(both_chunks, 'tile', split_axis=0, concat_axis=0, tiled=True)  18.4 us
    all_to_all x1, starting transfers between devices, shards(): lax.all_to_all(both_chunks, 'tile', split_axis=0, concat_axis=0, tiled=True)  16.6 us
    all_to_all x1, waiting for transfers between devices, shards(): lax.all_to_all(send.reshape(tile_count, capacity, 4), 'tile', split_axis=...  15.8 us
    ppermute x1, starting transfers between devices, shards(): above = lax.ppermute(pack_down, 'rve', down)  13.4 us
    all_to_all x1, starting transfers between devices, shards(): lax.all_to_all(send.reshape(tile_count, capacity, 4), 'tile', split_axis=...  13 us
    psum x1, blocking collectives, shards(): lax.psum(lax.psum(jnp.concatenate([own_terms, partial_internal], 0), 'rve...  10.6 us
    pallas_call x1, Pallas kernels, relax_slab_kernel(): pl.pallas_call(relax_kernel, out_shape=out_shape, in_specs=[pl.BlockSpec(...  9.5 us
    psum x1, blocking collectives, shards(): lax.psum(jnp.concatenate([own_terms, partial_internal], 0), 'rve')  8.87 us
  transfers between devices with their start and end apart: 5, of which 2 were waited for; matrix products, arithmetic and copies ran while one was open for 4% of the time, Pallas kernels for 0%

profile of v7, /device:TPU:8, one launch (start us, length us, event | category | flops | bytes accessed | tf_op | source)
XLA Modules:
  0.0 131.3 jit_solution(6468763243837474569)
XLA Ops:
  0.7 0.8 fusion.35
  1.5 0.8 fusion.40
  2.3 0.1 multiply_add_fusion.3
  2.4 0.1 stack.10
  2.5 0.1 stack.11
  2.6 0.1 stack.24
  2.7 0.1 convert_element_type.125
  2.8 0.8 copy.74
  3.6 0.1 reshape.811
  3.7 0.2 fusion
  3.9 1.5 %fusion.37 = (f32[3,2,16,16,128]{4,3,2,1,0:T(8,128)S(1)}, f32[3,2,16,16,128]{4,3,2,1,0:T(8,128)S(1)}) fusion(f32[3,4,16,16,128]{4,3,2,1,0:T(8,128)} %state_ref.1), kind=kLoop, calls=%fused_computation.116 | loop fusion | bytes 3145728 | tf_op jit(solution)/shard_map/slice | solution.py:281
  5.5 0.1 reshape.813
  5.6 0.1 reshape.815
  5.7 0.1 pad_maximum_fusion
  5.8 0.2 fusion.12
  6.0 3.5 %collective-permute-start = (f32[97,16,128]{2,1,0:T(8,128)S(1)}, f32[97,16,128]{2,1,0:T(8,128)S(1)}, u32[]{:S(2)}, u32[]{:S(2)}) collective-permute-start(f32[97,16,128]{2,1,0:T(8,128)S(1)} %pad_maximum_fusion), channel_id=1, source_target_pairs={{0,1},{1,2},{2,3},{3,0},{4,5},{5,6},{6,7},{7,4},{8,9},{9,10},{10,1... | collective-permute-start | bytes 2383880 | tf_op jit(solution)/shard_map/ppermute | solution.py:302
  9.5 13.4 %collective-permute-start.1 = (f32[97,16,128]{2,1,0:T(8,128)S(1)}, f32[97,16,128]{2,1,0:T(8,128)S(1)}, u32[]{:S(2)}, u32[]{:S(2)}) collective-permute-start(f32[97,16,128]{2,1,0:T(8,128)S(1)} %pad_maximum_fusion.1), channel_id=1, source_target_pairs={{1,0},{2,1},{3,2},{0,3},{5,4},{6,5},{7,6},{4,7},{9,8},{10,9},{11,1... | collective-permute-start | bytes 2383880 | tf_op jit(solution)/shard_map/ppermute | solution.py:303
  23.0 0.7 copy.75
  23.7 13.0 %all-to-all-start = ((f32[64,2,4]{2,1,0:T(2,128)}), f32[64,2,4]{2,1,0:T(2,128)S(1)}, u32[]{:S(2)}, u32[]{:S(2)}) async-start(f32[64,2,4]{2,1,0:T(2,128)} %bitcast.9), calls=%async_computation | async-start | bytes 131072 | tf_op jit(solution)/shard_map/all_to_all | solution.py:306
  36.8 0.6 reshape.809
  37.4 0.9 copy.72
  38.4 0.7 add_convert_fusion
  39.1 0.1 copy.73
  39.2 0.1 pad_maximum_fusion.4
  39.3 15.8 %all-to-all-done = f32[64,2,4]{2,1,0:T(2,128)S(1)} async-done(((f32[64,2,4]{2,1,0:T(2,128)}), f32[64,2,4]{2,1,0:T(2,128)S(1)}, u32[]{:S(2)}, u32[]{:S(2)}) %all-to-all-start) | async-done | bytes 2080 | tf_op jit(solution)/shard_map/all_to_all | solution.py:306
  55.0 0.7 copy.96
  55.7 0.2 fusion.5
  55.9 0.1 convert_element_type.129
  56.1 0.1 convert_element_type.131
  56.2 2.2 %multiply_add_fusion = (f32[8,16,16,128]{3,2,1,0:T(8,128)}, f32[8,16,16,128]{3,2,1,0:T(8,128)}) fusion(f32[128]{0:T(128)S(1)} %get-tuple-element.70, f32[8,16,16]{2,1,0:T(8,128)S(1)} %get-tuple-element.46, f32[128]{0:T(128)S(1)} %get-tuple-element.71, f32[8,16,16]{2,1,0:T(8,128)S(1)} %get-tuple-element.47, f32[128]{0:T(128)S(1)} %get-tuple-element.72, ...), kind=kLoop, calls=%fused_computation.6 | loop fusion | flops 2883584 | bytes 2131968 | tf_op jit(solution)/shard_map/add | solution.py:124
  58.4 9.5 %shard_map.121 = (f32[3,4,16,16,128]{4,3,2,1,0:T(8,128)}, f32[6,128]{1,0:T(8,128)}) custom-call(f32[97,16,128]{2,1,0:T(8,128)} %copy-done, f32[3,4,16,16,128]{4,3,2,1,0:T(8,128)} %state_ref.1, f32[97,16,128]{2,1,0:T(8,128)} %copy-done.1, f32[8,16,16,128]{3,2,1,0:T(8,128)} %get-tuple-element.44.lame_ref, f32[8,16,16,128]{3,2,1,0:T(8,128)} %get-tuple-element.43.shear_ref, ...), custom_call_target="tpu_custom_call" | custom-call | tf_op jit(solution)/shard_map/pallas_call | solution.py:240
  68.0 0.9 reshape.818
  68.9 0.1 copy.77
  69.0 0.8 copy.78
  69.8 16.6 %all-to-all-start.1 = ((f32[64,4,3]{1,2,0:T(4,128)}), f32[64,4,3]{1,2,0:T(4,128)S(1)}, u32[]{:S(2)}, u32[]{:S(2)}) async-start(f32[64,4,3]{1,2,0:T(4,128)} %copy.78), calls=%async_computation.1 | async-start | bytes 262144 | tf_op jit(solution)/shard_map/all_to_all | solution.py:325
  86.3 0.6 compare_reduce_fusion
  87.0 2.0 %collective-permute-start.2 = (f32[150,32]{0,1:T(8,128)S(1)}, f32[150,32]{0,1:T(8,128)S(1)}, u32[]{:S(2)}, u32[]{:S(2)}) collective-permute-start(f32[150,32]{0,1:T(8,128)S(1)} %pad_maximum_fusion.4), channel_id=1, source_target_pairs={{0,16},{16,32},{32,48},{48,64},{64,80},{80,96},{96,112},{112,128},... | collective-permute-start | bytes 57608 | tf_op jit(solution)/shard_map/ppermute | solution.py:44
  88.9 18.4 %all-to-all-done.1 = f32[64,4,3]{1,2,0:T(4,128)S(1)} async-done(((f32[64,4,3]{1,2,0:T(4,128)}), f32[64,4,3]{1,2,0:T(4,128)S(1)}, u32[]{:S(2)}, u32[]{:S(2)}) %all-to-all-start.1) | async-done | bytes 3104 | tf_op jit(solution)/shard_map/all_to_all | solution.py:325
  107.3 0.1 fusion.38
  107.4 0.1 reshape.820
  107.6 0.2 fusion.11
  107.8 0.1 reshape.821
  108.0 0.1 slice_convert_fusion.7
  108.0 0.1 slice.191
  108.1 0.1 reshape.822
  108.2 0.2 fusion.1
  108.4 0.2 fusion.13
  108.6 0.1 slice_reduce_fusion.2
  108.6 0.1 squeeze.12
  108.7 0.1 squeeze.13
  108.9 0.1 squeeze.28
  109.0 0.1 squeeze.29
  109.1 0.1 squeeze.30
  109.2 0.1 squeeze.31
  109.4 0.1 fusion.7
  109.5 0.1 copy.81
  109.6 0.1 copy.82
  109.8 0.2 convolution_bitcast_fusion.1
  110.1 0.2 convolution_bitcast_fusion
  110.3 0.7 add_select_fusion
  111.0 0.1 scatter-add.4
  111.2 8.9 %psum.14 = f32[12,32]{1,0:T(8,128)S(1)} all-reduce(f32[12,32]{1,0:T(8,128)S(1)} %pad_maximum_fusion.5), channel_id=1, replica_groups=mesh['tile'=64,'thick'=4,'rve'=4] {'rve'}, use_global_device_ids=true, to_apply=%region_7.0 | all-reduce | flops 384 | bytes 3072 | tf_op jit(solution)/shard_map/psum | solution.py:339
  120.0 10.6 %psum.15 = f32[12,32]{1,0:T(8,128)S(1)} all-reduce(f32[12,32]{1,0:T(8,128)S(1)} %psum.14), channel_id=1, replica_groups=mesh['tile'=64,'thick'=4,'rve'=4] {'thick'}, use_global_device_ids=true, to_apply=%region_8.0 | all-reduce | flops 384 | bytes 3072 | tf_op jit(solution)/shard_map/psum | solution.py:339
  130.7 0.6 fusion.39
  (70 shorter events, 0.5 us)
Async XLA Ops:
  0.6 1.7 %copy-start.12 = (f32[2]{0:T(128)}, f32[2]{0:T(128)S(1)}, u32[]{:S(2)}) copy-start(f32[2]{0:T(128)S(1)} %multiply_add_fusion.7) | copy-start | bytes 28
  1.5 2.4 %copy-start.8 = (f32[2]{0:T(128)}, f32[2]{0:T(128)S(1)}, u32[]{:S(2)}) copy-start(f32[2]{0:T(128)S(1)} %get-tuple-element.79) | copy-start | bytes 28
  1.5 4.0 %copy-start.4 = (f32[2]{0:T(128)}, f32[2]{0:T(128)S(1)}, u32[]{:S(2)}) copy-start(f32[2]{0:T(128)S(1)} %get-tuple-element.77) | copy-start | bytes 28
  1.5 4.0 %copy-start.6 = (f32[2]{0:T(128)}, f32[2]{0:T(128)S(1)}, u32[]{:S(2)}) copy-start(f32[2]{0:T(128)S(1)} %get-tuple-element.78) | copy-start | bytes 28
  3.9 1.9 %copy-start.16 = (s32[64]{0:T(128)}, s32[64]{0:T(128)S(1)}, u32[]{:S(2)}) copy-start(s32[64]{0:T(128)S(1)} %convert_add_fusion.1) | copy-start | bytes 772
  3.9 1.6 %copy-start.2 = (s32[4,4,16,16]{3,2,1,0:T(8,128)S(1)}, s32[4,4,16,16]{3,2,1,0:T(8,128)}, u32[]{:S(2)}) copy-start(s32[4,4,16,16]{3,2,1,0:T(8,128)} %param.15) | copy-start | bytes 49156
  5.7 31.1 %copy-start.3 = (f32[4,6,6,32]{3,0,2,1:T(4,128)S(1)}, f32[4,6,6,32]{3,0,2,1:T(4,128)}, u32[]{:S(2)}) copy-start(f32[4,6,6,32]{3,0,2,1:T(4,128)} %param.18) | copy-start | bytes 55300
  6.0 49.9 %collective-permute-start = (f32[97,16,128]{2,1,0:T(8,128)S(1)}, f32[97,16,128]{2,1,0:T(8,128)S(1)}, u32[]{:S(2)}, u32[]{:S(2)}) collective-permute-start(f32[97,16,128]{2,1,0:T(8,128)S(1)} %pad_maximum_fusion), channel_id=1, source_target_pairs={{0,1},{1,2},{2,3},{3,0},{4,5},{5,6},{6,7},{7,4},{8,9},{9,10},{10,1... | collective-permute-start | bytes 2383880 | tf_op jit(solution)/shard_map/ppermute | solution.py:302
  9.5 46.5 %collective-permute-start.1 = (f32[97,16,128]{2,1,0:T(8,128)S(1)}, f32[97,16,128]{2,1,0:T(8,128)S(1)}, u32[]{:S(2)}, u32[]{:S(2)}) collective-permute-start(f32[97,16,128]{2,1,0:T(8,128)S(1)} %pad_maximum_fusion.1), channel_id=1, source_target_pairs={{1,0},{2,1},{3,2},{0,3},{5,4},{6,5},{7,6},{4,7},{9,8},{10,9},{11,1... | collective-permute-start | bytes 2383880 | tf_op jit(solution)/shard_map/ppermute | solution.py:303
  23.7 31.3 %all-to-all-start = ((f32[64,2,4]{2,1,0:T(2,128)}), f32[64,2,4]{2,1,0:T(2,128)S(1)}, u32[]{:S(2)}, u32[]{:S(2)}) async-start(f32[64,2,4]{2,1,0:T(2,128)} %bitcast.9), calls=%async_computation | async-start | bytes 131072 | tf_op jit(solution)/shard_map/all_to_all | solution.py:306
  55.9 2.5 %copy-start = (f32[97,16,128]{2,1,0:T(8,128)}, f32[97,16,128]{2,1,0:T(8,128)S(1)}, u32[]{:S(2)}) copy-start(f32[97,16,128]{2,1,0:T(8,128)S(1)} %collective-permute-done.low_ref) | copy-start | bytes 2383876
  56.0 2.4 %copy-start.1 = (f32[97,16,128]{2,1,0:T(8,128)}, f32[97,16,128]{2,1,0:T(8,128)S(1)}, u32[]{:S(2)}) copy-start(f32[97,16,128]{2,1,0:T(8,128)S(1)} %collective-permute-done.1.high_ref) | copy-start | bytes 2383876
  68.0 39.6 %copy-start.17 = (s32[64]{0:T(128)S(1)}, s32[64]{0:T(128)}, u32[]{:S(2)}) copy-start(s32[64]{0:T(128)} %copy-done.16) | copy-start | bytes 772
  68.0 41.3 %copy-start.5 = (f32[2]{0:T(128)S(1)}, f32[2]{0:T(128)}, u32[]{:S(2)}) copy-start(f32[2]{0:T(128)} %copy-done.4) | copy-start | bytes 28
  68.0 41.3 %copy-start.7 = (f32[2]{0:T(128)S(1)}, f32[2]{0:T(128)}, u32[]{:S(2)}) copy-start(f32[2]{0:T(128)} %copy-done.6) | copy-start | bytes 28
  68.0 41.3 %copy-start.9 = (f32[2]{0:T(128)S(1)}, f32[2]{0:T(128)}, u32[]{:S(2)}) copy-start(f32[2]{0:T(128)} %copy-done.8) | copy-start | bytes 28
  68.0 41.4 %copy-start.13 = (f32[2]{0:T(128)S(1)}, f32[2]{0:T(128)}, u32[]{:S(2)}) copy-start(f32[2]{0:T(128)} %copy-done.12) | copy-start | bytes 28
  68.0 41.8 %copy-start.14 = (s32[4,32]{1,0:T(4,128)S(1)}, s32[4,32]{1,0:T(4,128)}, u32[]{:S(2)}) copy-start(s32[4,32]{1,0:T(4,128)} %param.17) | copy-start | bytes 1540
  69.0 61.7 %copy-start.10 = (f32[6,32]{1,0:T(8,128)S(1)}, f32[6,32]{1,0:T(8,128)}, u32[]{:S(2)}) copy-start(f32[6,32]{1,0:T(8,128)} %param.19) | copy-start | bytes 2308
  69.0 61.7 %copy-start.11 = (f32[6,32]{1,0:T(8,128)S(1)}, f32[6,32]{1,0:T(8,128)}, u32[]{:S(2)}) copy-start(f32[6,32]{1,0:T(8,128)} %param.20) | copy-start | bytes 2308
  69.0 61.7 %copy-start.15 = (f32[32]{0:T(128)S(1)}, f32[32]{0:T(128)}, u32[]{:S(2)}) copy-start(f32[32]{0:T(128)} %param.21) | copy-start | bytes 388
  69.8 37.5 %all-to-all-start.1 = ((f32[64,4,3]{1,2,0:T(4,128)}), f32[64,4,3]{1,2,0:T(4,128)S(1)}, u32[]{:S(2)}, u32[]{:S(2)}) async-start(f32[64,4,3]{1,2,0:T(4,128)} %copy.78), calls=%async_computation.1 | async-start | bytes 262144 | tf_op jit(solution)/shard_map/all_to_all | solution.py:325
  87.0 21.0 %collective-permute-start.2 = (f32[150,32]{0,1:T(8,128)S(1)}, f32[150,32]{0,1:T(8,128)S(1)}, u32[]{:S(2)}, u32[]{:S(2)}) collective-permute-start(f32[150,32]{0,1:T(8,128)S(1)} %pad_maximum_fusion.4), channel_id=1, source_target_pairs={{0,16},{16,32},{32,48},{48,64},{64,80},{80,96},{96,112},{112,128},... | collective-permute-start | bytes 57608 | tf_op jit(solution)/shard_map/ppermute | solution.py:44

commit v8 on v7

--- a/solution.py
+++ b/solution.py
@@ -113,6 +113,16 @@
     return (shifted, (s11, s22, s12))
 
 
+def share_planes(phase_planes, class_hot):
+    fiber_share = phase_planes[0].astype(jnp.float32)[..., None] * class_hot[0]
+    for class_number in range(1, NCLASS):
+        fiber_share = (
+            fiber_share
+            + phase_planes[class_number].astype(jnp.float32)[..., None] * class_hot[class_number]
+        )
+    return fiber_share
+
+
 def moduli_planes(phase_planes, class_hot):
     fiber_share = phase_planes[0].astype(jnp.float32)[..., None] * class_hot[0]
     for class_number in range(1, NCLASS):
@@ -196,7 +206,7 @@
     return (moved, (s11, s22, s12))
 
 
-def relax_kernel(low_ref, state_ref, high_ref, lame_ref, shear_ref, macro_ref, out_ref, mean_ref):
+def relax_kernel(low_ref, state_ref, high_ref, share_ref, macro_ref, out_ref, mean_ref):
     rows = state_ref.shape[2]
     depth = ITERS
 
@@ -211,8 +221,9 @@
         )
         for i in range(3)
     ]
-    lame_all = lame_ref[...]
-    shear_all = shear_ref[...]
+    fiber_share = share_ref[...]
+    lame_all = matrix_lame + (fiber_lame - matrix_lame) * fiber_share
+    shear_all = matrix_shear + (fiber_shear - matrix_shear) * fiber_share
     macro = [macro_ref[k : k + 1, :].reshape(1, 1, 1, -1) for k in range(3)]
     stress = None
     for round_number in range(ITERS):
@@ -232,7 +243,7 @@
         mean_ref[3 + k : 4 + k, :] = pltpu.roll(mean_row, 2, 1)
 
 
-def relax_slab_kernel(low, state, high, lame_field, shear_field, macro):
+def relax_slab_kernel(low, state, high, fiber_share, macro):
     out_shape = (
         jax.ShapeDtypeStruct(state.shape, jnp.float32),
         jax.ShapeDtypeStruct((6, state.shape[-1]), jnp.float32),
@@ -240,10 +251,10 @@
     return pl.pallas_call(
         relax_kernel,
         out_shape=out_shape,
-        in_specs=[pl.BlockSpec(memory_space=pltpu.VMEM)] * 6,
+        in_specs=[pl.BlockSpec(memory_space=pltpu.VMEM)] * 5,
         out_specs=(pl.BlockSpec(memory_space=pltpu.VMEM), pl.BlockSpec(memory_space=pltpu.VMEM)),
         compiler_params=pltpu.CompilerParams(vmem_limit_bytes=60 * 1024 * 1024),
-    )(low, state, high, lame_field, shear_field, macro)
+    )(low, state, high, fiber_share, macro)
 
 
 def halo_pack(cells, phase_planes):
@@ -312,8 +323,8 @@
         jnp.float32
     )
     wide_phase = jnp.concatenate([phase_below, phase, phase_above], 1)
-    lame_field, shear_field = moduli_planes(wide_phase, class_hot)
-    displace, average = relax_slab_kernel(below, rve_state, above, lame_field, shear_field, macro)
+    fiber_share = share_planes(wide_phase, class_hot)
+    displace, average = relax_slab_kernel(below, rve_state, above, fiber_share, macro)
     ghost_rows = jnp.concatenate([flat_bmat, int_rows.astype(jnp.float32)], 0)
     ghost_rows, average = lax.optimization_barrier((ghost_rows, average))
     prev_pack = from_behind(ghost_rows, "tile", 1)

time: 132 us -> 132 us (level)
  no operation moved by 1% of the time
where the time goes in v8:
time: 132 us; the launch traced here: 131 us
  starting transfers between devices  48.5 us (37%)
  waiting for transfers between devices  34.1 us (26%)
  blocking collectives  19.5 us (15%)
  local copies, waits for them, and re-layouts  10.4 us (8%)
  Pallas kernels  9.51 us (7%)
  other arithmetic  6.48 us (5%)
    all_to_all x1, waiting for transfers between devices, shards(): lax.all_to_all(both_chunks, 'tile', split_axis=0, concat_axis=0, tiled=True)  18.4 us
    all_to_all x1, starting transfers between devices, shards(): lax.all_to_all(both_chunks, 'tile', split_axis=0, concat_axis=0, tiled=True)  16.6 us
    all_to_all x1, waiting for transfers between devices, shards(): lax.all_to_all(send.reshape(tile_count, capacity, 4), 'tile', split_axis=...  15.8 us
    ppermute x1, starting transfers between devices, shards(): above = lax.ppermute(pack_down, 'rve', down)  13.4 us
    all_to_all x1, starting transfers between devices, shards(): lax.all_to_all(send.reshape(tile_count, capacity, 4), 'tile', split_axis=...  13 us
    psum x1, blocking collectives, shards(): lax.psum(lax.psum(jnp.concatenate([own_terms, partial_internal], 0), 'rve...  10.6 us
    pallas_call x1, Pallas kernels, relax_slab_kernel(): pl.pallas_call(relax_kernel, out_shape=out_shape, in_specs=[pl.BlockSpec(...  9.51 us
    psum x1, blocking collectives, shards(): lax.psum(jnp.concatenate([own_terms, partial_internal], 0), 'rve')  8.87 us
  transfers between devices with their start and end apart: 5, of which 2 were waited for; matrix products, arithmetic and copies ran while one was open for 4% of the time, Pallas kernels for 0%

profile of v8, /device:TPU:8, one launch (start us, length us, event | category | flops | bytes accessed | tf_op | source)
XLA Modules:
  0.0 131.1 jit_solution(12991212527451262157)
XLA Ops:
  0.7 0.8 fusion.35
  1.5 0.8 fusion.40
  2.3 0.1 multiply_add_fusion.1
  2.4 0.1 stack.10
  2.5 0.1 stack.11
  2.6 0.1 stack.24
  2.7 0.1 convert_element_type.125
  2.8 0.8 copy.74
  3.6 0.1 reshape.811
  3.7 0.2 fusion
  3.9 1.5 %fusion.37 = (f32[3,2,16,16,128]{4,3,2,1,0:T(8,128)S(1)}, f32[3,2,16,16,128]{4,3,2,1,0:T(8,128)S(1)}) fusion(f32[3,4,16,16,128]{4,3,2,1,0:T(8,128)} %state_ref.1), kind=kLoop, calls=%fused_computation.114 | loop fusion | bytes 3145728 | tf_op jit(solution)/shard_map/slice | solution.py:292
  5.5 0.1 reshape.813
  5.6 0.1 reshape.815
  5.7 0.1 pad_maximum_fusion
  5.8 0.2 fusion.12
  6.0 3.5 %collective-permute-start = (f32[97,16,128]{2,1,0:T(8,128)S(1)}, f32[97,16,128]{2,1,0:T(8,128)S(1)}, u32[]{:S(2)}, u32[]{:S(2)}) collective-permute-start(f32[97,16,128]{2,1,0:T(8,128)S(1)} %pad_maximum_fusion), channel_id=1, source_target_pairs={{0,1},{1,2},{2,3},{3,0},{4,5},{5,6},{6,7},{7,4},{8,9},{9,10},{10,1... | collective-permute-start | bytes 2383880 | tf_op jit(solution)/shard_map/ppermute | solution.py:313
  9.5 13.4 %collective-permute-start.1 = (f32[97,16,128]{2,1,0:T(8,128)S(1)}, f32[97,16,128]{2,1,0:T(8,128)S(1)}, u32[]{:S(2)}, u32[]{:S(2)}) collective-permute-start(f32[97,16,128]{2,1,0:T(8,128)S(1)} %pad_maximum_fusion.1), channel_id=1, source_target_pairs={{1,0},{2,1},{3,2},{0,3},{5,4},{6,5},{7,6},{4,7},{9,8},{10,9},{11,1... | collective-permute-start | bytes 2383880 | tf_op jit(solution)/shard_map/ppermute | solution.py:314
  23.0 0.7 copy.75
  23.7 13.0 %all-to-all-start = ((f32[64,2,4]{2,1,0:T(2,128)}), f32[64,2,4]{2,1,0:T(2,128)S(1)}, u32[]{:S(2)}, u32[]{:S(2)}) async-start(f32[64,2,4]{2,1,0:T(2,128)} %bitcast.9), calls=%async_computation | async-start | bytes 131072 | tf_op jit(solution)/shard_map/all_to_all | solution.py:317
  36.8 0.6 reshape.809
  37.4 0.9 copy.72
  38.4 0.7 add_convert_fusion
  39.1 0.1 copy.73
  39.2 0.1 pad_maximum_fusion.4
  39.3 15.8 %all-to-all-done = f32[64,2,4]{2,1,0:T(2,128)S(1)} async-done(((f32[64,2,4]{2,1,0:T(2,128)}), f32[64,2,4]{2,1,0:T(2,128)S(1)}, u32[]{:S(2)}, u32[]{:S(2)}) %all-to-all-start) | async-done | bytes 2080 | tf_op jit(solution)/shard_map/all_to_all | solution.py:317
  55.0 0.7 copy.96
  55.7 0.2 fusion.5
  55.9 0.1 convert_element_type.129
  56.1 0.1 convert_element_type.131
  56.2 2.1 %multiply_add_fusion.share_ref = f32[8,16,16,128]{3,2,1,0:T(8,128)} fusion(f32[128]{0:T(128)S(1)} %get-tuple-element.68, f32[8,16,16]{2,1,0:T(8,128)S(1)} %get-tuple-element.44, f32[128]{0:T(128)S(1)} %get-tuple-element.69, f32[8,16,16]{2,1,0:T(8,128)S(1)} %get-tuple-element.45, f32[128]{0:T(128)S(1)} %get-tuple-element.70, ...), kind=kLoop, calls=%fused_computation.6 | loop fusion | flops 1835008 | bytes 1083392 | tf_op jit(solution)/shard_map/add | solution.py:120
  58.3 9.5 %shard_map.121 = (f32[3,4,16,16,128]{4,3,2,1,0:T(8,128)}, f32[6,128]{1,0:T(8,128)}) custom-call(f32[97,16,128]{2,1,0:T(8,128)} %copy-done, f32[3,4,16,16,128]{4,3,2,1,0:T(8,128)} %state_ref.1, f32[97,16,128]{2,1,0:T(8,128)} %copy-done.1, f32[8,16,16,128]{3,2,1,0:T(8,128)} %multiply_add_fusion.share_ref, f32[3,128]{1,0:T(4,128)} %bitcast.71), custom_call_target="tpu_custom_call" | custom-call | tf_op jit(solution)/shard_map/pallas_call | solution.py:251
  67.8 0.9 reshape.818
  68.7 0.1 copy.77
  68.8 0.8 copy.78
  69.6 16.6 %all-to-all-start.1 = ((f32[64,4,3]{1,2,0:T(4,128)}), f32[64,4,3]{1,2,0:T(4,128)S(1)}, u32[]{:S(2)}, u32[]{:S(2)}) async-start(f32[64,4,3]{1,2,0:T(4,128)} %copy.78), calls=%async_computation.1 | async-start | bytes 262144 | tf_op jit(solution)/shard_map/all_to_all | solution.py:336
  86.1 0.6 compare_reduce_fusion
  86.8 2.0 %collective-permute-start.2 = (f32[150,32]{0,1:T(8,128)S(1)}, f32[150,32]{0,1:T(8,128)S(1)}, u32[]{:S(2)}, u32[]{:S(2)}) collective-permute-start(f32[150,32]{0,1:T(8,128)S(1)} %pad_maximum_fusion.4), channel_id=1, source_target_pairs={{0,16},{16,32},{32,48},{48,64},{64,80},{80,96},{96,112},{112,128},... | collective-permute-start | bytes 57608 | tf_op jit(solution)/shard_map/ppermute | solution.py:44
  88.7 18.4 %all-to-all-done.1 = f32[64,4,3]{1,2,0:T(4,128)S(1)} async-done(((f32[64,4,3]{1,2,0:T(4,128)}), f32[64,4,3]{1,2,0:T(4,128)S(1)}, u32[]{:S(2)}, u32[]{:S(2)}) %all-to-all-start.1) | async-done | bytes 3104 | tf_op jit(solution)/shard_map/all_to_all | solution.py:336
  107.1 0.1 fusion.38
  107.2 0.1 reshape.820
  107.4 0.2 fusion.11
  107.6 0.1 reshape.821
  107.8 0.1 slice_convert_fusion.7
  107.8 0.1 slice.191
  107.9 0.1 reshape.822
  108.0 0.2 fusion.1
  108.2 0.2 fusion.13
  108.4 0.1 slice_reduce_fusion.2
  108.5 0.1 squeeze.12
  108.6 0.1 squeeze.13
  108.7 0.1 squeeze.28
  108.8 0.1 squeeze.29
  108.9 0.1 squeeze.30
  109.0 0.1 squeeze.31
  109.2 0.1 fusion.7
  109.3 0.1 copy.81
  109.4 0.1 copy.82
  109.6 0.2 convolution_bitcast_fusion.1
  109.9 0.2 convolution_bitcast_fusion
  110.1 0.7 add_select_fusion
  110.8 0.1 scatter-add.4
  111.0 8.9 %psum.14 = f32[12,32]{1,0:T(8,128)S(1)} all-reduce(f32[12,32]{1,0:T(8,128)S(1)} %pad_maximum_fusion.5), channel_id=1, replica_groups=mesh['tile'=64,'thick'=4,'rve'=4] {'rve'}, use_global_device_ids=true, to_apply=%region_7.0 | all-reduce | flops 384 | bytes 3072 | tf_op jit(solution)/shard_map/psum | solution.py:350
  119.9 10.6 %psum.15 = f32[12,32]{1,0:T(8,128)S(1)} all-reduce(f32[12,32]{1,0:T(8,128)S(1)} %psum.14), channel_id=1, replica_groups=mesh['tile'=64,'thick'=4,'rve'=4] {'thick'}, use_global_device_ids=true, to_apply=%region_8.0 | all-reduce | flops 384 | bytes 3072 | tf_op jit(solution)/shard_map/psum | solution.py:350
  130.5 0.6 fusion.39
  (70 shorter events, 0.5 us)
Async XLA Ops:
  0.6 1.7 %copy-start.12 = (f32[2]{0:T(128)}, f32[2]{0:T(128)S(1)}, u32[]{:S(2)}) copy-start(f32[2]{0:T(128)S(1)} %multiply_add_fusion.5) | copy-start | bytes 28
  1.5 2.4 %copy-start.8 = (f32[2]{0:T(128)}, f32[2]{0:T(128)S(1)}, u32[]{:S(2)}) copy-start(f32[2]{0:T(128)S(1)} %get-tuple-element.77) | copy-start | bytes 28
  1.5 4.0 %copy-start.4 = (f32[2]{0:T(128)}, f32[2]{0:T(128)S(1)}, u32[]{:S(2)}) copy-start(f32[2]{0:T(128)S(1)} %get-tuple-element.75) | copy-start | bytes 28
  1.5 4.0 %copy-start.6 = (f32[2]{0:T(128)}, f32[2]{0:T(128)S(1)}, u32[]{:S(2)}) copy-start(f32[2]{0:T(128)S(1)} %get-tuple-element.76) | copy-start | bytes 28
  3.9 1.9 %copy-start.16 = (s32[64]{0:T(128)}, s32[64]{0:T(128)S(1)}, u32[]{:S(2)}) copy-start(s32[64]{0:T(128)S(1)} %convert_add_fusion.1) | copy-start | bytes 772
  3.9 1.6 %copy-start.2 = (s32[4,4,16,16]{3,2,1,0:T(8,128)S(1)}, s32[4,4,16,16]{3,2,1,0:T(8,128)}, u32[]{:S(2)}) copy-start(s32[4,4,16,16]{3,2,1,0:T(8,128)} %param.15) | copy-start | bytes 49156
  5.7 31.1 %copy-start.3 = (f32[4,6,6,32]{3,0,2,1:T(4,128)S(1)}, f32[4,6,6,32]{3,0,2,1:T(4,128)}, u32[]{:S(2)}) copy-start(f32[4,6,6,32]{3,0,2,1:T(4,128)} %param.18) | copy-start | bytes 55300
  6.0 49.9 %collective-permute-start = (f32[97,16,128]{2,1,0:T(8,128)S(1)}, f32[97,16,128]{2,1,0:T(8,128)S(1)}, u32[]{:S(2)}, u32[]{:S(2)}) collective-permute-start(f32[97,16,128]{2,1,0:T(8,128)S(1)} %pad_maximum_fusion), channel_id=1, source_target_pairs={{0,1},{1,2},{2,3},{3,0},{4,5},{5,6},{6,7},{7,4},{8,9},{9,10},{10,1... | collective-permute-start | bytes 2383880 | tf_op jit(solution)/shard_map/ppermute | solution.py:313
  9.5 46.5 %collective-permute-start.1 = (f32[97,16,128]{2,1,0:T(8,128)S(1)}, f32[97,16,128]{2,1,0:T(8,128)S(1)}, u32[]{:S(2)}, u32[]{:S(2)}) collective-permute-start(f32[97,16,128]{2,1,0:T(8,128)S(1)} %pad_maximum_fusion.1), channel_id=1, source_target_pairs={{1,0},{2,1},{3,2},{0,3},{5,4},{6,5},{7,6},{4,7},{9,8},{10,9},{11,1... | collective-permute-start | bytes 2383880 | tf_op jit(solution)/shard_map/ppermute | solution.py:314
  23.7 31.3 %all-to-all-start = ((f32[64,2,4]{2,1,0:T(2,128)}), f32[64,2,4]{2,1,0:T(2,128)S(1)}, u32[]{:S(2)}, u32[]{:S(2)}) async-start(f32[64,2,4]{2,1,0:T(2,128)} %bitcast.9), calls=%async_computation | async-start | bytes 131072 | tf_op jit(solution)/shard_map/all_to_all | solution.py:317
  55.9 2.4 %copy-start = (f32[97,16,128]{2,1,0:T(8,128)}, f32[97,16,128]{2,1,0:T(8,128)S(1)}, u32[]{:S(2)}) copy-start(f32[97,16,128]{2,1,0:T(8,128)S(1)} %collective-permute-done.low_ref) | copy-start | bytes 2383876
  56.0 2.2 %copy-start.1 = (f32[97,16,128]{2,1,0:T(8,128)}, f32[97,16,128]{2,1,0:T(8,128)S(1)}, u32[]{:S(2)}) copy-start(f32[97,16,128]{2,1,0:T(8,128)S(1)} %collective-permute-done.1.high_ref) | copy-start | bytes 2383876
  67.8 39.6 %copy-start.17 = (s32[64]{0:T(128)S(1)}, s32[64]{0:T(128)}, u32[]{:S(2)}) copy-start(s32[64]{0:T(128)} %copy-done.16) | copy-start | bytes 772
  67.8 41.3 %copy-start.5 = (f32[2]{0:T(128)S(1)}, f32[2]{0:T(128)}, u32[]{:S(2)}) copy-start(f32[2]{0:T(128)} %copy-done.4) | copy-start | bytes 28
  67.8 41.3 %copy-start.7 = (f32[2]{0:T(128)S(1)}, f32[2]{0:T(128)}, u32[]{:S(2)}) copy-start(f32[2]{0:T(128)} %copy-done.6) | copy-start | bytes 28
  67.8 41.3 %copy-start.9 = (f32[2]{0:T(128)S(1)}, f32[2]{0:T(128)}, u32[]{:S(2)}) copy-start(f32[2]{0:T(128)} %copy-done.8) | copy-start | bytes 28
  67.8 41.4 %copy-start.13 = (f32[2]{0:T(128)S(1)}, f32[2]{0:T(128)}, u32[]{:S(2)}) copy-start(f32[2]{0:T(128)} %copy-done.12) | copy-start | bytes 28
  67.8 41.8 %copy-start.14 = (s32[4,32]{1,0:T(4,128)S(1)}, s32[4,32]{1,0:T(4,128)}, u32[]{:S(2)}) copy-start(s32[4,32]{1,0:T(4,128)} %param.17) | copy-start | bytes 1540
  68.8 61.7 %copy-start.10 = (f32[6,32]{1,0:T(8,128)S(1)}, f32[6,32]{1,0:T(8,128)}, u32[]{:S(2)}) copy-start(f32[6,32]{1,0:T(8,128)} %param.19) | copy-start | bytes 2308
  68.8 61.7 %copy-start.11 = (f32[6,32]{1,0:T(8,128)S(1)}, f32[6,32]{1,0:T(8,128)}, u32[]{:S(2)}) copy-start(f32[6,32]{1,0:T(8,128)} %param.20) | copy-start | bytes 2308
  68.8 61.7 %copy-start.15 = (f32[32]{0:T(128)S(1)}, f32[32]{0:T(128)}, u32[]{:S(2)}) copy-start(f32[32]{0:T(128)} %param.21) | copy-start | bytes 388
  69.6 37.5 %all-to-all-start.1 = ((f32[64,4,3]{1,2,0:T(4,128)}), f32[64,4,3]{1,2,0:T(4,128)S(1)}, u32[]{:S(2)}, u32[]{:S(2)}) async-start(f32[64,4,3]{1,2,0:T(4,128)} %copy.78), calls=%async_computation.1 | async-start | bytes 262144 | tf_op jit(solution)/shard_map/all_to_all | solution.py:336
  86.8 21.0 %collective-permute-start.2 = (f32[150,32]{0,1:T(8,128)S(1)}, f32[150,32]{0,1:T(8,128)S(1)}, u32[]{:S(2)}, u32[]{:S(2)}) collective-permute-start(f32[150,32]{0,1:T(8,128)S(1)} %pad_maximum_fusion.4), channel_id=1, source_target_pairs={{0,16},{16,32},{32,48},{48,64},{64,80},{80,96},{96,112},{112,128},... | collective-permute-start | bytes 57608 | tf_op jit(solution)/shard_map/ppermute | solution.py:44

commit v9 on v8

--- a/solution.py
+++ b/solution.py
@@ -236,11 +236,17 @@
         )
     for i in range(3):
         out_ref[i] = cells[i]
+    lanes = mean_ref.shape[1]
+    lane_from = lax.broadcasted_iota(jnp.int32, (lanes, lanes), 0)
+    lane_to = lax.broadcasted_iota(jnp.int32, (lanes, lanes), 1)
+    lane_shift = (lane_to == (lane_from + 2) % lanes).astype(jnp.float32)
     for k in range(3):
         total = jnp.sum(stress[k][1:], axis=(0, 1))
         mean_row = jnp.sum(total, axis=0, keepdims=True) / float(RES**3)
         mean_ref[k : k + 1, :] = mean_row
-        mean_ref[3 + k : 4 + k, :] = pltpu.roll(mean_row, 2, 1)
+        mean_ref[3 + k : 4 + k, :] = jnp.dot(
+            mean_row, lane_shift, precision=lax.Precision.HIGHEST, preferred_element_type=jnp.float32
+        )
 
 
 def relax_slab_kernel(low, state, high, fiber_share, macro):

time: 132 us -> 132 us (level)
  no operation moved by 1% of the time
where the time goes in v9:
time: 132 us; the launch traced here: 131 us
  starting transfers between devices  48.5 us (37%)
  waiting for transfers between devices  34.1 us (26%)
  blocking collectives  19.5 us (15%)
  local copies, waits for them, and re-layouts  10.4 us (8%)
  Pallas kernels  9.82 us (7%)
  other arithmetic  6.48 us (5%)
    all_to_all x1, waiting for transfers between devices, shards(): lax.all_to_all(both_chunks, 'tile', split_axis=0, concat_axis=0, tiled=True)  18.4 us
    all_to_all x1, starting transfers between devices, shards(): lax.all_to_all(both_chunks, 'tile', split_axis=0, concat_axis=0, tiled=True)  16.6 us
    all_to_all x1, waiting for transfers between devices, shards(): lax.all_to_all(send.reshape(tile_count, capacity, 4), 'tile', split_axis=...  15.8 us
    ppermute x1, starting transfers between devices, shards(): above = lax.ppermute(pack_down, 'rve', down)  13.4 us
    all_to_all x1, starting transfers between devices, shards(): lax.all_to_all(send.reshape(tile_count, capacity, 4), 'tile', split_axis=...  13 us
    psum x1, blocking collectives, shards(): lax.psum(lax.psum(jnp.concatenate([own_terms, partial_internal], 0), 'rve...  10.6 us
    pallas_call x1, Pallas kernels, relax_slab_kernel(): pl.pallas_call(relax_kernel, out_shape=out_shape, in_specs=[pl.BlockSpec(...  9.82 us
    psum x1, blocking collectives, shards(): lax.psum(jnp.concatenate([own_terms, partial_internal], 0), 'rve')  8.87 us
  transfers between devices with their start and end apart: 5, of which 2 were waited for; matrix products, arithmetic and copies ran while one was open for 4% of the time, Pallas kernels for 0%

profile of v9, /device:TPU:8, one launch (start us, length us, event | category | flops | bytes accessed | tf_op | source)
XLA Modules:
  0.0 131.4 jit_solution(8515171322264431994)
XLA Ops:
  0.7 0.8 fusion.35
  1.5 0.8 fusion.40
  2.3 0.1 multiply_add_fusion.1
  2.4 0.1 stack.10
  2.5 0.1 stack.11
  2.6 0.1 stack.24
  2.7 0.1 convert_element_type.125
  2.8 0.8 copy.74
  3.6 0.1 reshape.811
  3.7 0.2 fusion
  3.9 1.5 %fusion.37 = (f32[3,2,16,16,128]{4,3,2,1,0:T(8,128)S(1)}, f32[3,2,16,16,128]{4,3,2,1,0:T(8,128)S(1)}) fusion(f32[3,4,16,16,128]{4,3,2,1,0:T(8,128)} %state_ref.1), kind=kLoop, calls=%fused_computation.114 | loop fusion | bytes 3145728 | tf_op jit(solution)/shard_map/slice | solution.py:298
  5.5 0.1 reshape.813
  5.6 0.1 reshape.815
  5.7 0.1 pad_maximum_fusion
  5.8 0.2 fusion.12
  6.0 3.5 %collective-permute-start = (f32[97,16,128]{2,1,0:T(8,128)S(1)}, f32[97,16,128]{2,1,0:T(8,128)S(1)}, u32[]{:S(2)}, u32[]{:S(2)}) collective-permute-start(f32[97,16,128]{2,1,0:T(8,128)S(1)} %pad_maximum_fusion), channel_id=1, source_target_pairs={{0,1},{1,2},{2,3},{3,0},{4,5},{5,6},{6,7},{7,4},{8,9},{9,10},{10,1... | collective-permute-start | bytes 2383880 | tf_op jit(solution)/shard_map/ppermute | solution.py:319
  9.5 13.4 %collective-permute-start.1 = (f32[97,16,128]{2,1,0:T(8,128)S(1)}, f32[97,16,128]{2,1,0:T(8,128)S(1)}, u32[]{:S(2)}, u32[]{:S(2)}) collective-permute-start(f32[97,16,128]{2,1,0:T(8,128)S(1)} %pad_maximum_fusion.1), channel_id=1, source_target_pairs={{1,0},{2,1},{3,2},{0,3},{5,4},{6,5},{7,6},{4,7},{9,8},{10,9},{11,1... | collective-permute-start | bytes 2383880 | tf_op jit(solution)/shard_map/ppermute | solution.py:320
  23.0 0.7 copy.75
  23.7 13.0 %all-to-all-start = ((f32[64,2,4]{2,1,0:T(2,128)}), f32[64,2,4]{2,1,0:T(2,128)S(1)}, u32[]{:S(2)}, u32[]{:S(2)}) async-start(f32[64,2,4]{2,1,0:T(2,128)} %bitcast.9), calls=%async_computation | async-start | bytes 131072 | tf_op jit(solution)/shard_map/all_to_all | solution.py:323
  36.8 0.6 reshape.809
  37.4 0.9 copy.72
  38.4 0.7 add_convert_fusion
  39.1 0.1 copy.73
  39.2 0.1 pad_maximum_fusion.4
  39.3 15.8 %all-to-all-done = f32[64,2,4]{2,1,0:T(2,128)S(1)} async-done(((f32[64,2,4]{2,1,0:T(2,128)}), f32[64,2,4]{2,1,0:T(2,128)S(1)}, u32[]{:S(2)}, u32[]{:S(2)}) %all-to-all-start) | async-done | bytes 2080 | tf_op jit(solution)/shard_map/all_to_all | solution.py:323
  55.0 0.7 copy.96
  55.7 0.2 fusion.5
  55.9 0.1 convert_element_type.129
  56.1 0.1 convert_element_type.131
  56.2 2.1 %multiply_add_fusion.share_ref = f32[8,16,16,128]{3,2,1,0:T(8,128)} fusion(f32[128]{0:T(128)S(1)} %get-tuple-element.68, f32[8,16,16]{2,1,0:T(8,128)S(1)} %get-tuple-element.44, f32[128]{0:T(128)S(1)} %get-tuple-element.69, f32[8,16,16]{2,1,0:T(8,128)S(1)} %get-tuple-element.45, f32[128]{0:T(128)S(1)} %get-tuple-element.70, ...), kind=kLoop, calls=%fused_computation.6 | loop fusion | flops 1835008 | bytes 1083392 | tf_op jit(solution)/shard_map/add | solution.py:120
  58.3 9.8 %shard_map.121 = (f32[3,4,16,16,128]{4,3,2,1,0:T(8,128)}, f32[6,128]{1,0:T(8,128)}) custom-call(f32[97,16,128]{2,1,0:T(8,128)} %copy-done, f32[3,4,16,16,128]{4,3,2,1,0:T(8,128)} %state_ref.1, f32[97,16,128]{2,1,0:T(8,128)} %copy-done.1, f32[8,16,16,128]{3,2,1,0:T(8,128)} %multiply_add_fusion.share_ref, f32[3,128]{1,0:T(4,128)} %bitcast.71), custom_call_target="tpu_custom_call" | custom-call | tf_op jit(solution)/shard_map/pallas_call | solution.py:257
  68.1 0.9 reshape.818
  69.0 0.1 copy.77
  69.1 0.8 copy.78
  69.9 16.6 %all-to-all-start.1 = ((f32[64,4,3]{1,2,0:T(4,128)}), f32[64,4,3]{1,2,0:T(4,128)S(1)}, u32[]{:S(2)}, u32[]{:S(2)}) async-start(f32[64,4,3]{1,2,0:T(4,128)} %copy.78), calls=%async_computation.1 | async-start | bytes 262144 | tf_op jit(solution)/shard_map/all_to_all | solution.py:342
  86.4 0.6 compare_reduce_fusion
  87.1 2.0 %collective-permute-start.2 = (f32[150,32]{0,1:T(8,128)S(1)}, f32[150,32]{0,1:T(8,128)S(1)}, u32[]{:S(2)}, u32[]{:S(2)}) collective-permute-start(f32[150,32]{0,1:T(8,128)S(1)} %pad_maximum_fusion.4), channel_id=1, source_target_pairs={{0,16},{16,32},{32,48},{48,64},{64,80},{80,96},{96,112},{112,128},... | collective-permute-start | bytes 57608 | tf_op jit(solution)/shard_map/ppermute | solution.py:44
  89.0 18.4 %all-to-all-done.1 = f32[64,4,3]{1,2,0:T(4,128)S(1)} async-done(((f32[64,4,3]{1,2,0:T(4,128)}), f32[64,4,3]{1,2,0:T(4,128)S(1)}, u32[]{:S(2)}, u32[]{:S(2)}) %all-to-all-start.1) | async-done | bytes 3104 | tf_op jit(solution)/shard_map/all_to_all | solution.py:342
  107.4 0.1 fusion.38
  107.5 0.1 reshape.820
  107.7 0.2 fusion.11
  107.9 0.1 reshape.821
  108.1 0.1 slice_convert_fusion.7
  108.2 0.1 slice.191
  108.2 0.1 reshape.822
  108.3 0.2 fusion.1
  108.5 0.2 fusion.13
  108.7 0.1 slice_reduce_fusion.2
  108.8 0.1 squeeze.12
  108.9 0.1 squeeze.13
  109.0 0.1 squeeze.28
  109.1 0.1 squeeze.29
  109.2 0.1 squeeze.30
  109.3 0.1 squeeze.31
  109.5 0.1 fusion.7
  109.6 0.1 copy.81
  109.8 0.1 copy.82
  109.9 0.2 convolution_bitcast_fusion.1
  110.2 0.2 convolution_bitcast_fusion
  110.4 0.7 add_select_fusion
  111.1 0.1 scatter-add.4
  111.3 8.9 %psum.14 = f32[12,32]{1,0:T(8,128)S(1)} all-reduce(f32[12,32]{1,0:T(8,128)S(1)} %pad_maximum_fusion.5), channel_id=1, replica_groups=mesh['tile'=64,'thick'=4,'rve'=4] {'rve'}, use_global_device_ids=true, to_apply=%region_7.0 | all-reduce | flops 384 | bytes 3072 | tf_op jit(solution)/shard_map/psum | solution.py:356
  120.2 10.6 %psum.15 = f32[12,32]{1,0:T(8,128)S(1)} all-reduce(f32[12,32]{1,0:T(8,128)S(1)} %psum.14), channel_id=1, replica_groups=mesh['tile'=64,'thick'=4,'rve'=4] {'thick'}, use_global_device_ids=true, to_apply=%region_8.0 | all-reduce | flops 384 | bytes 3072 | tf_op jit(solution)/shard_map/psum | solution.py:356
  130.8 0.6 fusion.39
  (70 shorter events, 0.5 us)
Async XLA Ops:
  0.6 1.7 %copy-start.12 = (f32[2]{0:T(128)}, f32[2]{0:T(128)S(1)}, u32[]{:S(2)}) copy-start(f32[2]{0:T(128)S(1)} %multiply_add_fusion.5) | copy-start | bytes 28
  1.5 2.4 %copy-start.8 = (f32[2]{0:T(128)}, f32[2]{0:T(128)S(1)}, u32[]{:S(2)}) copy-start(f32[2]{0:T(128)S(1)} %get-tuple-element.77) | copy-start | bytes 28
  1.5 4.0 %copy-start.4 = (f32[2]{0:T(128)}, f32[2]{0:T(128)S(1)}, u32[]{:S(2)}) copy-start(f32[2]{0:T(128)S(1)} %get-tuple-element.75) | copy-start | bytes 28
  1.5 4.0 %copy-start.6 = (f32[2]{0:T(128)}, f32[2]{0:T(128)S(1)}, u32[]{:S(2)}) copy-start(f32[2]{0:T(128)S(1)} %get-tuple-element.76) | copy-start | bytes 28
  3.9 1.9 %copy-start.16 = (s32[64]{0:T(128)}, s32[64]{0:T(128)S(1)}, u32[]{:S(2)}) copy-start(s32[64]{0:T(128)S(1)} %convert_add_fusion.1) | copy-start | bytes 772
  3.9 1.6 %copy-start.2 = (s32[4,4,16,16]{3,2,1,0:T(8,128)S(1)}, s32[4,4,16,16]{3,2,1,0:T(8,128)}, u32[]{:S(2)}) copy-start(s32[4,4,16,16]{3,2,1,0:T(8,128)} %param.15) | copy-start | bytes 49156
  5.7 31.1 %copy-start.3 = (f32[4,6,6,32]{3,0,2,1:T(4,128)S(1)}, f32[4,6,6,32]{3,0,2,1:T(4,128)}, u32[]{:S(2)}) copy-start(f32[4,6,6,32]{3,0,2,1:T(4,128)} %param.18) | copy-start | bytes 55300
  6.0 49.9 %collective-permute-start = (f32[97,16,128]{2,1,0:T(8,128)S(1)}, f32[97,16,128]{2,1,0:T(8,128)S(1)}, u32[]{:S(2)}, u32[]{:S(2)}) collective-permute-start(f32[97,16,128]{2,1,0:T(8,128)S(1)} %pad_maximum_fusion), channel_id=1, source_target_pairs={{0,1},{1,2},{2,3},{3,0},{4,5},{5,6},{6,7},{7,4},{8,9},{9,10},{10,1... | collective-permute-start | bytes 2383880 | tf_op jit(solution)/shard_map/ppermute | solution.py:319
  9.5 46.5 %collective-permute-start.1 = (f32[97,16,128]{2,1,0:T(8,128)S(1)}, f32[97,16,128]{2,1,0:T(8,128)S(1)}, u32[]{:S(2)}, u32[]{:S(2)}) collective-permute-start(f32[97,16,128]{2,1,0:T(8,128)S(1)} %pad_maximum_fusion.1), channel_id=1, source_target_pairs={{1,0},{2,1},{3,2},{0,3},{5,4},{6,5},{7,6},{4,7},{9,8},{10,9},{11,1... | collective-permute-start | bytes 2383880 | tf_op jit(solution)/shard_map/ppermute | solution.py:320
  23.7 31.3 %all-to-all-start = ((f32[64,2,4]{2,1,0:T(2,128)}), f32[64,2,4]{2,1,0:T(2,128)S(1)}, u32[]{:S(2)}, u32[]{:S(2)}) async-start(f32[64,2,4]{2,1,0:T(2,128)} %bitcast.9), calls=%async_computation | async-start | bytes 131072 | tf_op jit(solution)/shard_map/all_to_all | solution.py:323
  55.9 2.4 %copy-start = (f32[97,16,128]{2,1,0:T(8,128)}, f32[97,16,128]{2,1,0:T(8,128)S(1)}, u32[]{:S(2)}) copy-start(f32[97,16,128]{2,1,0:T(8,128)S(1)} %collective-permute-done.low_ref) | copy-start | bytes 2383876
  56.0 2.2 %copy-start.1 = (f32[97,16,128]{2,1,0:T(8,128)}, f32[97,16,128]{2,1,0:T(8,128)S(1)}, u32[]{:S(2)}) copy-start(f32[97,16,128]{2,1,0:T(8,128)S(1)} %collective-permute-done.1.high_ref) | copy-start | bytes 2383876
  68.1 39.6 %copy-start.17 = (s32[64]{0:T(128)S(1)}, s32[64]{0:T(128)}, u32[]{:S(2)}) copy-start(s32[64]{0:T(128)} %copy-done.16) | copy-start | bytes 772
  68.1 41.3 %copy-start.5 = (f32[2]{0:T(128)S(1)}, f32[2]{0:T(128)}, u32[]{:S(2)}) copy-start(f32[2]{0:T(128)} %copy-done.4) | copy-start | bytes 28
  68.1 41.3 %copy-start.7 = (f32[2]{0:T(128)S(1)}, f32[2]{0:T(128)}, u32[]{:S(2)}) copy-start(f32[2]{0:T(128)} %copy-done.6) | copy-start | bytes 28
  68.1 41.3 %copy-start.9 = (f32[2]{0:T(128)S(1)}, f32[2]{0:T(128)}, u32[]{:S(2)}) copy-start(f32[2]{0:T(128)} %copy-done.8) | copy-start | bytes 28
  68.1 41.4 %copy-start.13 = (f32[2]{0:T(128)S(1)}, f32[2]{0:T(128)}, u32[]{:S(2)}) copy-start(f32[2]{0:T(128)} %copy-done.12) | copy-start | bytes 28
  68.1 41.8 %copy-start.14 = (s32[4,32]{1,0:T(4,128)S(1)}, s32[4,32]{1,0:T(4,128)}, u32[]{:S(2)}) copy-start(s32[4,32]{1,0:T(4,128)} %param.17) | copy-start | bytes 1540
  69.1 61.7 %copy-start.10 = (f32[6,32]{1,0:T(8,128)S(1)}, f32[6,32]{1,0:T(8,128)}, u32[]{:S(2)}) copy-start(f32[6,32]{1,0:T(8,128)} %param.19) | copy-start | bytes 2308
  69.1 61.7 %copy-start.11 = (f32[6,32]{1,0:T(8,128)S(1)}, f32[6,32]{1,0:T(8,128)}, u32[]{:S(2)}) copy-start(f32[6,32]{1,0:T(8,128)} %param.20) | copy-start | bytes 2308
  69.1 61.7 %copy-start.15 = (f32[32]{0:T(128)S(1)}, f32[32]{0:T(128)}, u32[]{:S(2)}) copy-start(f32[32]{0:T(128)} %param.21) | copy-start | bytes 388
  69.9 37.5 %all-to-all-start.1 = ((f32[64,4,3]{1,2,0:T(4,128)}), f32[64,4,3]{1,2,0:T(4,128)S(1)}, u32[]{:S(2)}, u32[]{:S(2)}) async-start(f32[64,4,3]{1,2,0:T(4,128)} %copy.78), calls=%async_computation.1 | async-start | bytes 262144 | tf_op jit(solution)/shard_map/all_to_all | solution.py:342
  87.1 21.0 %collective-permute-start.2 = (f32[150,32]{0,1:T(8,128)S(1)}, f32[150,32]{0,1:T(8,128)S(1)}, u32[]{:S(2)}, u32[]{:S(2)}) collective-permute-start(f32[150,32]{0,1:T(8,128)S(1)} %pad_maximum_fusion.4), channel_id=1, source_target_pairs={{0,16},{16,32},{32,48},{48,64},{64,80},{80,96},{96,112},{112,128},... | collective-permute-start | bytes 57608 | tf_op jit(solution)/shard_map/ppermute | solution.py:44

commit v10 on v8

--- a/solution.py
+++ b/solution.py
@@ -238,15 +238,13 @@
         out_ref[i] = cells[i]
     for k in range(3):
         total = jnp.sum(stress[k][1:], axis=(0, 1))
-        mean_row = jnp.sum(total, axis=0, keepdims=True) / float(RES**3)
-        mean_ref[k : k + 1, :] = mean_row
-        mean_ref[3 + k : 4 + k, :] = pltpu.roll(mean_row, 2, 1)
+        mean_ref[k : k + 1, :] = jnp.sum(total, axis=0, keepdims=True) / float(RES**3)
 
 
 def relax_slab_kernel(low, state, high, fiber_share, macro):
     out_shape = (
         jax.ShapeDtypeStruct(state.shape, jnp.float32),
-        jax.ShapeDtypeStruct((6, state.shape[-1]), jnp.float32),
+        jax.ShapeDtypeStruct((3, state.shape[-1]), jnp.float32),
     )
     return pl.pallas_call(
         relax_kernel,
@@ -328,8 +326,9 @@
     ghost_rows = jnp.concatenate([flat_bmat, int_rows.astype(jnp.float32)], 0)
     ghost_rows, average = lax.optimization_barrier((ghost_rows, average))
     prev_pack = from_behind(ghost_rows, "tile", 1)
+    both_means = jnp.concatenate([average, jnp.roll(average, capacity, axis=1)], 0)
     both_chunks = (
-        average.reshape(2, 3, tile_count, capacity)
+        both_means.reshape(2, 3, tile_count, capacity)
         .transpose(2, 0, 3, 1)
         .reshape(tile_count, 2 * capacity, 3)
     )

time: 132 us -> 130 us (0.985)
  Pallas kernels: 9.51 us -> 6.93 us
    pallas_call x1, Pallas kernels: 9.51 us -> 6.93 us  [relax_slab_kernel(): pl.pallas_call(relax_kernel, out_shape=out_shape, in_specs=[pl.BlockSpec(...]
where the time goes in v10:
time: 130 us; the launch traced here: 129 us
  starting transfers between devices  48.5 us (37%)
  waiting for transfers between devices  34.1 us (26%)
  blocking collectives  19.5 us (15%)
  local copies, waits for them, and re-layouts  10.5 us (8%)
  other arithmetic  7.31 us (6%)
  Pallas kernels  6.93 us (5%)
  between operations  1.31 us (1%)
    all_to_all x1, waiting for transfers between devices, shards(): lax.all_to_all(both_chunks, 'tile', split_axis=0, concat_axis=0, tiled=True)  18.4 us
    all_to_all x1, starting transfers between devices, shards(): lax.all_to_all(both_chunks, 'tile', split_axis=0, concat_axis=0, tiled=True)  16.6 us
    all_to_all x1, waiting for transfers between devices, shards(): lax.all_to_all(send.reshape(tile_count, capacity, 4), 'tile', split_axis=...  15.8 us
    ppermute x1, starting transfers between devices, shards(): above = lax.ppermute(pack_down, 'rve', down)  13.4 us
    all_to_all x1, starting transfers between devices, shards(): lax.all_to_all(send.reshape(tile_count, capacity, 4), 'tile', split_axis=...  13 us
    psum x1, blocking collectives, shards(): lax.psum(lax.psum(jnp.concatenate([own_terms, partial_internal], 0), 'rve...  10.6 us
    psum x1, blocking collectives, shards(): lax.psum(jnp.concatenate([own_terms, partial_internal], 0), 'rve')  8.87 us
    pallas_call x1, Pallas kernels, relax_slab_kernel(): pl.pallas_call(relax_kernel, out_shape=out_shape, in_specs=[pl.BlockSpec(...  6.93 us
  transfers between devices with their start and end apart: 5, of which 2 were waited for; matrix products, arithmetic and copies ran while one was open for 4% of the time, Pallas kernels for 0%

profile of v10, /device:TPU:8, one launch (start us, length us, event | category | flops | bytes accessed | tf_op | source)
XLA Modules:
  0.0 129.4 jit_solution(17564039828166425130)
XLA Ops:
  0.7 0.8 fusion.35
  1.5 0.8 fusion.40
  2.3 0.1 multiply_add_fusion.1
  2.4 0.1 stack.10
  2.5 0.1 stack.11
  2.6 0.1 stack.24
  2.7 0.1 convert_element_type.125
  2.8 0.8 copy.74
  3.6 0.1 reshape.811
  3.7 0.2 fusion
  3.9 1.5 %fusion.37 = (f32[3,2,16,16,128]{4,3,2,1,0:T(8,128)S(1)}, f32[3,2,16,16,128]{4,3,2,1,0:T(8,128)S(1)}) fusion(f32[3,4,16,16,128]{4,3,2,1,0:T(8,128)} %state_ref.1), kind=kLoop, calls=%fused_computation.115 | loop fusion | bytes 3145728 | tf_op jit(solution)/shard_map/slice | solution.py:290
  5.5 0.1 reshape.813
  5.6 0.1 reshape.815
  5.8 0.2 fusion.12
  6.0 3.5 %collective-permute-start = (f32[97,16,128]{2,1,0:T(8,128)S(1)}, f32[97,16,128]{2,1,0:T(8,128)S(1)}, u32[]{:S(2)}, u32[]{:S(2)}) collective-permute-start(f32[97,16,128]{2,1,0:T(8,128)S(1)} %pad_maximum_fusion), channel_id=1, source_target_pairs={{0,1},{1,2},{2,3},{3,0},{4,5},{5,6},{6,7},{7,4},{8,9},{9,10},{10,1... | collective-permute-start | bytes 2383880 | tf_op jit(solution)/shard_map/ppermute | solution.py:311
  9.5 13.4 %collective-permute-start.1 = (f32[97,16,128]{2,1,0:T(8,128)S(1)}, f32[97,16,128]{2,1,0:T(8,128)S(1)}, u32[]{:S(2)}, u32[]{:S(2)}) collective-permute-start(f32[97,16,128]{2,1,0:T(8,128)S(1)} %pad_maximum_fusion.1), channel_id=1, source_target_pairs={{1,0},{2,1},{3,2},{0,3},{5,4},{6,5},{7,6},{4,7},{9,8},{10,9},{11,1... | collective-permute-start | bytes 2383880 | tf_op jit(solution)/shard_map/ppermute | solution.py:312
  23.0 0.7 copy.75
  23.7 13.0 %all-to-all-start = ((f32[64,2,4]{2,1,0:T(2,128)}), f32[64,2,4]{2,1,0:T(2,128)S(1)}, u32[]{:S(2)}, u32[]{:S(2)}) async-start(f32[64,2,4]{2,1,0:T(2,128)} %bitcast.9), calls=%async_computation | async-start | bytes 131072 | tf_op jit(solution)/shard_map/all_to_all | solution.py:315
  36.8 0.6 reshape.809
  37.4 0.9 copy.72
  38.4 0.7 add_convert_fusion
  39.1 0.1 copy.73
  39.2 0.1 pad_maximum_fusion.4
  39.3 15.8 %all-to-all-done = f32[64,2,4]{2,1,0:T(2,128)S(1)} async-done(((f32[64,2,4]{2,1,0:T(2,128)}), f32[64,2,4]{2,1,0:T(2,128)S(1)}, u32[]{:S(2)}, u32[]{:S(2)}) %all-to-all-start) | async-done | bytes 2080 | tf_op jit(solution)/shard_map/all_to_all | solution.py:315
  55.0 0.7 copy.96
  55.7 0.2 fusion.5
  55.9 0.1 convert_element_type.129
  56.1 0.1 convert_element_type.131
  56.2 2.1 %multiply_add_fusion.share_ref = f32[8,16,16,128]{3,2,1,0:T(8,128)} fusion(f32[128]{0:T(128)S(1)} %get-tuple-element.68, f32[8,16,16]{2,1,0:T(8,128)S(1)} %get-tuple-element.44, f32[128]{0:T(128)S(1)} %get-tuple-element.69, f32[8,16,16]{2,1,0:T(8,128)S(1)} %get-tuple-element.45, f32[128]{0:T(128)S(1)} %get-tuple-element.70, ...), kind=kLoop, calls=%fused_computation.6 | loop fusion | flops 1835008 | bytes 1083392 | tf_op jit(solution)/shard_map/add | solution.py:120
  58.3 6.9 %shard_map.121 = (f32[3,4,16,16,128]{4,3,2,1,0:T(8,128)}, f32[3,128]{1,0:T(4,128)}) custom-call(f32[97,16,128]{2,1,0:T(8,128)} %copy-done, f32[3,4,16,16,128]{4,3,2,1,0:T(8,128)} %state_ref.1, f32[97,16,128]{2,1,0:T(8,128)} %copy-done.1, f32[8,16,16,128]{3,2,1,0:T(8,128)} %multiply_add_fusion.share_ref, f32[3,128]{1,0:T(4,128)} %bitcast.73), custom_call_target="tpu_custom_call" | custom-call | tf_op jit(solution)/shard_map/pallas_call | solution.py:249
  65.2 0.8 slice.166
  66.0 0.8 maximum_maximum_fusion
  66.8 0.2 reshape.818
  67.0 0.1 copy.77
  67.1 0.8 copy.78
  67.9 16.6 %all-to-all-start.1 = ((f32[64,4,3]{1,2,0:T(4,128)}), f32[64,4,3]{1,2,0:T(4,128)S(1)}, u32[]{:S(2)}, u32[]{:S(2)}) async-start(f32[64,4,3]{1,2,0:T(4,128)} %copy.78), calls=%async_computation.1 | async-start | bytes 262144 | tf_op jit(solution)/shard_map/all_to_all | solution.py:335
  84.4 0.6 compare_reduce_fusion
  85.1 2.0 %collective-permute-start.2 = (f32[150,32]{0,1:T(8,128)S(1)}, f32[150,32]{0,1:T(8,128)S(1)}, u32[]{:S(2)}, u32[]{:S(2)}) collective-permute-start(f32[150,32]{0,1:T(8,128)S(1)} %pad_maximum_fusion.4), channel_id=1, source_target_pairs={{0,16},{16,32},{32,48},{48,64},{64,80},{80,96},{96,112},{112,128},... | collective-permute-start | bytes 57608 | tf_op jit(solution)/shard_map/ppermute | solution.py:44
  87.0 18.4 %all-to-all-done.1 = f32[64,4,3]{1,2,0:T(4,128)S(1)} async-done(((f32[64,4,3]{1,2,0:T(4,128)}), f32[64,4,3]{1,2,0:T(4,128)S(1)}, u32[]{:S(2)}, u32[]{:S(2)}) %all-to-all-start.1) | async-done | bytes 3104 | tf_op jit(solution)/shard_map/all_to_all | solution.py:335
  105.4 0.1 fusion.38
  105.5 0.1 reshape.820
  105.7 0.2 fusion.11
  105.9 0.1 reshape.821
  106.1 0.1 slice_convert_fusion.7
  106.2 0.1 slice.201
  106.2 0.1 reshape.822
  106.3 0.2 fusion.1
  106.5 0.2 fusion.13
  106.8 0.1 squeeze.12
  106.9 0.1 squeeze.13
  107.0 0.1 squeeze.28
  107.1 0.1 squeeze.29
  107.2 0.1 squeeze.30
  107.3 0.1 squeeze.31
  107.5 0.1 fusion.7
  107.6 0.1 copy.81
  107.8 0.1 copy.82
  107.9 0.2 convolution_bitcast_fusion.1
  108.2 0.2 convolution_bitcast_fusion
  108.4 0.7 add_select_fusion
  109.1 0.1 scatter-add.4
  109.3 8.9 %psum.14 = f32[12,32]{1,0:T(8,128)S(1)} all-reduce(f32[12,32]{1,0:T(8,128)S(1)} %pad_maximum_fusion.5), channel_id=1, replica_groups=mesh['tile'=64,'thick'=4,'rve'=4] {'rve'}, use_global_device_ids=true, to_apply=%region_7.8 | all-reduce | flops 384 | bytes 3072 | tf_op jit(solution)/shard_map/psum | solution.py:349
  118.2 10.6 %psum.15 = f32[12,32]{1,0:T(8,128)S(1)} all-reduce(f32[12,32]{1,0:T(8,128)S(1)} %psum.14), channel_id=1, replica_groups=mesh['tile'=64,'thick'=4,'rve'=4] {'thick'}, use_global_device_ids=true, to_apply=%region_8.9 | all-reduce | flops 384 | bytes 3072 | tf_op jit(solution)/shard_map/psum | solution.py:349
  128.8 0.6 fusion.39
  (72 shorter events, 0.7 us)
Async XLA Ops:
  0.6 1.7 %copy-start.12 = (f32[2]{0:T(128)}, f32[2]{0:T(128)S(1)}, u32[]{:S(2)}) copy-start(f32[2]{0:T(128)S(1)} %multiply_add_fusion.5) | copy-start | bytes 28
  1.5 2.4 %copy-start.8 = (f32[2]{0:T(128)}, f32[2]{0:T(128)S(1)}, u32[]{:S(2)}) copy-start(f32[2]{0:T(128)S(1)} %get-tuple-element.77) | copy-start | bytes 28
  1.5 4.0 %copy-start.4 = (f32[2]{0:T(128)}, f32[2]{0:T(128)S(1)}, u32[]{:S(2)}) copy-start(f32[2]{0:T(128)S(1)} %get-tuple-element.75) | copy-start | bytes 28
  1.5 4.0 %copy-start.6 = (f32[2]{0:T(128)}, f32[2]{0:T(128)S(1)}, u32[]{:S(2)}) copy-start(f32[2]{0:T(128)S(1)} %get-tuple-element.76) | copy-start | bytes 28
  3.9 1.9 %copy-start.16 = (s32[64]{0:T(128)}, s32[64]{0:T(128)S(1)}, u32[]{:S(2)}) copy-start(s32[64]{0:T(128)S(1)} %convert_add_fusion.1) | copy-start | bytes 772
  3.9 1.6 %copy-start.2 = (s32[4,4,16,16]{3,2,1,0:T(8,128)S(1)}, s32[4,4,16,16]{3,2,1,0:T(8,128)}, u32[]{:S(2)}) copy-start(s32[4,4,16,16]{3,2,1,0:T(8,128)} %param.15) | copy-start | bytes 49156
  5.7 31.1 %copy-start.3 = (f32[4,6,6,32]{3,0,2,1:T(4,128)S(1)}, f32[4,6,6,32]{3,0,2,1:T(4,128)}, u32[]{:S(2)}) copy-start(f32[4,6,6,32]{3,0,2,1:T(4,128)} %param.18) | copy-start | bytes 55300
  6.0 49.9 %collective-permute-start = (f32[97,16,128]{2,1,0:T(8,128)S(1)}, f32[97,16,128]{2,1,0:T(8,128)S(1)}, u32[]{:S(2)}, u32[]{:S(2)}) collective-permute-start(f32[97,16,128]{2,1,0:T(8,128)S(1)} %pad_maximum_fusion), channel_id=1, source_target_pairs={{0,1},{1,2},{2,3},{3,0},{4,5},{5,6},{6,7},{7,4},{8,9},{9,10},{10,1... | collective-permute-start | bytes 2383880 | tf_op jit(solution)/shard_map/ppermute | solution.py:311
  9.5 46.5 %collective-permute-start.1 = (f32[97,16,128]{2,1,0:T(8,128)S(1)}, f32[97,16,128]{2,1,0:T(8,128)S(1)}, u32[]{:S(2)}, u32[]{:S(2)}) collective-permute-start(f32[97,16,128]{2,1,0:T(8,128)S(1)} %pad_maximum_fusion.1), channel_id=1, source_target_pairs={{1,0},{2,1},{3,2},{0,3},{5,4},{6,5},{7,6},{4,7},{9,8},{10,9},{11,1... | collective-permute-start | bytes 2383880 | tf_op jit(solution)/shard_map/ppermute | solution.py:312
  23.7 31.3 %all-to-all-start = ((f32[64,2,4]{2,1,0:T(2,128)}), f32[64,2,4]{2,1,0:T(2,128)S(1)}, u32[]{:S(2)}, u32[]{:S(2)}) async-start(f32[64,2,4]{2,1,0:T(2,128)} %bitcast.9), calls=%async_computation | async-start | bytes 131072 | tf_op jit(solution)/shard_map/all_to_all | solution.py:315
  55.9 2.4 %copy-start = (f32[97,16,128]{2,1,0:T(8,128)}, f32[97,16,128]{2,1,0:T(8,128)S(1)}, u32[]{:S(2)}) copy-start(f32[97,16,128]{2,1,0:T(8,128)S(1)} %collective-permute-done.low_ref) | copy-start | bytes 2383876
  56.0 2.2 %copy-start.1 = (f32[97,16,128]{2,1,0:T(8,128)}, f32[97,16,128]{2,1,0:T(8,128)S(1)}, u32[]{:S(2)}) copy-start(f32[97,16,128]{2,1,0:T(8,128)S(1)} %collective-permute-done.1.high_ref) | copy-start | bytes 2383876
  65.2 40.5 %copy-start.17 = (s32[64]{0:T(128)S(1)}, s32[64]{0:T(128)}, u32[]{:S(2)}) copy-start(s32[64]{0:T(128)} %copy-done.16) | copy-start | bytes 772
  65.2 42.2 %copy-start.5 = (f32[2]{0:T(128)S(1)}, f32[2]{0:T(128)}, u32[]{:S(2)}) copy-start(f32[2]{0:T(128)} %copy-done.4) | copy-start | bytes 28
  65.2 42.2 %copy-start.7 = (f32[2]{0:T(128)S(1)}, f32[2]{0:T(128)}, u32[]{:S(2)}) copy-start(f32[2]{0:T(128)} %copy-done.6) | copy-start | bytes 28
  65.2 42.2 %copy-start.9 = (f32[2]{0:T(128)S(1)}, f32[2]{0:T(128)}, u32[]{:S(2)}) copy-start(f32[2]{0:T(128)} %copy-done.8) | copy-start | bytes 28
  65.2 42.3 %copy-start.13 = (f32[2]{0:T(128)S(1)}, f32[2]{0:T(128)}, u32[]{:S(2)}) copy-start(f32[2]{0:T(128)} %copy-done.12) | copy-start | bytes 28
  66.8 41.1 %copy-start.14 = (s32[4,32]{1,0:T(4,128)S(1)}, s32[4,32]{1,0:T(4,128)}, u32[]{:S(2)}) copy-start(s32[4,32]{1,0:T(4,128)} %param.17) | copy-start | bytes 1540
  67.1 61.7 %copy-start.10 = (f32[6,32]{1,0:T(8,128)S(1)}, f32[6,32]{1,0:T(8,128)}, u32[]{:S(2)}) copy-start(f32[6,32]{1,0:T(8,128)} %param.19) | copy-start | bytes 2308
  67.1 61.7 %copy-start.11 = (f32[6,32]{1,0:T(8,128)S(1)}, f32[6,32]{1,0:T(8,128)}, u32[]{:S(2)}) copy-start(f32[6,32]{1,0:T(8,128)} %param.20) | copy-start | bytes 2308
  67.1 61.7 %copy-start.15 = (f32[32]{0:T(128)S(1)}, f32[32]{0:T(128)}, u32[]{:S(2)}) copy-start(f32[32]{0:T(128)} %param.21) | copy-start | bytes 388
  67.9 37.5 %all-to-all-start.1 = ((f32[64,4,3]{1,2,0:T(4,128)}), f32[64,4,3]{1,2,0:T(4,128)S(1)}, u32[]{:S(2)}, u32[]{:S(2)}) async-start(f32[64,4,3]{1,2,0:T(4,128)} %copy.78), calls=%async_computation.1 | async-start | bytes 262144 | tf_op jit(solution)/shard_map/all_to_all | solution.py:335
  85.1 21.0 %collective-permute-start.2 = (f32[150,32]{0,1:T(8,128)S(1)}, f32[150,32]{0,1:T(8,128)S(1)}, u32[]{:S(2)}, u32[]{:S(2)}) collective-permute-start(f32[150,32]{0,1:T(8,128)S(1)} %pad_maximum_fusion.4), channel_id=1, source_target_pairs={{0,16},{16,32},{32,48},{48,64},{64,80},{80,96},{96,112},{112,128},... | collective-permute-start | bytes 57608 | tf_op jit(solution)/shard_map/ppermute | solution.py:44
